TPU v7x, 32 devices: a whole 2x2x4 slice. The times are simulated.
32 devices in a mesh: elem: 8 (over z, x), cuts: 4 (over y, core).
Axes of the slice: x: 2, y: 2, z: 4, core: 2. Of those that a mesh axis runs over, the one named last changes fastest.
Arguments:
- basis: bfloat16 [8, 32768, 160], P('elem', 'cuts'), may hold values from -6 to 6
- quad_weight: float32 [8, 32768], P('elem', 'cuts'), may hold values from 0.5 to 2
- projectors: bfloat16 [8, 3, 20, 16, 32768], P('elem', None, None, None, 'cuts'), may hold values from -0.03125 to 0.03125
- species: int32 [8, 20], P('elem'), may hold values from 0 to 3
- counts: int32 [8, 20], P('elem'), may hold values from 1 to 16
- gamma_table: float32 [4, 16], replicated, may hold values from -0.4375 to 0.4375
Outputs:
- blocks: float32 [8, 3, 160, 160], P(None, None, 'elem', 'cuts')
Inputs may be any that keep to these rules, and one draw needn't show every extreme that they name: `counts`: each atom has at least one projector and at most 16.
All inputs are finite; a program needn't handle non-finite values.
Results may differ from a plain program's by a relative error of at most 0.004.
Values sent between devices are 32-bit elements; how exact they have to be, the bound alone decides.
No kernel may reach another device: no remote copies, remote signals or barrier semaphores. Data moves between devices by JAX's collectives and lax.ppermute only.
A program may use at most 64 MiB of HBM per device.

v0:
```python
import jax
import jax.numpy as jnp
from jax import lax
from jax.sharding import PartitionSpec as P


def passed_along(block, axis, distance):
    devices = range(lax.axis_size(axis))
    route = [((i - distance) % len(devices), i) for i in devices]
    return lax.ppermute(block, axis, route)


def pair_block(left, weights, right):
    return jnp.einsum("ib,ic->bc", left * weights[:, None], right, precision=lax.Precision.HIGHEST)


def local(basis, quad_weight, projectors, species, counts, gamma_table):
    width = basis.shape[2]
    groups, atoms, slots, points = projectors.shape[1:]
    span = atoms * slots
    quarter = width // lax.axis_size("cuts")
    cut_index = lax.axis_index("cuts")
    scaled = (basis[0].astype(jnp.float32) * quad_weight[0][:, None]).astype(jnp.bfloat16)
    partial_value = jnp.dot(
        projectors[0].reshape(groups * span, points), scaled, preferred_element_type=jnp.float32
    )
    onehot = (
        species[0][:, None] == jnp.arange(gamma_table.shape[0], dtype=jnp.int32)[None, :]
    ).astype(jnp.float32)
    table = jnp.dot(onehot, gamma_table, precision=lax.Precision.HIGHEST)
    active = (jnp.arange(slots, dtype=jnp.int32)[None, :] < counts[0][:, None]).astype(jnp.float32)
    energy = (table * active).reshape(span)
    full = lax.psum(partial_value, "cuts")
    left_whole, left_energy = passed_along((full[span:], energy), "elem", 1)
    right_whole, right_energy = passed_along((full[: 2 * span], energy), "elem", -1)
    start = cut_index * quarter
    own_share = lax.dynamic_slice_in_dim(full, start, quarter, 1)
    left_coef = lax.dynamic_slice_in_dim(left_whole, start, quarter, 1)
    right_coef = lax.dynamic_slice_in_dim(right_whole, start, quarter, 1)
    group0, group1, group2 = (full[:span], full[span : 2 * span], full[2 * span :])
    share0, share1, share2 = (own_share[:span], own_share[span : 2 * span], own_share[2 * span :])
    block_left = pair_block(group0, left_energy, left_coef[:span]) + pair_block(
        group1, energy, left_coef[span:]
    )
    block_diag = (
        pair_block(group0, left_energy, share0)
        + pair_block(group1, energy, share1)
        + pair_block(group2, right_energy, share2)
    )
    block_right = pair_block(group1, energy, right_coef[:span]) + pair_block(
        group2, right_energy, right_coef[span:]
    )
    stacked = jnp.stack([block_left, block_diag, block_right], axis=0)[None]
    return lax.all_to_all(stacked, "elem", split_axis=2, concat_axis=0, tiled=True)


def solution(mesh):
    in_specs = (
        P("elem", "cuts", None),
        P("elem", "cuts"),
        P("elem", None, None, None, "cuts"),
        P("elem", None),
        P("elem", None),
        P(),
    )
    out_specs = P(None, None, "elem", "cuts")
    return jax.shard_map(local, mesh=mesh, in_specs=in_specs, out_specs=out_specs, check_vma=False)
```

profile of v0, /device:TPU:0, one launch (start us, length us, event | category | flops | bytes accessed | tf_op | source)
XLA Modules:
  0.0 105.4 jit_solution(16012741648585391315)
XLA Ops:
  6.5 0.0 copy-start
  6.5 0.0 all-reduce.2.cloned.1.call-start
  6.5 0.0 copy-start.1
  6.5 0.0 copy-start.2
  6.5 12.2 %fusion.4 = f32[960,160]{0,1:T(8,128)} fusion(bf16[960,8192]{1,0:T(8,128)(2,1)} %bitcast.32, bf16[1,8192,160]{1,2,0:T(8,128)(2,1)} %param.6, f32[8192]{0:T(1024)} %bitcast.33), kind=kOutput, calls=%fused_computation.4 | convolution fusion | flops 2520514560 | bytes 18997248 | tf_op jit(solution)/shard_map/dot_general | solution.py:24
  18.7 0.0 all-reduce.2.cloned.1.call-update
  18.7 0.0 copy-done
  18.7 0.0 copy-done.1
  18.8 0.0 copy-done.2
  18.8 0.2 convolution_select_fusion
  19.0 0.1 copy.18
  19.1 0.1 reshape.16
  19.1 2.9 %collective-permute-start = (f32[320]{0:T(512)S(1)}, f32[320]{0:T(512)S(1)}, u32[]{:S(2)}, u32[]{:S(2)}) collective-permute-start(f32[320]{0:T(512)S(1)} %reshape.16), channel_id=1, source_target_pairs={{28,0},{0,4},{4,8},{8,12},{12,16},{16,20},{20,24},{24,28},{29,1},{... | collective-permute-start | bytes 3848 | tf_op jit(solution)/shard_map/ppermute | solution.py:10
  22.1 3.1 %collective-permute-start.2 = (f32[320]{0:T(512)S(1)}, f32[320]{0:T(512)S(1)}, u32[]{:S(2)}, u32[]{:S(2)}) collective-permute-start(f32[320]{0:T(512)S(1)} %reshape.16), channel_id=1, source_target_pairs={{4,0},{8,4},{12,8},{16,12},{20,16},{24,20},{28,24},{0,28},{5,1},{9... | collective-permute-start | bytes 3848 | tf_op jit(solution)/shard_map/ppermute | solution.py:10
  25.2 30.2 %all-reduce.2.cloned.1.call-done = f32[960,160]{0,1:T(8,128)} async-done(((f32[960,160]{0,1:T(8,128)}), f32[960,160]{0,1:T(8,128)}) %all-reduce.2.cloned.1.call-update) | async-done | bytes 614416 | tf_op jit(solution)/shard_map/psum | solution.py:33
  55.4 1.4 %fusion.33 = (f32[640,160]{0,1:T(8,128)S(1)}, f32[640,160]{0,1:T(8,128)S(1)}) fusion(f32[960,160]{0,1:T(8,128)} %all-reduce.2.cloned.1.call-done), kind=kLoop, calls=%fused_computation.42 | loop fusion | bytes 1638400 | tf_op jit(solution)/shard_map/slice | solution.py:34
  56.8 1.5 %collective-permute-start.1 = (f32[640,160]{0,1:T(8,128)S(1)}, f32[640,160]{0,1:T(8,128)S(1)}, u32[]{:S(2)}, u32[]{:S(2)}) collective-permute-start(f32[640,160]{0,1:T(8,128)S(1)} %get-tuple-element.5), channel_id=1, source_target_pairs={{28,0},{0,4},{4,8},{8,12},{12,16},{16,20},{20,24},{24,28},{29,1},{... | collective-permute-start | bytes 1228808 | tf_op jit(solution)/shard_map/ppermute | solution.py:10
  58.3 3.3 %collective-permute-start.3 = (f32[640,160]{0,1:T(8,128)S(1)}, f32[640,160]{0,1:T(8,128)S(1)}, u32[]{:S(2)}, u32[]{:S(2)}) collective-permute-start(f32[640,160]{0,1:T(8,128)S(1)} %get-tuple-element.6), channel_id=1, source_target_pairs={{4,0},{8,4},{12,8},{16,12},{20,16},{24,20},{28,24},{0,28},{5,1},{9... | collective-permute-start | bytes 1228808 | tf_op jit(solution)/shard_map/ppermute | solution.py:10
  61.5 1.5 %fusion.13 = f32[160,40]{0,1:T(8,128)S(1)} fusion(f32[960,160]{0,1:T(8,128)} %all-reduce.2.cloned.1.call-done, f32[320]{0:T(512)S(1)} %reshape.16, s32[]{:T(128)S(6)} %add.24, s32[]{:T(128)S(6)} %select_n.2), kind=kOutput, calls=%fused_computation.19 | convolution fusion | flops 24627200 | bytes 334088 | tf_op jit(solution)/shard_map/ib,ic->bc/dot_general | solution.py:14
  63.0 0.0 collective-permute-done.2
  63.0 1.4 %fusion.12 = f32[160,40]{0,1:T(8,128)S(1)} fusion(f32[960,160]{0,1:T(8,128)} %all-reduce.2.cloned.1.call-done, f32[320]{0:T(512)S(1)} %collective-permute-done.2, s32[]{:T(128)S(6)} %add.26, s32[]{:T(128)S(6)} %select_n.2), kind=kOutput, calls=%fused_computation.18 | convolution fusion | flops 24627200 | bytes 334088 | tf_op jit(solution)/shard_map/ib,ic->bc/dot_general | solution.py:14
  64.4 0.0 collective-permute-done
  64.4 1.4 %fusion.10 = f32[1,160,40]{1,2,0:T(8,128)S(1)} fusion(f32[160,40]{0,1:T(8,128)S(1)} %fusion.12, f32[160,40]{0,1:T(8,128)S(1)} %fusion.13, f32[960,160]{0,1:T(8,128)} %all-reduce.2.cloned.1.call-done, f32[320]{0:T(512)S(1)} %collective-permute-done, s32[]{:T(128)S(6)} %select_n.2), kind=kOutput, calls=%fused_computation.11 | convolution fusion | flops 24640000 | bytes 385284 | tf_op jit(solution)/shard_map/ib,ic->bc/dot_general | solution.py:14
  65.8 9.1 %collective-permute-done.1 = f32[640,160]{0,1:T(8,128)S(1)} collective-permute-done((f32[640,160]{0,1:T(8,128)S(1)}, f32[640,160]{0,1:T(8,128)S(1)}, u32[]{:S(2)}, u32[]{:S(2)}) %collective-permute-start.1) | collective-permute-done | bytes 409632 | tf_op jit(solution)/shard_map/ppermute | solution.py:10
  74.9 1.5 %fusion.14 = f32[160,40]{0,1:T(8,128)S(1)} fusion(f32[960,160]{0,1:T(8,128)} %all-reduce.2.cloned.1.call-done, f32[320]{0:T(512)S(1)} %reshape.16, f32[640,160]{0,1:T(8,128)S(1)} %collective-permute-done.1, s32[]{:T(128)S(6)} %add.24, s32[]{:T(128)S(6)} %select_n.2), kind=kOutput, calls=%fused_computation.20 | convolution fusion | flops 24627200 | bytes 334856 | tf_op jit(solution)/shard_map/ib,ic->bc/dot_general | solution.py:14
  76.3 1.4 %fusion.8 = f32[1,160,40]{1,2,0:T(8,128)S(1)} fusion(f32[160,40]{0,1:T(8,128)S(1)} %fusion.14, f32[960,160]{0,1:T(8,128)} %all-reduce.2.cloned.1.call-done, f32[320]{0:T(512)S(1)} %collective-permute-done, f32[640,160]{0,1:T(8,128)S(1)} %collective-permute-done.1, s32[]{:T(128)S(6)} %select_n.2), kind=kOutput, calls=%fused_computation.9 | convolution fusion | flops 24633600 | bytes 375812 | tf_op jit(solution)/shard_map/ib,ic->bc/dot_general | solution.py:14
  77.7 0.0 collective-permute-done.3
  77.7 1.4 %fusion.11 = f32[160,40]{0,1:T(8,128)S(1)} fusion(f32[960,160]{0,1:T(8,128)} %all-reduce.2.cloned.1.call-done, f32[320]{0:T(512)S(1)} %collective-permute-done.2, f32[640,160]{0,1:T(8,128)S(1)} %collective-permute-done.3, s32[]{:T(128)S(6)} %add.24, s32[]{:T(128)S(6)} %select_n.2), kind=kOutput, calls=%fused_computation.17 | convolution fusion | flops 24627200 | bytes 334856 | tf_op jit(solution)/shard_map/ib,ic->bc/dot_general | solution.py:14
  79.1 1.5 %fusion.7 = f32[1,160,40]{1,2,0:T(8,128)S(1)} fusion(f32[160,40]{0,1:T(8,128)S(1)} %fusion.11, f32[960,160]{0,1:T(8,128)} %all-reduce.2.cloned.1.call-done, f32[320]{0:T(512)S(1)} %reshape.16, f32[640,160]{0,1:T(8,128)S(1)} %collective-permute-done.3, s32[]{:T(128)S(6)} %select_n.2), kind=kOutput, calls=%fused_computation.6 | convolution fusion | flops 24633600 | bytes 375812 | tf_op jit(solution)/shard_map/ib,ic->bc/dot_general | solution.py:14
  80.6 0.2 copy.19
  80.8 0.5 broadcast.11
  81.3 1.4 %reduce = f32[160,3,40]{2,1,0:T(4,128)S(1)} reduce(f32[160,3,1,40]{3,2,1,0:T(1,128)S(1)} %bitcast.31, f32[]{:T(128)} %broadcast.11), dimensions={2}, to_apply=%bitcast.24.reduce_sub_computation | reduce | bytes 153604
  82.8 0.3 reshape.17
  83.1 13.3 %all_to_all.18 = f32[8,1,2400]{2,1,0:T(1,128)S(1)} all-to-all(f32[8,1,2400]{2,1,0:T(1,128)S(1)} %reshape.17), channel_id=1, replica_groups=mesh['elem'=8,'cuts'=4] {'elem'}, dimensions={0} | all-to-all | bytes 153600 | tf_op jit(solution)/shard_map/all_to_all | solution.py:54
  96.4 0.8 reduce.1
  97.2 0.5 reshape.18
  97.7 0.2 copy.20
  97.9 0.7 copy.23
  (1 shorter events, 0.0 us)
Async XLA Ops:
  6.5 12.2 %copy-start = (f32[4,16]{1,0:T(4,128)S(1)}, f32[4,16]{1,0:T(4,128)}, u32[]{:S(2)}) copy-start(f32[4,16]{1,0:T(4,128)} %param.11) | copy-start | bytes 772
  6.5 48.9 %all-reduce.2.cloned.1.call-start = ((), (), s32[]{:S(2)}) async-start(), calls=%async_computation.1 | async-start | bytes 1310720 | tf_op jit(solution)/shard_map/psum | solution.py:33
  6.5 12.2 %copy-start.1 = (s32[1,20]{1,0:T(1,128)S(1)}, s32[1,20]{1,0:T(1,128)}, u32[]{:S(2)}) copy-start(s32[1,20]{1,0:T(1,128)} %param.9) | copy-start | bytes 244
  6.5 12.2 %copy-start.2 = (s32[1,20]{1,0:T(1,128)S(1)}, s32[1,20]{1,0:T(1,128)}, u32[]{:S(2)}) copy-start(s32[1,20]{1,0:T(1,128)} %param.10) | copy-start | bytes 244
  19.1 45.3 %collective-permute-start = (f32[320]{0:T(512)S(1)}, f32[320]{0:T(512)S(1)}, u32[]{:S(2)}, u32[]{:S(2)}) collective-permute-start(f32[320]{0:T(512)S(1)} %reshape.16), channel_id=1, source_target_pairs={{28,0},{0,4},{4,8},{8,12},{12,16},{16,20},{20,24},{24,28},{29,1},{... | collective-permute-start | bytes 3848 | tf_op jit(solution)/shard_map/ppermute | solution.py:10
  22.1 40.9 %collective-permute-start.2 = (f32[320]{0:T(512)S(1)}, f32[320]{0:T(512)S(1)}, u32[]{:S(2)}, u32[]{:S(2)}) collective-permute-start(f32[320]{0:T(512)S(1)} %reshape.16), channel_id=1, source_target_pairs={{4,0},{8,4},{12,8},{16,12},{20,16},{24,20},{28,24},{0,28},{5,1},{9... | collective-permute-start | bytes 3848 | tf_op jit(solution)/shard_map/ppermute | solution.py:10
  56.8 18.1 %collective-permute-start.1 = (f32[640,160]{0,1:T(8,128)S(1)}, f32[640,160]{0,1:T(8,128)S(1)}, u32[]{:S(2)}, u32[]{:S(2)}) collective-permute-start(f32[640,160]{0,1:T(8,128)S(1)} %get-tuple-element.5), channel_id=1, source_target_pairs={{28,0},{0,4},{4,8},{8,12},{12,16},{16,20},{20,24},{24,28},{29,1},{... | collective-permute-start | bytes 1228808 | tf_op jit(solution)/shard_map/ppermute | solution.py:10
  58.3 19.4 %collective-permute-start.3 = (f32[640,160]{0,1:T(8,128)S(1)}, f32[640,160]{0,1:T(8,128)S(1)}, u32[]{:S(2)}, u32[]{:S(2)}) collective-permute-start(f32[640,160]{0,1:T(8,128)S(1)} %get-tuple-element.6), channel_id=1, source_target_pairs={{4,0},{8,4},{12,8},{16,12},{20,16},{24,20},{28,24},{0,28},{5,1},{9... | collective-permute-start | bytes 1228808 | tf_op jit(solution)/shard_map/ppermute | solution.py:10
Sparse Core Ops, SparseCore 0:
  18.9 36.5 all-reduce.1
where the time goes:
time: 106 us; the launch traced here: 105 us
  waiting for transfers between devices  39.3 us (37%)
  matrix products  22.3 us (21%)
  between operations  13.5 us (13%)
  blocking collectives  13.3 us (13%)
  starting transfers between devices  10.8 us (10%)
  local copies, waits for them, and re-layouts  3.83 us (4%)
  other arithmetic  2.29 us (2%)
    psum x1, waiting for transfers between devices, local(): full = lax.psum(partial_value, 'cuts')  30.2 us
    all_to_all x1, blocking collectives, local(): lax.all_to_all(stacked, 'elem', split_axis=2, concat_axis=0, tiled=True)  13.3 us
    dot_general x1, matrix products, local(): jnp.dot(projectors[0].reshape(groups * span, points), scaled, preferred_e...  12.2 us
    ppermute x4, starting transfers between devices, passed_along(): return lax.ppermute(block, axis, route)  10.8 us
    dot_general x7, matrix products, pair_block(): jnp.einsum('ib,ic->bc', left * weights[:, None], right, precision=lax.Pre...  9.95 us
    ppermute x4, waiting for transfers between devices, passed_along(): return lax.ppermute(block, axis, route)  9.06 us
  transfers between devices with their start and end apart: 5, of which 2 were waited for; matrix products, arithmetic and copies ran while one was open for 8% of the time, Pallas kernels for 0%

commit v1 on v0

v1 whole, which is shorter than its diff:
```python
import jax
import jax.numpy as jnp
from jax import lax
from jax.sharding import PartitionSpec as P


def passed_along(block, axis, distance):
    devices = range(lax.axis_size(axis))
    route = [((i - distance) % len(devices), i) for i in devices]
    return lax.ppermute(block, axis, route)


def swapped(block, axis, bit):
    devices = range(lax.axis_size(axis))
    return lax.ppermute(block, axis, [(i, i ^ bit) for i in devices])


def reduce_scatter_columns(partial_value, axis, quarter):
    rows = partial_value.shape[0]
    size = lax.axis_size(axis)
    me = lax.axis_index(axis)
    held = partial_value.reshape(rows, size, quarter)
    bit = 1
    while bit < size:
        pairs = held.reshape(rows, held.shape[1] // 2, 2, quarter)
        mine = (me & bit) != 0
        keep = jnp.where(mine, pairs[:, :, 1], pairs[:, :, 0])
        send = jnp.where(mine, pairs[:, :, 0], pairs[:, :, 1])
        held = keep + swapped(send, axis, bit)
        bit *= 2
    return held.reshape(rows, quarter)


def all_gather_columns(share, axis):
    rows, quarter = share.shape
    size = lax.axis_size(axis)
    me = lax.axis_index(axis)
    held = share.reshape(rows, 1, quarter)
    bit = size // 2
    while bit >= 1:
        other = swapped(held, axis, bit)
        mine = (me & bit) != 0
        low = jnp.where(mine, other, held)
        high = jnp.where(mine, held, other)
        held = jnp.stack([low, high], axis=2).reshape(rows, held.shape[1] * 2, quarter)
        bit //= 2
    return held.reshape(rows, size * quarter)


def pair_block(left, right):
    return jnp.einsum("ib,ic->bc", left, right, precision=lax.Precision.HIGHEST)


def local(basis, quad_weight, projectors, species, counts, gamma_table):
    width = basis.shape[2]
    groups, atoms, slots, points = projectors.shape[1:]
    span = atoms * slots
    quarter = width // lax.axis_size("cuts")
    scaled = (basis[0].astype(jnp.float32) * quad_weight[0][:, None]).astype(jnp.bfloat16)
    partial_value = jnp.dot(
        projectors[0].reshape(groups * span, points), scaled, preferred_element_type=jnp.float32
    )
    onehot = (
        species[0][:, None] == jnp.arange(gamma_table.shape[0], dtype=jnp.int32)[None, :]
    ).astype(jnp.float32)
    table = jnp.dot(onehot, gamma_table, precision=lax.Precision.HIGHEST)
    active = (jnp.arange(slots, dtype=jnp.int32)[None, :] < counts[0][:, None]).astype(jnp.float32)
    energy = (table * active).reshape(span)

    share = reduce_scatter_columns(partial_value, "cuts", quarter)
    energy_rows = -(-span // quarter)
    packed_energy = jnp.pad(energy, (0, energy_rows * quarter - span)).reshape(energy_rows, quarter)
    to_right = jnp.concatenate([share[span:], packed_energy], axis=0)
    to_left = jnp.concatenate([share[: 2 * span], packed_energy], axis=0)
    from_left = passed_along(to_right, "elem", 1)
    from_right = passed_along(to_left, "elem", -1)
    full = all_gather_columns(share, "cuts")

    left_energy = from_left[2 * span :].reshape(-1)[:span]
    right_energy = from_right[2 * span :].reshape(-1)[:span]
    weight_left = jnp.concatenate([left_energy, energy])
    weight_diag = jnp.concatenate([left_energy, energy, right_energy])
    weight_right = jnp.concatenate([energy, right_energy])
    block_left = pair_block(full[: 2 * span], weight_left[:, None] * from_left[: 2 * span])
    block_diag = pair_block(full, weight_diag[:, None] * share)
    block_right = pair_block(full[span:], weight_right[:, None] * from_right[: 2 * span])
    stacked = jnp.stack([block_left, block_diag, block_right], axis=0)[None]
    return lax.all_to_all(stacked, "elem", split_axis=2, concat_axis=0, tiled=True)


def solution(mesh):
    in_specs = (
        P("elem", "cuts", None),
        P("elem", "cuts"),
        P("elem", None, None, None, "cuts"),
        P("elem", None),
        P("elem", None),
        P(),
    )
    out_specs = P(None, None, "elem", "cuts")
    return jax.shard_map(local, mesh=mesh, in_specs=in_specs, out_specs=out_specs, check_vma=False)
```

time: 106 us -> 50.4 us (0.48)
  waiting for transfers between devices: 39.3 us -> 8.56 us
  between operations: 13.5 us -> 0.15 us
  matrix products: 22.3 us -> 13.4 us
  blocking collectives: 13.3 us -> 12 us
    psum x1 -> x0, waiting for transfers between devices: 30.2 us -> none  [local(): full = lax.psum(partial_value, 'cuts')]
    dot_general x7 -> x3, matrix products: 9.95 us -> 1.86 us  [pair_block(): return jnp.einsum('ib,ic->bc', left, right, precision=lax.Precision.HIGHEST)]
    ppermute x4 -> x2, starting transfers between devices: 10.8 us -> 4.78 us  [passed_along(): return lax.ppermute(block, axis, route)]
    ppermute x4 -> x2, waiting for transfers between devices: 9.06 us -> 3.26 us  [passed_along(): return lax.ppermute(block, axis, route)]
    ppermute x0 -> x4, starting transfers between devices: none -> 5.35 us  [swapped(): return lax.ppermute(block, axis, [(i, i ^ bit) for i in devices])]
    ppermute x0 -> x4, waiting for transfers between devices: none -> 5.31 us  [swapped(): return lax.ppermute(block, axis, [(i, i ^ bit) for i in devices])]
    all_to_all x1, blocking collectives: 13.3 us -> 12 us  [local(): lax.all_to_all(stacked, 'elem', split_axis=2, concat_axis=0, tiled=True)]
    slice x1 -> x5, local copies, waits for them, and re-layouts: 1.35 us -> 0.22 us  [the longest x1 0.08 us: local(): to_right = jnp.concatenate([share[span:], packed_energy], axis=0)]
  transfers between devices with their start and end apart: 5 -> 6, of which waited for: 2 -> 4; matrix products, arithmetic and copies ran while one was open for 8% -> 2% of each run, Pallas kernels for 0% -> 0%
where the time goes in v1:
time: 50.4 us; the launch traced here: 50.2 us
  matrix products  13.4 us (27%)
  blocking collectives  12 us (24%)
  starting transfers between devices  10.1 us (20%)
  waiting for transfers between devices  8.56 us (17%)
  local copies, waits for them, and re-layouts  3.02 us (6%)
  other arithmetic  2.95 us (6%)
    all_to_all x1, blocking collectives, local(): lax.all_to_all(stacked, 'elem', split_axis=2, concat_axis=0, tiled=True)  12 us
    dot_general x1, matrix products, local(): jnp.dot(projectors[0].reshape(groups * span, points), scaled, preferred_e...  11.3 us
    ppermute x4, starting transfers between devices, swapped(): return lax.ppermute(block, axis, [(i, i ^ bit) for i in devices])  5.35 us
    ppermute x4, waiting for transfers between devices, swapped(): return lax.ppermute(block, axis, [(i, i ^ bit) for i in devices])  5.31 us
    ppermute x2, starting transfers between devices, passed_along(): return lax.ppermute(block, axis, route)  4.78 us
    ppermute x2, waiting for transfers between devices, passed_along(): return lax.ppermute(block, axis, route)  3.26 us
    dot_general x3, matrix products, pair_block(): return jnp.einsum('ib,ic->bc', left, right, precision=lax.Precision.HIGHEST)  1.86 us
    unnamed x1, other arithmetic  1.45 us
  transfers between devices with their start and end apart: 6, of which 4 were waited for; matrix products, arithmetic and copies ran while one was open for 2% of the time, Pallas kernels for 0%

profile of v1, /device:TPU:0, one launch (start us, length us, event | category | flops | bytes accessed | tf_op | source)
XLA Modules:
  0.0 50.2 jit_solution(3426416584703911702)
XLA Ops:
  0.0 0.0 copy-start
  0.0 0.0 copy-start.1
  0.0 0.0 copy-start.2
  0.0 11.3 %fusion.1 = f32[160,960]{1,0:T(8,128)S(1)} fusion(bf16[960,8192]{1,0:T(8,128)(2,1)} %bitcast.89, bf16[1,8192,160]{1,2,0:T(8,128)(2,1)} %param.6, f32[8192]{0:T(1024)} %bitcast.90), kind=kOutput, calls=%fused_computation.2 | convolution fusion | flops 2520514560 | bytes 18997248 | tf_op jit(solution)/shard_map/dot_general | solution.py:60
  11.4 0.5 %collective-permute-start = (f32[960,2,40]{0,2,1:T(8,128)S(1)}, f32[960,2,40]{0,2,1:T(8,128)S(1)}, u32[]{:S(2)}, u32[]{:S(2)}) collective-permute-start(f32[960,2,40]{0,2,1:T(8,128)S(1)} %select_bitcast_fusion.2), channel_id=1, source_target_pairs={{0,1},{1,0},{2,3},{3,2},{4,5},{5,4},{6,7},{7,6},{8,9},{9,8},{10,11... | collective-permute-start | bytes 921608 | tf_op jit(solution)/shard_map/ppermute | solution.py:15
  11.9 1.3 %collective-permute-done = f32[960,2,40]{0,2,1:T(8,128)S(1)} collective-permute-done((f32[960,2,40]{0,2,1:T(8,128)S(1)}, f32[960,2,40]{0,2,1:T(8,128)S(1)}, u32[]{:S(2)}, u32[]{:S(2)}) %collective-permute-start) | collective-permute-done | bytes 307232 | tf_op jit(solution)/shard_map/ppermute | solution.py:15
  13.2 0.1 fusion.6
  13.2 2.9 %collective-permute-start.1 = (f32[960,1,40]{0,2,1:T(8,128)S(1)}, f32[960,1,40]{0,2,1:T(8,128)S(1)}, u32[]{:S(2)}, u32[]{:S(2)}) collective-permute-start(f32[960,1,40]{0,2,1:T(8,128)S(1)} %select_bitcast_fusion.5), channel_id=1, source_target_pairs={{0,2},{1,3},{2,0},{3,1},{4,6},{5,7},{6,4},{7,5},{8,10},{9,11},{10,... | collective-permute-start | bytes 460808 | tf_op jit(solution)/shard_map/ppermute | solution.py:15
  16.2 0.0 copy-done
  16.2 0.0 copy-done.1
  16.2 0.0 copy-done.2
  16.2 0.2 convolution_select_fusion
  16.4 0.1 copy.49
  16.5 0.1 reshape.93
  16.6 0.1 copy.50
  16.6 4.0 %collective-permute-done.1 = f32[960,1,40]{0,2,1:T(8,128)S(1)} collective-permute-done((f32[960,1,40]{0,2,1:T(8,128)S(1)}, f32[960,1,40]{0,2,1:T(8,128)S(1)}, u32[]{:S(2)}, u32[]{:S(2)}) %collective-permute-start.1) | collective-permute-done | bytes 153632 | tf_op jit(solution)/shard_map/ppermute | solution.py:15
  20.7 1.8 %collective-permute-start.2 = (f32[960,1,40]{0,2,1:T(8,128)S(1)}, f32[960,1,40]{0,2,1:T(8,128)S(1)}, u32[]{:S(2)}, u32[]{:S(2)}) collective-permute-start(f32[960,1,40]{0,2,1:T(8,128)S(1)} %bitcast_add_fusion.1), channel_id=1, source_target_pairs={{0,2},{1,3},{2,0},{3,1},{4,6},{5,7},{6,4},{7,5},{8,10},{9,11},{10,... | collective-permute-start | bytes 460808 | tf_op jit(solution)/shard_map/ppermute | solution.py:15
  22.5 0.1 slice_bitcast_fusion.3
  22.7 1.6 %collective-permute-start.4 = (f32[648,40]{0,1:T(8,128)S(1)}, f32[648,40]{0,1:T(8,128)S(1)}, u32[]{:S(2)}, u32[]{:S(2)}) collective-permute-start(f32[648,40]{0,1:T(8,128)S(1)} %get-tuple-element.13), channel_id=1, source_target_pairs={{28,0},{0,4},{4,8},{8,12},{12,16},{16,20},{20,24},{24,28},{29,1},{... | collective-permute-start | bytes 311048 | tf_op jit(solution)/shard_map/ppermute | solution.py:10
  24.2 3.2 %collective-permute-start.5 = (f32[648,40]{0,1:T(8,128)S(1)}, f32[648,40]{0,1:T(8,128)S(1)}, u32[]{:S(2)}, u32[]{:S(2)}) collective-permute-start(f32[648,40]{0,1:T(8,128)S(1)} %get-tuple-element.14), channel_id=1, source_target_pairs={{4,0},{8,4},{12,8},{16,12},{20,16},{24,20},{28,24},{0,28},{5,1},{9... | collective-permute-start | bytes 311048 | tf_op jit(solution)/shard_map/ppermute | solution.py:10
  27.4 0.0 collective-permute-done.2
  27.5 0.1 collective-permute-start.3
  27.6 0.1 reshape.95
  27.7 2.7 %collective-permute-done.4 = f32[648,40]{0,1:T(8,128)S(1)} collective-permute-done((f32[648,40]{0,1:T(8,128)S(1)}, f32[648,40]{0,1:T(8,128)S(1)}, u32[]{:S(2)}, u32[]{:S(2)}) %collective-permute-start.4) | collective-permute-done | bytes 103712 | tf_op jit(solution)/shard_map/ppermute | solution.py:10
  30.4 0.1 copy.51
  30.5 0.1 reshape.94
  30.5 0.5 %collective-permute-done.5 = f32[648,40]{0,1:T(8,128)S(1)} collective-permute-done((f32[648,40]{0,1:T(8,128)S(1)}, f32[648,40]{0,1:T(8,128)S(1)}, u32[]{:S(2)}, u32[]{:S(2)}) %collective-permute-start.5) | collective-permute-done | bytes 103712 | tf_op jit(solution)/shard_map/ppermute | solution.py:10
  31.1 0.1 copy.54
  31.1 0.1 reshape.96
  31.2 0.1 pad_maximum_fusion.4
  31.3 0.1 pad_maximum_fusion.3
  31.4 0.0 collective-permute-done.3
  31.4 0.1 select_bitcast_fusion
  31.4 0.1 pad_maximum_fusion
  31.5 0.2 fusion.4
  31.7 0.7 %convolution_bitcast_fusion = f32[1,160,40]{1,2,0:T(8,128)S(1)} fusion(f32[960,160]{0,1:T(8,128)S(1)} %bitcast.83, f32[960,1,40]{0,2,1:T(8,128)S(1)} %bitcast_add_fusion.1, f32[960]{0:T(1024)S(1)} %pad_maximum_fusion.4), kind=kOutput, calls=%fused_computation.4 | convolution fusion | flops 73766400 | bytes 797440 | tf_op jit(solution)/shard_map/ib,ic->bc/dot_general | solution.py:51
  32.4 0.6 %convolution_bitcast_fusion.2 = f32[1,160,40]{1,2,0:T(8,128)S(1)} fusion(f32[640,160]{0,1:T(8,128)S(1)} %bitcast.85, f32[648,40]{0,1:T(8,128)S(1)} %collective-permute-done.4, f32[640]{0:T(1024)S(1)} %get-tuple-element.15), kind=kOutput, calls=%fused_computation.6 | convolution fusion | flops 49177600 | bytes 541696 | tf_op jit(solution)/shard_map/ib,ic->bc/dot_general | solution.py:51
  33.0 0.6 %convolution_bitcast_fusion.1 = f32[1,160,40]{1,2,0:T(8,128)S(1)} fusion(f32[640,160]{0,1:T(8,128)S(1)} %bitcast.84, f32[648,40]{0,1:T(8,128)S(1)} %collective-permute-done.5, f32[640]{0:T(1024)S(1)} %get-tuple-element.16), kind=kOutput, calls=%fused_computation.5 | convolution fusion | flops 49177600 | bytes 541696 | tf_op jit(solution)/shard_map/ib,ic->bc/dot_general | solution.py:51
  33.6 0.2 copy.55
  33.7 0.5 %broadcast.36 = f32[]{:T(128)} broadcast(f32[]{:T(128)} %constant.58), dimensions={} | broadcast | bytes 8
  34.3 1.4 %reduce = f32[160,3,40]{2,1,0:T(4,128)S(1)} reduce(f32[160,3,1,40]{3,2,1,0:T(1,128)S(1)} %bitcast.88, f32[]{:T(128)} %broadcast.36), dimensions={2}, to_apply=%bitcast.73.reduce_sub_computation | reduce | bytes 153604
  35.7 0.3 reshape.97
  36.0 12.0 %all_to_all.18 = f32[8,1,2400]{2,1,0:T(1,128)S(1)} all-to-all(f32[8,1,2400]{2,1,0:T(1,128)S(1)} %reshape.97), channel_id=1, replica_groups=mesh['elem'=8,'cuts'=4] {'elem'}, dimensions={0} | all-to-all | bytes 153600 | tf_op jit(solution)/shard_map/all_to_all | solution.py:88
  48.0 0.8 %reduce.1 = f32[8,2400]{1,0:T(8,128)S(1)} reduce(f32[8,1,2400]{2,1,0:T(1,128)S(1)} %all_to_all.18, f32[]{:T(128)} %broadcast.36), dimensions={1}, to_apply=%all_to_all.13.reduce_sub_computation | reduce | bytes 153604 | tf_op jit(solution)/shard_map/all_to_all | solution.py:88
  48.8 0.5 reshape.98
  49.3 0.2 copy.56
  49.5 0.7 %copy.61 = f32[8,1,3,20,40]{4,0,3,2,1:T(8,128)} copy(f32[8,1,3,20,40]{4,1,3,0,2:T(1,128)S(1)} %bitcast.87) | data formatting | bytes 153600 | tf_op jit(solution)/shard_map/all_to_all | solution.py:88
  (9 shorter events, 0.2 us)
Async XLA Ops:
  0.0 16.2 %copy-start = (f32[4,16]{1,0:T(4,128)S(1)}, f32[4,16]{1,0:T(4,128)}, u32[]{:S(2)}) copy-start(f32[4,16]{1,0:T(4,128)} %param.11) | copy-start | bytes 772
  0.0 16.2 %copy-start.1 = (s32[1,20]{1,0:T(1,128)S(1)}, s32[1,20]{1,0:T(1,128)}, u32[]{:S(2)}) copy-start(s32[1,20]{1,0:T(1,128)} %param.9) | copy-start | bytes 244
  0.0 16.2 %copy-start.2 = (s32[1,20]{1,0:T(1,128)S(1)}, s32[1,20]{1,0:T(1,128)}, u32[]{:S(2)}) copy-start(s32[1,20]{1,0:T(1,128)} %param.10) | copy-start | bytes 244
  11.4 1.8 %collective-permute-start = (f32[960,2,40]{0,2,1:T(8,128)S(1)}, f32[960,2,40]{0,2,1:T(8,128)S(1)}, u32[]{:S(2)}, u32[]{:S(2)}) collective-permute-start(f32[960,2,40]{0,2,1:T(8,128)S(1)} %select_bitcast_fusion.2), channel_id=1, source_target_pairs={{0,1},{1,0},{2,3},{3,2},{4,5},{5,4},{6,7},{7,6},{8,9},{9,8},{10,11... | collective-permute-start | bytes 921608 | tf_op jit(solution)/shard_map/ppermute | solution.py:15
  13.2 7.4 %collective-permute-start.1 = (f32[960,1,40]{0,2,1:T(8,128)S(1)}, f32[960,1,40]{0,2,1:T(8,128)S(1)}, u32[]{:S(2)}, u32[]{:S(2)}) collective-permute-start(f32[960,1,40]{0,2,1:T(8,128)S(1)} %select_bitcast_fusion.5), channel_id=1, source_target_pairs={{0,2},{1,3},{2,0},{3,1},{4,6},{5,7},{6,4},{7,5},{8,10},{9,11},{10,... | collective-permute-start | bytes 460808 | tf_op jit(solution)/shard_map/ppermute | solution.py:15
  20.7 6.7 %collective-permute-start.2 = (f32[960,1,40]{0,2,1:T(8,128)S(1)}, f32[960,1,40]{0,2,1:T(8,128)S(1)}, u32[]{:S(2)}, u32[]{:S(2)}) collective-permute-start(f32[960,1,40]{0,2,1:T(8,128)S(1)} %bitcast_add_fusion.1), channel_id=1, source_target_pairs={{0,2},{1,3},{2,0},{3,1},{4,6},{5,7},{6,4},{7,5},{8,10},{9,11},{10,... | collective-permute-start | bytes 460808 | tf_op jit(solution)/shard_map/ppermute | solution.py:15
  22.7 7.7 %collective-permute-start.4 = (f32[648,40]{0,1:T(8,128)S(1)}, f32[648,40]{0,1:T(8,128)S(1)}, u32[]{:S(2)}, u32[]{:S(2)}) collective-permute-start(f32[648,40]{0,1:T(8,128)S(1)} %get-tuple-element.13), channel_id=1, source_target_pairs={{28,0},{0,4},{4,8},{8,12},{12,16},{16,20},{20,24},{24,28},{29,1},{... | collective-permute-start | bytes 311048 | tf_op jit(solution)/shard_map/ppermute | solution.py:10
  24.2 6.9 %collective-permute-start.5 = (f32[648,40]{0,1:T(8,128)S(1)}, f32[648,40]{0,1:T(8,128)S(1)}, u32[]{:S(2)}, u32[]{:S(2)}) collective-permute-start(f32[648,40]{0,1:T(8,128)S(1)} %get-tuple-element.14), channel_id=1, source_target_pairs={{4,0},{8,4},{12,8},{16,12},{20,16},{24,20},{28,24},{0,28},{5,1},{9... | collective-permute-start | bytes 311048 | tf_op jit(solution)/shard_map/ppermute | solution.py:10
  27.5 3.9 %collective-permute-start.3 = (f32[960,2,40]{0,2,1:T(8,128)S(1)}, f32[960,2,40]{0,2,1:T(8,128)S(1)}, u32[]{:S(2)}, u32[]{:S(2)}) collective-permute-start(f32[960,2,40]{0,2,1:T(8,128)S(1)} %maximum_bitcast_fusion), channel_id=1, source_target_pairs={{0,1},{1,0},{2,3},{3,2},{4,5},{5,4},{6,7},{7,6},{8,9},{9,8},{10,11... | collective-permute-start | bytes 921608 | tf_op jit(solution)/shard_map/ppermute | solution.py:15

commit v2 on v1

--- a/solution.py
+++ b/solution.py
@@ -15,36 +15,30 @@
     return lax.ppermute(block, axis, [(i, i ^ bit) for i in devices])
 
 
-def reduce_scatter_columns(partial_value, axis, quarter):
+def summed_columns(partial_value, axis, quarter):
     rows = partial_value.shape[0]
     size = lax.axis_size(axis)
     me = lax.axis_index(axis)
-    held = partial_value.reshape(rows, size, quarter)
-    bit = 1
+    pairs = partial_value.reshape(rows, size // 2, 2, quarter)
+    odd = (me & 1) != 0
+    keep = jnp.where(odd, pairs[:, :, 1], pairs[:, :, 0])
+    send = jnp.where(odd, pairs[:, :, 0], pairs[:, :, 1])
+    half = keep + swapped(send, axis, 1)
+    bit = 2
     while bit < size:
-        pairs = held.reshape(rows, held.shape[1] // 2, 2, quarter)
-        mine = (me & bit) != 0
-        keep = jnp.where(mine, pairs[:, :, 1], pairs[:, :, 0])
-        send = jnp.where(mine, pairs[:, :, 0], pairs[:, :, 1])
-        held = keep + swapped(send, axis, bit)
+        half = half + swapped(half, axis, bit)
         bit *= 2
-    return held.reshape(rows, quarter)
+    share = lax.dynamic_index_in_dim(half, me // 2, 1, keepdims=False)
+    return half, share
 
 
-def all_gather_columns(share, axis):
-    rows, quarter = share.shape
-    size = lax.axis_size(axis)
-    me = lax.axis_index(axis)
-    held = share.reshape(rows, 1, quarter)
-    bit = size // 2
-    while bit >= 1:
-        other = swapped(held, axis, bit)
-        mine = (me & bit) != 0
-        low = jnp.where(mine, other, held)
-        high = jnp.where(mine, held, other)
-        held = jnp.stack([low, high], axis=2).reshape(rows, held.shape[1] * 2, quarter)
-        bit //= 2
-    return held.reshape(rows, size * quarter)
+def gathered_columns(half, axis):
+    rows, count, quarter = half.shape
+    odd = (lax.axis_index(axis) & 1) != 0
+    other = swapped(half, axis, 1)
+    low = jnp.where(odd, other, half)
+    high = jnp.where(odd, half, other)
+    return jnp.stack([low, high], axis=2).reshape(rows, count * 2 * quarter)
 
 
 def pair_block(left, right):
@@ -67,14 +61,14 @@
     active = (jnp.arange(slots, dtype=jnp.int32)[None, :] < counts[0][:, None]).astype(jnp.float32)
     energy = (table * active).reshape(span)
 
-    share = reduce_scatter_columns(partial_value, "cuts", quarter)
+    half, share = summed_columns(partial_value, "cuts", quarter)
     energy_rows = -(-span // quarter)
     packed_energy = jnp.pad(energy, (0, energy_rows * quarter - span)).reshape(energy_rows, quarter)
     to_right = jnp.concatenate([share[span:], packed_energy], axis=0)
     to_left = jnp.concatenate([share[: 2 * span], packed_energy], axis=0)
     from_left = passed_along(to_right, "elem", 1)
     from_right = passed_along(to_left, "elem", -1)
-    full = all_gather_columns(share, "cuts")
+    full = gathered_columns(half, "cuts")
 
     left_energy = from_left[2 * span :].reshape(-1)[:span]
     right_energy = from_right[2 * span :].reshape(-1)[:span]
@@ -84,8 +78,10 @@
     block_left = pair_block(full[: 2 * span], weight_left[:, None] * from_left[: 2 * span])
     block_diag = pair_block(full, weight_diag[:, None] * share)
     block_right = pair_block(full[span:], weight_right[:, None] * from_right[: 2 * span])
-    stacked = jnp.stack([block_left, block_diag, block_right], axis=0)[None]
-    return lax.all_to_all(stacked, "elem", split_axis=2, concat_axis=0, tiled=True)
+    owners = lax.axis_size("elem")
+    stacked = jnp.stack([block_left, block_diag, block_right], axis=0)
+    pieces = stacked.reshape(3, owners, width // owners, quarter).transpose(1, 0, 2, 3)
+    return lax.all_to_all(pieces, "elem", split_axis=0, concat_axis=0, tiled=True)
 
 
 def solution(mesh):

time: 50.4 us -> 50.2 us (level)
  waiting for transfers between devices: 8.56 us -> 12.6 us
  starting transfers between devices: 10.1 us -> 8.34 us
  other arithmetic: 2.95 us -> 1.47 us
    ppermute x4 -> x3, waiting for transfers between devices: 5.31 us -> 8.81 us  [swapped(): return lax.ppermute(block, axis, [(i, i ^ bit) for i in devices])]
    ppermute x4 -> x3, starting transfers between devices: 5.35 us -> 3.47 us  [swapped(): return lax.ppermute(block, axis, [(i, i ^ bit) for i in devices])]
    unnamed x1 -> x0, other arithmetic: 1.45 us -> none
    unnamed x9 -> x8, local copies, waits for them, and re-layouts: 1.27 us -> 0.37 us
    ppermute x2, waiting for transfers between devices: 3.26 us -> 3.81 us  [passed_along(): return lax.ppermute(block, axis, route)]
  transfers between devices with their start and end apart: 6 -> 5, of which waited for: 4 -> 4; matrix products, arithmetic and copies ran while one was open for 2% -> 2% of each run, Pallas kernels for 0% -> 0%
where the time goes in v2:
time: 50.2 us; the launch traced here: 50 us
  matrix products  13.4 us (27%)
  waiting for transfers between devices  12.6 us (25%)
  blocking collectives  11.6 us (23%)
  starting transfers between devices  8.34 us (17%)
  local copies, waits for them, and re-layouts  2.52 us (5%)
  other arithmetic  1.47 us (3%)
    all_to_all x1, blocking collectives, local(): lax.all_to_all(pieces, 'elem', split_axis=0, concat_axis=0, tiled=True)  11.6 us
    dot_general x1, matrix products, local(): jnp.dot(projectors[0].reshape(groups * span, points), scaled, preferred_e...  11.3 us
    ppermute x3, waiting for transfers between devices, swapped(): return lax.ppermute(block, axis, [(i, i ^ bit) for i in devices])  8.81 us
    ppermute x2, starting transfers between devices, passed_along(): return lax.ppermute(block, axis, route)  4.87 us
    ppermute x2, waiting for transfers between devices, passed_along(): return lax.ppermute(block, axis, route)  3.81 us
    ppermute x3, starting transfers between devices, swapped(): return lax.ppermute(block, axis, [(i, i ^ bit) for i in devices])  3.47 us
    dot_general x3, matrix products, pair_block(): return jnp.einsum('ib,ic->bc', left, right, precision=lax.Precision.HIGHEST)  1.83 us
    all_to_all x2, local copies, waits for them, and re-layouts, local(): lax.all_to_all(pieces, 'elem', split_axis=0, concat_axis=0, tiled=True)  1.25 us
  transfers between devices with their start and end apart: 5, of which 4 were waited for; matrix products, arithmetic and copies ran while one was open for 2% of the time, Pallas kernels for 0%

profile of v2, /device:TPU:0, one launch (start us, length us, event | category | flops | bytes accessed | tf_op | source)
XLA Modules:
  0.0 50.0 jit_solution(10592542522228835882)
XLA Ops:
  0.0 0.0 copy-start
  0.0 0.0 copy-start.1
  0.0 0.0 copy-start.2
  0.0 11.3 %fusion.1 = f32[160,960]{1,0:T(8,128)S(1)} fusion(bf16[960,8192]{1,0:T(8,128)(2,1)} %bitcast.73, bf16[1,8192,160]{1,2,0:T(8,128)(2,1)} %param.6, f32[8192]{0:T(1024)} %bitcast.74), kind=kOutput, calls=%fused_computation.2 | convolution fusion | flops 2520514560 | bytes 18997248 | tf_op jit(solution)/shard_map/dot_general | solution.py:54
  11.4 0.5 %collective-permute-start = (f32[960,2,40]{0,2,1:T(8,128)S(1)}, f32[960,2,40]{0,2,1:T(8,128)S(1)}, u32[]{:S(2)}, u32[]{:S(2)}) collective-permute-start(f32[960,2,40]{0,2,1:T(8,128)S(1)} %select_bitcast_fusion.2), channel_id=1, source_target_pairs={{0,1},{1,0},{2,3},{3,2},{4,5},{5,4},{6,7},{7,6},{8,9},{9,8},{10,11... | collective-permute-start | bytes 921608 | tf_op jit(solution)/shard_map/ppermute | solution.py:15
  11.9 1.3 %collective-permute-done = f32[960,2,40]{0,2,1:T(8,128)S(1)} collective-permute-done((f32[960,2,40]{0,2,1:T(8,128)S(1)}, f32[960,2,40]{0,2,1:T(8,128)S(1)}, u32[]{:S(2)}, u32[]{:S(2)}) %collective-permute-start) | collective-permute-done | bytes 307232 | tf_op jit(solution)/shard_map/ppermute | solution.py:15
  13.2 0.1 bitcast_add_fusion
  13.2 3.0 %collective-permute-start.1 = (f32[960,2,40]{0,2,1:T(8,128)S(1)}, f32[960,2,40]{0,2,1:T(8,128)S(1)}, u32[]{:S(2)}, u32[]{:S(2)}) collective-permute-start(f32[960,2,40]{0,2,1:T(8,128)S(1)} %bitcast_add_fusion), channel_id=1, source_target_pairs={{0,2},{1,3},{2,0},{3,1},{4,6},{5,7},{6,4},{7,5},{8,10},{9,11},{10,... | collective-permute-start | bytes 921608 | tf_op jit(solution)/shard_map/ppermute | solution.py:15
  16.2 0.0 copy-done
  16.2 0.0 copy-done.1
  16.2 0.0 copy-done.2
  16.2 0.2 convolution_select_fusion
  16.4 0.1 copy.23
  16.5 0.1 reshape.73
  16.6 0.1 copy.24
  16.6 7.6 %collective-permute-done.1 = f32[960,2,40]{0,2,1:T(8,128)S(1)} collective-permute-done((f32[960,2,40]{0,2,1:T(8,128)S(1)}, f32[960,2,40]{0,2,1:T(8,128)S(1)}, u32[]{:S(2)}, u32[]{:S(2)}) %collective-permute-start.1) | collective-permute-done | bytes 307232 | tf_op jit(solution)/shard_map/ppermute | solution.py:15
  24.2 0.1 dynamic-slice_bitcast_fusion.1
  24.4 1.8 %collective-permute-start.3 = (f32[648,40]{0,1:T(8,128)S(1)}, f32[648,40]{0,1:T(8,128)S(1)}, u32[]{:S(2)}, u32[]{:S(2)}) collective-permute-start(f32[648,40]{0,1:T(8,128)S(1)} %get-tuple-element.11), channel_id=1, source_target_pairs={{28,0},{0,4},{4,8},{8,12},{12,16},{16,20},{20,24},{24,28},{29,1},{... | collective-permute-start | bytes 311048 | tf_op jit(solution)/shard_map/ppermute | solution.py:10
  26.1 3.1 %collective-permute-start.4 = (f32[648,40]{0,1:T(8,128)S(1)}, f32[648,40]{0,1:T(8,128)S(1)}, u32[]{:S(2)}, u32[]{:S(2)}) collective-permute-start(f32[648,40]{0,1:T(8,128)S(1)} %get-tuple-element.12), channel_id=1, source_target_pairs={{4,0},{8,4},{12,8},{16,12},{20,16},{24,20},{28,24},{0,28},{5,1},{9... | collective-permute-start | bytes 311048 | tf_op jit(solution)/shard_map/ppermute | solution.py:10
  29.2 0.0 collective-permute-start.2
  29.2 0.1 reshape.75
  29.3 2.8 %collective-permute-done.3 = f32[648,40]{0,1:T(8,128)S(1)} collective-permute-done((f32[648,40]{0,1:T(8,128)S(1)}, f32[648,40]{0,1:T(8,128)S(1)}, u32[]{:S(2)}, u32[]{:S(2)}) %collective-permute-start.3) | collective-permute-done | bytes 103712 | tf_op jit(solution)/shard_map/ppermute | solution.py:10
  32.1 0.1 copy.25
  32.2 0.1 reshape.74
  32.2 1.0 %collective-permute-done.4 = f32[648,40]{0,1:T(8,128)S(1)} collective-permute-done((f32[648,40]{0,1:T(8,128)S(1)}, f32[648,40]{0,1:T(8,128)S(1)}, u32[]{:S(2)}, u32[]{:S(2)}) %collective-permute-start.4) | collective-permute-done | bytes 103712 | tf_op jit(solution)/shard_map/ppermute | solution.py:10
  33.3 0.1 copy.28
  33.4 0.1 reshape.78
  33.4 0.1 pad_maximum_fusion.4
  33.5 0.1 pad_maximum_fusion.3
  33.6 0.0 collective-permute-done.2
  33.6 0.1 select_bitcast_fusion
  33.7 0.2 fusion.4
  33.8 0.1 pad_maximum_fusion
  34.0 0.1 reshape.77
  34.1 0.8 %convolution_bitcast_fusion = f32[1,8,20,40]{3,2,1,0:T(8,128)S(1)} fusion(f32[8,20,960]{2,1,0:T(8,128)S(1)} %reshape.77, f32[960,2,40]{0,2,1:T(8,128)S(1)} %add.12, s32[]{:T(128)S(6)} %select_n.46, f32[960]{0:T(1024)S(1)} %pad_maximum_fusion.4), kind=kOutput, calls=%fused_computation.4 | convolution fusion | flops 73766400 | bytes 979972 | tf_op jit(solution)/shard_map/ib,ic->bc/dot_general | solution.py:45
  34.9 0.5 %convolution_bitcast_fusion.1 = f32[1,8,20,40]{3,2,1,0:T(8,128)S(1)} fusion(f32[8,20,640]{2,1,0:T(8,128)S(1)} %reshape.79, f32[648,40]{0,1:T(8,128)S(1)} %collective-permute-done.4, f32[640]{0:T(1024)S(1)} %get-tuple-element.14), kind=kOutput, calls=%fused_computation.5 | convolution fusion | flops 49177600 | bytes 623616 | tf_op jit(solution)/shard_map/ib,ic->bc/dot_general | solution.py:45
  35.4 0.5 %convolution_bitcast_fusion.2 = f32[1,8,20,40]{3,2,1,0:T(8,128)S(1)} fusion(f32[8,20,640]{2,1,0:T(8,128)S(1)} %reshape.72, f32[648,40]{0,1:T(8,128)S(1)} %collective-permute-done.3, f32[640]{0:T(1024)S(1)} %get-tuple-element.13), kind=kOutput, calls=%fused_computation.6 | convolution fusion | flops 49177600 | bytes 623616 | tf_op jit(solution)/shard_map/ib,ic->bc/dot_general | solution.py:45
  36.0 0.2 reshape.83
  36.2 11.6 %all_to_all.5 = f32[8,1,2400]{2,1,0:T(1,128)S(1)} all-to-all(f32[8,1,2400]{2,1,0:T(1,128)S(1)} %reshape.83), channel_id=1, replica_groups=mesh['elem'=8,'cuts'=4] {'elem'}, dimensions={0} | all-to-all | bytes 153600 | tf_op jit(solution)/shard_map/all_to_all | solution.py:84
  47.8 0.5 %broadcast.18 = f32[]{:T(128)} broadcast(f32[]{:T(128)} %constant.69), dimensions={} | broadcast | bytes 8 | tf_op jit(solution)/shard_map/all_to_all | solution.py:84
  48.3 0.8 %reduce = f32[8,2400]{1,0:T(8,128)S(1)} reduce(f32[8,1,2400]{2,1,0:T(1,128)S(1)} %all_to_all.5, f32[]{:T(128)} %broadcast.18), dimensions={1}, to_apply=%all_to_all.3.reduce_sub_computation | reduce | bytes 153604 | tf_op jit(solution)/shard_map/all_to_all | solution.py:84
  49.2 0.1 reshape.84
  49.3 0.7 %copy.30 = f32[8,3,20,40]{3,0,2,1:T(8,128)} copy(f32[8,3,20,40]{3,2,1,0:T(8,128)S(1)} %reshape.84) | data formatting | bytes 153600 | tf_op jit(solution)/shard_map/all_to_all | solution.py:84
  (9 shorter events, 0.2 us)
Async XLA Ops:
  0.0 16.2 %copy-start = (f32[4,16]{1,0:T(4,128)S(1)}, f32[4,16]{1,0:T(4,128)}, u32[]{:S(2)}) copy-start(f32[4,16]{1,0:T(4,128)} %param.11) | copy-start | bytes 772
  0.0 16.2 %copy-start.1 = (s32[1,20]{1,0:T(1,128)S(1)}, s32[1,20]{1,0:T(1,128)}, u32[]{:S(2)}) copy-start(s32[1,20]{1,0:T(1,128)} %param.9) | copy-start | bytes 244
  0.0 16.2 %copy-start.2 = (s32[1,20]{1,0:T(1,128)S(1)}, s32[1,20]{1,0:T(1,128)}, u32[]{:S(2)}) copy-start(s32[1,20]{1,0:T(1,128)} %param.10) | copy-start | bytes 244
  11.4 1.8 %collective-permute-start = (f32[960,2,40]{0,2,1:T(8,128)S(1)}, f32[960,2,40]{0,2,1:T(8,128)S(1)}, u32[]{:S(2)}, u32[]{:S(2)}) collective-permute-start(f32[960,2,40]{0,2,1:T(8,128)S(1)} %select_bitcast_fusion.2), channel_id=1, source_target_pairs={{0,1},{1,0},{2,3},{3,2},{4,5},{5,4},{6,7},{7,6},{8,9},{9,8},{10,11... | collective-permute-start | bytes 921608 | tf_op jit(solution)/shard_map/ppermute | solution.py:15
  13.2 11.0 %collective-permute-start.1 = (f32[960,2,40]{0,2,1:T(8,128)S(1)}, f32[960,2,40]{0,2,1:T(8,128)S(1)}, u32[]{:S(2)}, u32[]{:S(2)}) collective-permute-start(f32[960,2,40]{0,2,1:T(8,128)S(1)} %bitcast_add_fusion), channel_id=1, source_target_pairs={{0,2},{1,3},{2,0},{3,1},{4,6},{5,7},{6,4},{7,5},{8,10},{9,11},{10,... | collective-permute-start | bytes 921608 | tf_op jit(solution)/shard_map/ppermute | solution.py:15
  24.4 7.7 %collective-permute-start.3 = (f32[648,40]{0,1:T(8,128)S(1)}, f32[648,40]{0,1:T(8,128)S(1)}, u32[]{:S(2)}, u32[]{:S(2)}) collective-permute-start(f32[648,40]{0,1:T(8,128)S(1)} %get-tuple-element.11), channel_id=1, source_target_pairs={{28,0},{0,4},{4,8},{8,12},{12,16},{16,20},{20,24},{24,28},{29,1},{... | collective-permute-start | bytes 311048 | tf_op jit(solution)/shard_map/ppermute | solution.py:10
  26.1 7.2 %collective-permute-start.4 = (f32[648,40]{0,1:T(8,128)S(1)}, f32[648,40]{0,1:T(8,128)S(1)}, u32[]{:S(2)}, u32[]{:S(2)}) collective-permute-start(f32[648,40]{0,1:T(8,128)S(1)} %get-tuple-element.12), channel_id=1, source_target_pairs={{4,0},{8,4},{12,8},{16,12},{20,16},{24,20},{28,24},{0,28},{5,1},{9... | collective-permute-start | bytes 311048 | tf_op jit(solution)/shard_map/ppermute | solution.py:10
  29.2 4.4 %collective-permute-start.2 = (f32[960,2,40]{0,2,1:T(8,128)S(1)}, f32[960,2,40]{0,2,1:T(8,128)S(1)}, u32[]{:S(2)}, u32[]{:S(2)}) collective-permute-start(f32[960,2,40]{0,2,1:T(8,128)S(1)} %add.12), channel_id=1, source_target_pairs={{0,1},{1,0},{2,3},{3,2},{4,5},{5,4},{6,7},{7,6},{8,9},{9,8},{10,11... | collective-permute-start | bytes 921608 | tf_op jit(solution)/shard_map/ppermute | solution.py:15

commit v3 on v2

--- a/solution.py
+++ b/solution.py
@@ -1,6 +1,8 @@
 import jax
 import jax.numpy as jnp
 from jax import lax
+from jax.experimental import pallas as pl
+from jax.experimental.pallas import tpu as pltpu
 from jax.sharding import PartitionSpec as P
 
 
@@ -41,6 +43,45 @@
     return jnp.stack([low, high], axis=2).reshape(rows, count * 2 * quarter)
 
 
+def coefficient_kernel(weight_ref, basis_ref, projector_ref, out_ref):
+    step = pl.program_id(0)
+    depth = weight_ref.shape[1]
+    column = jnp.transpose(jnp.broadcast_to(weight_ref[...], (8, depth)))[:, :1]
+    scaled = (basis_ref[...].astype(jnp.float32) * column).astype(jnp.bfloat16)
+    product = jnp.dot(projector_ref[...], scaled, preferred_element_type=jnp.float32)
+
+    @pl.when(step == 0)
+    def _():
+        out_ref[...] = product
+
+    @pl.when(step > 0)
+    def _():
+        out_ref[...] += product
+
+
+def partial_coefficients(flat_projectors, basis, weight):
+    rows, points = flat_projectors.shape
+    width = basis.shape[1]
+    depth = min(points, 1024)
+    return pl.pallas_call(
+        coefficient_kernel,
+        out_shape=jax.ShapeDtypeStruct((rows, width), jnp.float32),
+        grid=(points // depth,),
+        in_specs=[
+            pl.BlockSpec((1, depth), lambda k: (0, k)),
+            pl.BlockSpec((depth, width), lambda k: (k, 0)),
+            pl.BlockSpec((rows, depth), lambda k: (0, k)),
+        ],
+        out_specs=pl.BlockSpec((rows, width), lambda k: (0, 0)),
+        compiler_params=pltpu.CompilerParams(dimension_semantics=("arbitrary",)),
+        cost_estimate=pl.CostEstimate(
+            flops=2 * rows * points * width,
+            bytes_accessed=2 * rows * points + 2 * points * width + 4 * points + 4 * rows * width,
+            transcendentals=0,
+        ),
+    )(weight.reshape(1, points), basis, flat_projectors)
+
+
 def pair_block(left, right):
     return jnp.einsum("ib,ic->bc", left, right, precision=lax.Precision.HIGHEST)
 
@@ -50,9 +91,8 @@
     groups, atoms, slots, points = projectors.shape[1:]
     span = atoms * slots
     quarter = width // lax.axis_size("cuts")
-    scaled = (basis[0].astype(jnp.float32) * quad_weight[0][:, None]).astype(jnp.bfloat16)
-    partial_value = jnp.dot(
-        projectors[0].reshape(groups * span, points), scaled, preferred_element_type=jnp.float32
+    partial_value = partial_coefficients(
+        projectors[0].reshape(groups * span, points), basis[0], quad_weight[0]
     )
     onehot = (
         species[0][:, None] == jnp.arange(gamma_table.shape[0], dtype=jnp.int32)[None, :]

time: 50.2 us -> 59.8 us (1.19)
  Pallas kernels: 0 us -> 13.3 us
  matrix products: 13.4 us -> 2.03 us
  local copies, waits for them, and re-layouts: 2.52 us -> 9.82 us
    pallas_call x0 -> x1, Pallas kernels: none -> 13.3 us  [partial_coefficients(): pl.pallas_call(coefficient_kernel, out_shape=jax.ShapeDtypeStruct((rows,...]
    dot_general x1 -> x0, matrix products: 11.3 us -> none  [local(): jnp.dot(projectors[0].reshape(groups * span, points), scaled, preferred_e...]
    unnamed x8 -> x9, local copies, waits for them, and re-layouts: 0.37 us -> 6.05 us
    pallas_call x0 -> x1, local copies, waits for them, and re-layouts: none -> 1.5 us  [partial_coefficients(): pl.pallas_call(coefficient_kernel, out_shape=jax.ShapeDtypeStruct((rows,...]
where the time goes in v3:
time: 59.8 us; the launch traced here: 59.3 us
  Pallas kernels  13.3 us (22%)
  waiting for transfers between devices  12.6 us (21%)
  blocking collectives  11.6 us (19%)
  local copies, waits for them, and re-layouts  9.82 us (16%)
  starting transfers between devices  8.34 us (14%)
  matrix products  2.03 us (3%)
  other arithmetic  1.47 us (2%)
    pallas_call x1, Pallas kernels, partial_coefficients(): pl.pallas_call(coefficient_kernel, out_shape=jax.ShapeDtypeStruct((rows,...  13.3 us
    all_to_all x1, blocking collectives, local(): lax.all_to_all(pieces, 'elem', split_axis=0, concat_axis=0, tiled=True)  11.6 us
    ppermute x3, waiting for transfers between devices, swapped(): return lax.ppermute(block, axis, [(i, i ^ bit) for i in devices])  8.81 us
    unnamed x9, local copies, waits for them, and re-layouts  6.05 us
    ppermute x2, starting transfers between devices, passed_along(): return lax.ppermute(block, axis, route)  4.87 us
    ppermute x2, waiting for transfers between devices, passed_along(): return lax.ppermute(block, axis, route)  3.81 us
    ppermute x3, starting transfers between devices, swapped(): return lax.ppermute(block, axis, [(i, i ^ bit) for i in devices])  3.47 us
    dot_general x3, matrix products, pair_block(): return jnp.einsum('ib,ic->bc', left, right, precision=lax.Precision.HIGHEST)  1.83 us
  transfers between devices with their start and end apart: 5, of which 4 were waited for; matrix products, arithmetic and copies ran while one was open for 2% of the time, Pallas kernels for 0%

profile of v3, /device:TPU:0, one launch (start us, length us, event | category | flops | bytes accessed | tf_op | source)
XLA Modules:
  0.0 59.3 jit_solution(16163472375729594241)
XLA Ops:
  0.0 0.0 copy-start
  0.0 5.7 %copy.27 = bf16[1,8192,160]{2,1,0:T(8,128)(2,1)} copy(bf16[1,8192,160]{1,2,0:T(8,128)(2,1)} %param.6) | data formatting | bytes 5242880 | tf_op args[0]
  5.7 0.0 copy-start.1
  5.7 0.0 copy-start.2
  5.7 13.3 %shard_map.64 = f32[960,160]{1,0:T(8,128)} custom-call(f32[1,8192]{1,0:T(1,128)} %weight_ref.1, bf16[8192,160]{1,0:T(8,128)(2,1)} %bitcast.62, bf16[960,8192]{1,0:T(8,128)(2,1)} %bitcast.63), custom_call_target="tpu_custom_call" | custom-call | flops 2516582400 | bytes 18997248 | tf_op jit(solution)/shard_map/pallas_call | solution.py:66
  19.0 1.5 %copy.28 = f32[960,160]{0,1:T(8,128)S(1)} copy(f32[960,160]{1,0:T(8,128)} %shard_map.64) | data formatting | bytes 1228800 | tf_op jit(solution)/shard_map/pallas_call | solution.py:66
  20.5 0.5 collective-permute-start
  21.1 1.3 %collective-permute-done = f32[960,2,40]{0,2,1:T(8,128)S(1)} collective-permute-done((f32[960,2,40]{0,2,1:T(8,128)S(1)}, f32[960,2,40]{0,2,1:T(8,128)S(1)}, u32[]{:S(2)}, u32[]{:S(2)}) %collective-permute-start) | collective-permute-done | bytes 307232 | tf_op jit(solution)/shard_map/ppermute | solution.py:17
  22.3 0.1 fusion.3
  22.4 3.0 %collective-permute-start.1 = (f32[960,2,40]{0,2,1:T(8,128)S(1)}, f32[960,2,40]{0,2,1:T(8,128)S(1)}, u32[]{:S(2)}, u32[]{:S(2)}) collective-permute-start(f32[960,2,40]{0,2,1:T(8,128)S(1)} %fusion.3), channel_id=1, source_target_pairs={{0,2},{1,3},{2,0},{3,1},{4,6},{5,7},{6,4},{7,5},{8,10},{9,11},{10,... | collective-permute-start | bytes 921608 | tf_op jit(solution)/shard_map/ppermute | solution.py:17
  25.3 0.0 copy-done
  25.3 0.0 copy-done.1
  25.3 0.0 copy-done.2
  25.4 0.2 convolution_select_fusion
  25.6 0.1 copy.34
  25.6 0.1 reshape.65
  25.7 0.1 copy.35
  25.8 7.6 %collective-permute-done.1 = f32[960,2,40]{0,2,1:T(8,128)S(1)} collective-permute-done((f32[960,2,40]{0,2,1:T(8,128)S(1)}, f32[960,2,40]{0,2,1:T(8,128)S(1)}, u32[]{:S(2)}, u32[]{:S(2)}) %collective-permute-start.1) | collective-permute-done | bytes 307232 | tf_op jit(solution)/shard_map/ppermute | solution.py:17
  33.4 0.1 dynamic-slice_bitcast_fusion.1
  33.5 1.8 %collective-permute-start.3 = (f32[648,40]{0,1:T(8,128)S(1)}, f32[648,40]{0,1:T(8,128)S(1)}, u32[]{:S(2)}, u32[]{:S(2)}) collective-permute-start(f32[648,40]{0,1:T(8,128)S(1)} %get-tuple-element.11), channel_id=1, source_target_pairs={{28,0},{0,4},{4,8},{8,12},{12,16},{16,20},{20,24},{24,28},{29,1},{... | collective-permute-start | bytes 311048 | tf_op jit(solution)/shard_map/ppermute | solution.py:12
  35.3 3.1 %collective-permute-start.4 = (f32[648,40]{0,1:T(8,128)S(1)}, f32[648,40]{0,1:T(8,128)S(1)}, u32[]{:S(2)}, u32[]{:S(2)}) collective-permute-start(f32[648,40]{0,1:T(8,128)S(1)} %get-tuple-element.12), channel_id=1, source_target_pairs={{4,0},{8,4},{12,8},{16,12},{20,16},{24,20},{28,24},{0,28},{5,1},{9... | collective-permute-start | bytes 311048 | tf_op jit(solution)/shard_map/ppermute | solution.py:12
  38.4 0.0 collective-permute-start.2
  38.4 0.1 reshape.67
  38.5 2.8 %collective-permute-done.3 = f32[648,40]{0,1:T(8,128)S(1)} collective-permute-done((f32[648,40]{0,1:T(8,128)S(1)}, f32[648,40]{0,1:T(8,128)S(1)}, u32[]{:S(2)}, u32[]{:S(2)}) %collective-permute-start.3) | collective-permute-done | bytes 103712 | tf_op jit(solution)/shard_map/ppermute | solution.py:12
  41.3 0.1 copy.36
  41.3 0.1 reshape.66
  41.4 1.0 %collective-permute-done.4 = f32[648,40]{0,1:T(8,128)S(1)} collective-permute-done((f32[648,40]{0,1:T(8,128)S(1)}, f32[648,40]{0,1:T(8,128)S(1)}, u32[]{:S(2)}, u32[]{:S(2)}) %collective-permute-start.4) | collective-permute-done | bytes 103712 | tf_op jit(solution)/shard_map/ppermute | solution.py:12
  42.5 0.1 copy.40
  42.5 0.1 reshape.70
  42.6 0.1 pad_maximum_fusion.4
  42.7 0.1 pad_maximum_fusion.3
  42.8 0.0 collective-permute-done.2
  42.8 0.1 select_bitcast_fusion
  42.8 0.2 fusion
  43.1 0.1 copy.38
  43.2 0.1 reshape.69
  43.4 0.8 %convolution_bitcast_fusion = f32[1,8,20,40]{3,2,1,0:T(8,128)S(1)} fusion(f32[8,20,960]{2,1,0:T(8,128)S(1)} %reshape.69, f32[960,2,40]{0,2,1:T(8,128)S(1)} %add.12, s32[]{:T(128)S(6)} %select_n.46, f32[960]{0:T(1024)S(1)} %pad_maximum_fusion.4), kind=kOutput, calls=%fused_computation | convolution fusion | flops 73766400 | bytes 979972 | tf_op jit(solution)/shard_map/ib,ic->bc/dot_general | solution.py:86
  44.2 0.5 convolution_bitcast_fusion.1
  44.7 0.5 convolution_bitcast_fusion.2
  45.3 0.2 reshape.75
  45.5 11.6 %all_to_all.5 = f32[8,1,2400]{2,1,0:T(1,128)S(1)} all-to-all(f32[8,1,2400]{2,1,0:T(1,128)S(1)} %reshape.75), channel_id=1, replica_groups=mesh['elem'=8,'cuts'=4] {'elem'}, dimensions={0} | all-to-all | bytes 153600 | tf_op jit(solution)/shard_map/all_to_all | solution.py:124
  57.1 0.5 broadcast.14
  57.6 0.8 %reduce = f32[8,2400]{1,0:T(8,128)S(1)} reduce(f32[8,1,2400]{2,1,0:T(1,128)S(1)} %all_to_all.5, f32[]{:T(128)} %broadcast.14), dimensions={1}, to_apply=%all_to_all.3.reduce_sub_computation | reduce | bytes 153604 | tf_op jit(solution)/shard_map/all_to_all | solution.py:124
  58.5 0.1 reshape.76
  58.6 0.7 %copy.43 = f32[8,3,20,40]{3,0,2,1:T(8,128)} copy(f32[8,3,20,40]{3,2,1,0:T(8,128)S(1)} %reshape.76) | data formatting | bytes 153600 | tf_op jit(solution)/shard_map/all_to_all | solution.py:124
  (12 shorter events, 0.4 us)
Async XLA Ops:
  0.0 25.3 %copy-start = (f32[4,16]{1,0:T(4,128)S(1)}, f32[4,16]{1,0:T(4,128)}, u32[]{:S(2)}) copy-start(f32[4,16]{1,0:T(4,128)} %param.11) | copy-start | bytes 772
  5.7 19.7 %copy-start.1 = (s32[1,20]{1,0:T(1,128)S(1)}, s32[1,20]{1,0:T(1,128)}, u32[]{:S(2)}) copy-start(s32[1,20]{1,0:T(1,128)} %param.9) | copy-start | bytes 244
  5.7 19.7 %copy-start.2 = (s32[1,20]{1,0:T(1,128)S(1)}, s32[1,20]{1,0:T(1,128)}, u32[]{:S(2)}) copy-start(s32[1,20]{1,0:T(1,128)} %param.10) | copy-start | bytes 244
  20.5 1.8 %collective-permute-start = (f32[960,2,40]{0,2,1:T(8,128)S(1)}, f32[960,2,40]{0,2,1:T(8,128)S(1)}, u32[]{:S(2)}, u32[]{:S(2)}) collective-permute-start(f32[960,2,40]{0,2,1:T(8,128)S(1)} %select_bitcast_fusion.2), channel_id=1, source_target_pairs={{0,1},{1,0},{2,3},{3,2},{4,5},{5,4},{6,7},{7,6},{8,9},{9,8},{10,11... | collective-permute-start | bytes 921608 | tf_op jit(solution)/shard_map/ppermute | solution.py:17
  22.4 11.0 %collective-permute-start.1 = (f32[960,2,40]{0,2,1:T(8,128)S(1)}, f32[960,2,40]{0,2,1:T(8,128)S(1)}, u32[]{:S(2)}, u32[]{:S(2)}) collective-permute-start(f32[960,2,40]{0,2,1:T(8,128)S(1)} %fusion.3), channel_id=1, source_target_pairs={{0,2},{1,3},{2,0},{3,1},{4,6},{5,7},{6,4},{7,5},{8,10},{9,11},{10,... | collective-permute-start | bytes 921608 | tf_op jit(solution)/shard_map/ppermute | solution.py:17
  33.5 7.7 %collective-permute-start.3 = (f32[648,40]{0,1:T(8,128)S(1)}, f32[648,40]{0,1:T(8,128)S(1)}, u32[]{:S(2)}, u32[]{:S(2)}) collective-permute-start(f32[648,40]{0,1:T(8,128)S(1)} %get-tuple-element.11), channel_id=1, source_target_pairs={{28,0},{0,4},{4,8},{8,12},{12,16},{16,20},{20,24},{24,28},{29,1},{... | collective-permute-start | bytes 311048 | tf_op jit(solution)/shard_map/ppermute | solution.py:12
  35.3 7.2 %collective-permute-start.4 = (f32[648,40]{0,1:T(8,128)S(1)}, f32[648,40]{0,1:T(8,128)S(1)}, u32[]{:S(2)}, u32[]{:S(2)}) collective-permute-start(f32[648,40]{0,1:T(8,128)S(1)} %get-tuple-element.12), channel_id=1, source_target_pairs={{4,0},{8,4},{12,8},{16,12},{20,16},{24,20},{28,24},{0,28},{5,1},{9... | collective-permute-start | bytes 311048 | tf_op jit(solution)/shard_map/ppermute | solution.py:12
  38.4 4.4 %collective-permute-start.2 = (f32[960,2,40]{0,2,1:T(8,128)S(1)}, f32[960,2,40]{0,2,1:T(8,128)S(1)}, u32[]{:S(2)}, u32[]{:S(2)}) collective-permute-start(f32[960,2,40]{0,2,1:T(8,128)S(1)} %add.12), channel_id=1, source_target_pairs={{0,1},{1,0},{2,3},{3,2},{4,5},{5,4},{6,7},{7,6},{8,9},{9,8},{10,11... | collective-permute-start | bytes 921608 | tf_op jit(solution)/shard_map/ppermute | solution.py:17

commit v4 on v3

--- a/solution.py
+++ b/solution.py
@@ -45,10 +45,10 @@
 
 def coefficient_kernel(weight_ref, basis_ref, projector_ref, out_ref):
     step = pl.program_id(0)
-    depth = weight_ref.shape[1]
-    column = jnp.transpose(jnp.broadcast_to(weight_ref[...], (8, depth)))[:, :1]
-    scaled = (basis_ref[...].astype(jnp.float32) * column).astype(jnp.bfloat16)
-    product = jnp.dot(projector_ref[...], scaled, preferred_element_type=jnp.float32)
+    scaled = (basis_ref[...].astype(jnp.float32) * weight_ref[...]).astype(jnp.bfloat16)
+    product = lax.dot_general(
+        scaled, projector_ref[...], (((1,), (1,)), ((), ())), preferred_element_type=jnp.float32
+    )
 
     @pl.when(step == 0)
     def _():
@@ -59,27 +59,28 @@
         out_ref[...] += product
 
 
-def partial_coefficients(flat_projectors, basis, weight):
+def partial_coefficients(flat_projectors, basis_t, weight):
     rows, points = flat_projectors.shape
-    width = basis.shape[1]
+    width = basis_t.shape[0]
     depth = min(points, 1024)
-    return pl.pallas_call(
+    transposed = pl.pallas_call(
         coefficient_kernel,
-        out_shape=jax.ShapeDtypeStruct((rows, width), jnp.float32),
+        out_shape=jax.ShapeDtypeStruct((width, rows), jnp.float32),
         grid=(points // depth,),
         in_specs=[
             pl.BlockSpec((1, depth), lambda k: (0, k)),
-            pl.BlockSpec((depth, width), lambda k: (k, 0)),
+            pl.BlockSpec((width, depth), lambda k: (0, k)),
             pl.BlockSpec((rows, depth), lambda k: (0, k)),
         ],
-        out_specs=pl.BlockSpec((rows, width), lambda k: (0, 0)),
+        out_specs=pl.BlockSpec((width, rows), lambda k: (0, 0)),
         compiler_params=pltpu.CompilerParams(dimension_semantics=("arbitrary",)),
         cost_estimate=pl.CostEstimate(
             flops=2 * rows * points * width,
             bytes_accessed=2 * rows * points + 2 * points * width + 4 * points + 4 * rows * width,
             transcendentals=0,
         ),
-    )(weight.reshape(1, points), basis, flat_projectors)
+    )(weight.reshape(1, points), basis_t, flat_projectors)
+    return transposed.T
 
 
 def pair_block(left, right):
@@ -92,7 +93,7 @@
     span = atoms * slots
     quarter = width // lax.axis_size("cuts")
     partial_value = partial_coefficients(
-        projectors[0].reshape(groups * span, points), basis[0], quad_weight[0]
+        projectors[0].reshape(groups * span, points), basis[0].T, quad_weight[0]
     )
     onehot = (
         species[0][:, None] == jnp.arange(gamma_table.shape[0], dtype=jnp.int32)[None, :]

time: 59.8 us -> 53.4 us (0.89)
  local copies, waits for them, and re-layouts: 9.82 us -> 2.52 us
  other arithmetic: 1.47 us -> 3.6 us
  Pallas kernels: 13.3 us -> 12.3 us
    unnamed x9 -> x8, local copies, waits for them, and re-layouts: 6.05 us -> 0.37 us
    pallas_call x1 -> x0, local copies, waits for them, and re-layouts: 1.5 us -> none  [partial_coefficients(): pl.pallas_call(coefficient_kernel, out_shape=jax.ShapeDtypeStruct((rows,...]
    add x1, other arithmetic: 0.07 us -> 1.14 us  [summed_columns(): half = keep + swapped(send, axis, 1)]
    select_n x1, other arithmetic: 0.04 us -> 1.11 us  [summed_columns(): send = jnp.where(odd, pairs[:, :, 0], pairs[:, :, 1])]
    pallas_call x1, Pallas kernels: 13.3 us -> 12.3 us  [partial_coefficients(): pl.pallas_call(coefficient_kernel, out_shape=jax.ShapeDtypeStruct((width,...]
where the time goes in v4:
time: 53.4 us; the launch traced here: 53.1 us
  waiting for transfers between devices  12.6 us (24%)
  Pallas kernels  12.3 us (23%)
  blocking collectives  11.6 us (22%)
  starting transfers between devices  8.34 us (16%)
  other arithmetic  3.6 us (7%)
  local copies, waits for them, and re-layouts  2.52 us (5%)
  matrix products  2.03 us (4%)
    pallas_call x1, Pallas kernels, partial_coefficients(): pl.pallas_call(coefficient_kernel, out_shape=jax.ShapeDtypeStruct((width,...  12.3 us
    all_to_all x1, blocking collectives, local(): lax.all_to_all(pieces, 'elem', split_axis=0, concat_axis=0, tiled=True)  11.6 us
    ppermute x3, waiting for transfers between devices, swapped(): return lax.ppermute(block, axis, [(i, i ^ bit) for i in devices])  8.81 us
    ppermute x2, starting transfers between devices, passed_along(): return lax.ppermute(block, axis, route)  4.86 us
    ppermute x2, waiting for transfers between devices, passed_along(): return lax.ppermute(block, axis, route)  3.82 us
    ppermute x3, starting transfers between devices, swapped(): return lax.ppermute(block, axis, [(i, i ^ bit) for i in devices])  3.48 us
    dot_general x3, matrix products, pair_block(): return jnp.einsum('ib,ic->bc', left, right, precision=lax.Precision.HIGHEST)  1.83 us
    all_to_all x2, local copies, waits for them, and re-layouts, local(): lax.all_to_all(pieces, 'elem', split_axis=0, concat_axis=0, tiled=True)  1.25 us
  transfers between devices with their start and end apart: 5, of which 4 were waited for; matrix products, arithmetic and copies ran while one was open for 2% of the time, Pallas kernels for 0%

profile of v4, /device:TPU:0, one launch (start us, length us, event | category | flops | bytes accessed | tf_op | source)
XLA Modules:
  0.0 53.1 jit_solution(6184311544495392187)
XLA Ops:
  0.0 0.0 copy-start
  0.0 0.0 copy-start.1
  0.0 0.0 copy-start.2
  0.0 12.3 %shard_map.64 = f32[160,960]{1,0:T(8,128)} custom-call(f32[1,8192]{1,0:T(1,128)} %weight_ref.1, bf16[160,8192]{1,0:T(8,128)(2,1)} %bitcast.69, bf16[960,8192]{1,0:T(8,128)(2,1)} %bitcast.66), custom_call_target="tpu_custom_call" | custom-call | flops 2516582400 | bytes 18997248 | tf_op jit(solution)/shard_map/pallas_call | solution.py:66
  12.3 1.1 %select_bitcast_fusion.2 = f32[960,2,40]{0,2,1:T(8,128)S(1)} fusion(f32[960,2,2,40]{0,3,2,1:T(8,128)} %bitcast.67, pred[]{:T(512)S(6)} %ne.12), kind=kLoop, calls=%fused_computation.16 | loop fusion | flops 76800 | bytes 921601 | tf_op jit(solution)/shard_map/jit(_where)/select_n | solution.py:27
  13.4 0.5 collective-permute-start
  13.9 1.3 %collective-permute-done = f32[960,2,40]{0,2,1:T(8,128)S(1)} collective-permute-done((f32[960,2,40]{0,2,1:T(8,128)S(1)}, f32[960,2,40]{0,2,1:T(8,128)S(1)}, u32[]{:S(2)}, u32[]{:S(2)}) %collective-permute-start) | collective-permute-done | bytes 307232 | tf_op jit(solution)/shard_map/ppermute | solution.py:17
  15.2 1.1 %bitcast_add_fusion = f32[960,2,40]{0,2,1:T(8,128)S(1)} fusion(f32[960,2,40]{0,2,1:T(8,128)S(1)} %collective-permute-done, f32[960,2,2,40]{0,3,2,1:T(8,128)} %bitcast.68, pred[]{:T(512)S(6)} %ne.12), kind=kLoop, calls=%fused_computation.13 | loop fusion | flops 153600 | bytes 1228801 | tf_op jit(solution)/shard_map/add | solution.py:28
  16.3 3.0 %collective-permute-start.1 = (f32[960,2,40]{0,2,1:T(8,128)S(1)}, f32[960,2,40]{0,2,1:T(8,128)S(1)}, u32[]{:S(2)}, u32[]{:S(2)}) collective-permute-start(f32[960,2,40]{0,2,1:T(8,128)S(1)} %bitcast_add_fusion), channel_id=1, source_target_pairs={{0,2},{1,3},{2,0},{3,1},{4,6},{5,7},{6,4},{7,5},{8,10},{9,11},{10,... | collective-permute-start | bytes 921608 | tf_op jit(solution)/shard_map/ppermute | solution.py:17
  19.3 0.0 copy-done
  19.3 0.0 copy-done.1
  19.3 0.0 copy-done.2
  19.3 0.2 convolution_select_fusion
  19.5 0.1 copy.23
  19.6 0.1 reshape.65
  19.6 0.1 copy.24
  19.7 7.6 %collective-permute-done.1 = f32[960,2,40]{0,2,1:T(8,128)S(1)} collective-permute-done((f32[960,2,40]{0,2,1:T(8,128)S(1)}, f32[960,2,40]{0,2,1:T(8,128)S(1)}, u32[]{:S(2)}, u32[]{:S(2)}) %collective-permute-start.1) | collective-permute-done | bytes 307232 | tf_op jit(solution)/shard_map/ppermute | solution.py:17
  27.3 0.1 dynamic-slice_bitcast_fusion.1
  27.5 1.8 %collective-permute-start.3 = (f32[648,40]{0,1:T(8,128)S(1)}, f32[648,40]{0,1:T(8,128)S(1)}, u32[]{:S(2)}, u32[]{:S(2)}) collective-permute-start(f32[648,40]{0,1:T(8,128)S(1)} %get-tuple-element.11), channel_id=1, source_target_pairs={{28,0},{0,4},{4,8},{8,12},{12,16},{16,20},{20,24},{24,28},{29,1},{... | collective-permute-start | bytes 311048 | tf_op jit(solution)/shard_map/ppermute | solution.py:12
  29.2 3.1 %collective-permute-start.4 = (f32[648,40]{0,1:T(8,128)S(1)}, f32[648,40]{0,1:T(8,128)S(1)}, u32[]{:S(2)}, u32[]{:S(2)}) collective-permute-start(f32[648,40]{0,1:T(8,128)S(1)} %get-tuple-element.12), channel_id=1, source_target_pairs={{4,0},{8,4},{12,8},{16,12},{20,16},{24,20},{28,24},{0,28},{5,1},{9... | collective-permute-start | bytes 311048 | tf_op jit(solution)/shard_map/ppermute | solution.py:12
  32.3 0.0 collective-permute-start.2
  32.3 0.1 reshape.67
  32.4 2.8 %collective-permute-done.3 = f32[648,40]{0,1:T(8,128)S(1)} collective-permute-done((f32[648,40]{0,1:T(8,128)S(1)}, f32[648,40]{0,1:T(8,128)S(1)}, u32[]{:S(2)}, u32[]{:S(2)}) %collective-permute-start.3) | collective-permute-done | bytes 103712 | tf_op jit(solution)/shard_map/ppermute | solution.py:12
  35.2 0.1 copy.25
  35.2 0.1 reshape.66
  35.3 1.1 %collective-permute-done.4 = f32[648,40]{0,1:T(8,128)S(1)} collective-permute-done((f32[648,40]{0,1:T(8,128)S(1)}, f32[648,40]{0,1:T(8,128)S(1)}, u32[]{:S(2)}, u32[]{:S(2)}) %collective-permute-start.4) | collective-permute-done | bytes 103712 | tf_op jit(solution)/shard_map/ppermute | solution.py:12
  36.4 0.1 copy.28
  36.4 0.1 reshape.70
  36.5 0.1 pad_maximum_fusion.4
  36.6 0.1 pad_maximum_fusion.3
  36.7 0.0 collective-permute-done.2
  36.7 0.1 select_bitcast_fusion
  36.7 0.2 fusion
  37.0 0.1 reshape.69
  37.2 0.8 %convolution_bitcast_fusion = f32[1,8,20,40]{3,2,1,0:T(8,128)S(1)} fusion(f32[8,20,960]{2,1,0:T(8,128)S(1)} %reshape.69, f32[960,2,40]{0,2,1:T(8,128)S(1)} %add.12, s32[]{:T(128)S(6)} %select_n.46, f32[960]{0:T(1024)S(1)} %pad_maximum_fusion.4), kind=kOutput, calls=%fused_computation | convolution fusion | flops 73766400 | bytes 979972 | tf_op jit(solution)/shard_map/ib,ic->bc/dot_general | solution.py:87
  37.9 0.5 %convolution_bitcast_fusion.1 = f32[1,8,20,40]{3,2,1,0:T(8,128)S(1)} fusion(f32[8,20,640]{2,1,0:T(8,128)S(1)} %reshape.71, f32[648,40]{0,1:T(8,128)S(1)} %collective-permute-done.4, f32[640]{0:T(1024)S(1)} %get-tuple-element.14), kind=kOutput, calls=%fused_computation.1 | convolution fusion | flops 49177600 | bytes 623616 | tf_op jit(solution)/shard_map/ib,ic->bc/dot_general | solution.py:87
  38.5 0.5 convolution_bitcast_fusion.2
  39.1 0.2 reshape.75
  39.3 11.6 %all_to_all.5 = f32[8,1,2400]{2,1,0:T(1,128)S(1)} all-to-all(f32[8,1,2400]{2,1,0:T(1,128)S(1)} %reshape.75), channel_id=1, replica_groups=mesh['elem'=8,'cuts'=4] {'elem'}, dimensions={0} | all-to-all | bytes 153600 | tf_op jit(solution)/shard_map/all_to_all | solution.py:125
  50.9 0.5 broadcast.14
  51.4 0.8 %reduce = f32[8,2400]{1,0:T(8,128)S(1)} reduce(f32[8,1,2400]{2,1,0:T(1,128)S(1)} %all_to_all.5, f32[]{:T(128)} %broadcast.14), dimensions={1}, to_apply=%all_to_all.3.reduce_sub_computation | reduce | bytes 153604 | tf_op jit(solution)/shard_map/all_to_all | solution.py:125
  52.2 0.1 reshape.76
  52.4 0.7 %copy.30 = f32[8,3,20,40]{3,0,2,1:T(8,128)} copy(f32[8,3,20,40]{3,2,1,0:T(8,128)S(1)} %reshape.76) | data formatting | bytes 153600 | tf_op jit(solution)/shard_map/all_to_all | solution.py:125
  (9 shorter events, 0.3 us)
Async XLA Ops:
  0.0 19.3 %copy-start = (f32[4,16]{1,0:T(4,128)S(1)}, f32[4,16]{1,0:T(4,128)}, u32[]{:S(2)}) copy-start(f32[4,16]{1,0:T(4,128)} %param.11) | copy-start | bytes 772
  0.0 19.3 %copy-start.1 = (s32[1,20]{1,0:T(1,128)S(1)}, s32[1,20]{1,0:T(1,128)}, u32[]{:S(2)}) copy-start(s32[1,20]{1,0:T(1,128)} %param.9) | copy-start | bytes 244
  0.0 19.3 %copy-start.2 = (s32[1,20]{1,0:T(1,128)S(1)}, s32[1,20]{1,0:T(1,128)}, u32[]{:S(2)}) copy-start(s32[1,20]{1,0:T(1,128)} %param.10) | copy-start | bytes 244
  13.4 1.8 %collective-permute-start = (f32[960,2,40]{0,2,1:T(8,128)S(1)}, f32[960,2,40]{0,2,1:T(8,128)S(1)}, u32[]{:S(2)}, u32[]{:S(2)}) collective-permute-start(f32[960,2,40]{0,2,1:T(8,128)S(1)} %select_bitcast_fusion.2), channel_id=1, source_target_pairs={{0,1},{1,0},{2,3},{3,2},{4,5},{5,4},{6,7},{7,6},{8,9},{9,8},{10,11... | collective-permute-start | bytes 921608 | tf_op jit(solution)/shard_map/ppermute | solution.py:17
  16.3 11.0 %collective-permute-start.1 = (f32[960,2,40]{0,2,1:T(8,128)S(1)}, f32[960,2,40]{0,2,1:T(8,128)S(1)}, u32[]{:S(2)}, u32[]{:S(2)}) collective-permute-start(f32[960,2,40]{0,2,1:T(8,128)S(1)} %bitcast_add_fusion), channel_id=1, source_target_pairs={{0,2},{1,3},{2,0},{3,1},{4,6},{5,7},{6,4},{7,5},{8,10},{9,11},{10,... | collective-permute-start | bytes 921608 | tf_op jit(solution)/shard_map/ppermute | solution.py:17
  27.5 7.7 %collective-permute-start.3 = (f32[648,40]{0,1:T(8,128)S(1)}, f32[648,40]{0,1:T(8,128)S(1)}, u32[]{:S(2)}, u32[]{:S(2)}) collective-permute-start(f32[648,40]{0,1:T(8,128)S(1)} %get-tuple-element.11), channel_id=1, source_target_pairs={{28,0},{0,4},{4,8},{8,12},{12,16},{16,20},{20,24},{24,28},{29,1},{... | collective-permute-start | bytes 311048 | tf_op jit(solution)/shard_map/ppermute | solution.py:12
  29.2 7.2 %collective-permute-start.4 = (f32[648,40]{0,1:T(8,128)S(1)}, f32[648,40]{0,1:T(8,128)S(1)}, u32[]{:S(2)}, u32[]{:S(2)}) collective-permute-start(f32[648,40]{0,1:T(8,128)S(1)} %get-tuple-element.12), channel_id=1, source_target_pairs={{4,0},{8,4},{12,8},{16,12},{20,16},{24,20},{28,24},{0,28},{5,1},{9... | collective-permute-start | bytes 311048 | tf_op jit(solution)/shard_map/ppermute | solution.py:12
  32.3 4.4 %collective-permute-start.2 = (f32[960,2,40]{0,2,1:T(8,128)S(1)}, f32[960,2,40]{0,2,1:T(8,128)S(1)}, u32[]{:S(2)}, u32[]{:S(2)}) collective-permute-start(f32[960,2,40]{0,2,1:T(8,128)S(1)} %add.12), channel_id=1, source_target_pairs={{0,1},{1,0},{2,3},{3,2},{4,5},{5,4},{6,7},{7,6},{8,9},{9,8},{10,11... | collective-permute-start | bytes 921608 | tf_op jit(solution)/shard_map/ppermute | solution.py:17

commit v5 on v4

--- a/solution.py
+++ b/solution.py
@@ -17,30 +17,30 @@
     return lax.ppermute(block, axis, [(i, i ^ bit) for i in devices])
 
 
-def summed_columns(partial_value, axis, quarter):
-    rows = partial_value.shape[0]
+def summed_rows(partial_t, axis, quarter):
+    columns = partial_t.shape[1]
     size = lax.axis_size(axis)
     me = lax.axis_index(axis)
-    pairs = partial_value.reshape(rows, size // 2, 2, quarter)
+    pairs = partial_t.reshape(size // 2, 2, quarter, columns)
     odd = (me & 1) != 0
-    keep = jnp.where(odd, pairs[:, :, 1], pairs[:, :, 0])
-    send = jnp.where(odd, pairs[:, :, 0], pairs[:, :, 1])
+    keep = jnp.where(odd, pairs[:, 1], pairs[:, 0])
+    send = jnp.where(odd, pairs[:, 0], pairs[:, 1])
     half = keep + swapped(send, axis, 1)
     bit = 2
     while bit < size:
         half = half + swapped(half, axis, bit)
         bit *= 2
-    share = lax.dynamic_index_in_dim(half, me // 2, 1, keepdims=False)
+    share = lax.dynamic_index_in_dim(half, me // 2, 0, keepdims=False)
     return half, share
 
 
-def gathered_columns(half, axis):
-    rows, count, quarter = half.shape
+def gathered_rows(half, axis):
+    count, quarter, columns = half.shape
     odd = (lax.axis_index(axis) & 1) != 0
     other = swapped(half, axis, 1)
     low = jnp.where(odd, other, half)
     high = jnp.where(odd, half, other)
-    return jnp.stack([low, high], axis=2).reshape(rows, count * 2 * quarter)
+    return jnp.stack([low, high], axis=1).reshape(count * 2 * quarter, columns)
 
 
 def coefficient_kernel(weight_ref, basis_ref, projector_ref, out_ref):
@@ -62,7 +62,7 @@
 def partial_coefficients(flat_projectors, basis_t, weight):
     rows, points = flat_projectors.shape
     width = basis_t.shape[0]
-    depth = min(points, 1024)
+    depth = min(points, 2048)
     transposed = pl.pallas_call(
         coefficient_kernel,
         out_shape=jax.ShapeDtypeStruct((width, rows), jnp.float32),
@@ -80,11 +80,13 @@
             transcendentals=0,
         ),
     )(weight.reshape(1, points), basis_t, flat_projectors)
-    return transposed.T
+    return transposed
 
 
-def pair_block(left, right):
-    return jnp.einsum("ib,ic->bc", left, right, precision=lax.Precision.HIGHEST)
+def pair_block(left_t, right_t):
+    return lax.dot_general(
+        left_t, right_t, (((1,), (1,)), ((), ())), precision=lax.Precision.HIGHEST
+    )
 
 
 def local(basis, quad_weight, projectors, species, counts, gamma_table):
@@ -92,7 +94,7 @@
     groups, atoms, slots, points = projectors.shape[1:]
     span = atoms * slots
     quarter = width // lax.axis_size("cuts")
-    partial_value = partial_coefficients(
+    partial_t = partial_coefficients(
         projectors[0].reshape(groups * span, points), basis[0].T, quad_weight[0]
     )
     onehot = (
@@ -102,23 +104,22 @@
     active = (jnp.arange(slots, dtype=jnp.int32)[None, :] < counts[0][:, None]).astype(jnp.float32)
     energy = (table * active).reshape(span)
 
-    half, share = summed_columns(partial_value, "cuts", quarter)
-    energy_rows = -(-span // quarter)
-    packed_energy = jnp.pad(energy, (0, energy_rows * quarter - span)).reshape(energy_rows, quarter)
-    to_right = jnp.concatenate([share[span:], packed_energy], axis=0)
-    to_left = jnp.concatenate([share[: 2 * span], packed_energy], axis=0)
+    half, share = summed_rows(partial_t, "cuts", quarter)
+    energy_row = jnp.pad(energy, (0, span))[None]
+    to_right = jnp.concatenate([share[:, span:], energy_row], axis=0)
+    to_left = jnp.concatenate([share[:, : 2 * span], energy_row], axis=0)
     from_left = passed_along(to_right, "elem", 1)
     from_right = passed_along(to_left, "elem", -1)
-    full = gathered_columns(half, "cuts")
+    full_t = gathered_rows(half, "cuts")
 
-    left_energy = from_left[2 * span :].reshape(-1)[:span]
-    right_energy = from_right[2 * span :].reshape(-1)[:span]
+    left_energy = from_left[quarter, :span]
+    right_energy = from_right[quarter, :span]
     weight_left = jnp.concatenate([left_energy, energy])
     weight_diag = jnp.concatenate([left_energy, energy, right_energy])
     weight_right = jnp.concatenate([energy, right_energy])
-    block_left = pair_block(full[: 2 * span], weight_left[:, None] * from_left[: 2 * span])
-    block_diag = pair_block(full, weight_diag[:, None] * share)
-    block_right = pair_block(full[span:], weight_right[:, None] * from_right[: 2 * span])
+    block_left = pair_block(full_t[:, : 2 * span], from_left[:quarter] * weight_left[None])
+    block_diag = pair_block(full_t, share * weight_diag[None])
+    block_right = pair_block(full_t[:, span:], from_right[:quarter] * weight_right[None])
     owners = lax.axis_size("elem")
     stacked = jnp.stack([block_left, block_diag, block_right], axis=0)
     pieces = stacked.reshape(3, owners, width // owners, quarter).transpose(1, 0, 2, 3)

time: 53.4 us -> 51.5 us (0.964)
  Pallas kernels: 12.3 us -> 10 us
  waiting for transfers between devices: 12.6 us -> 14 us
    pallas_call x1, Pallas kernels: 12.3 us -> 10 us  [partial_coefficients(): pl.pallas_call(coefficient_kernel, out_shape=jax.ShapeDtypeStruct((width,...]
    ppermute x2, waiting for transfers between devices: 3.82 us -> 5.17 us  [passed_along(): return lax.ppermute(block, axis, route)]
  transfers between devices with their start and end apart: 5 -> 5, of which waited for: 4 -> 4; matrix products, arithmetic and copies ran while one was open for 2% -> 1% of each run, Pallas kernels for 0% -> 0%
where the time goes in v5:
time: 51.5 us; the launch traced here: 51.3 us
  waiting for transfers between devices  14 us (27%)
  blocking collectives  11.2 us (22%)
  Pallas kernels  10 us (19%)
  starting transfers between devices  8.42 us (16%)
  other arithmetic  3.43 us (7%)
  local copies, waits for them, and re-layouts  2.05 us (4%)
  matrix products  1.97 us (4%)
    all_to_all x1, blocking collectives, local(): lax.all_to_all(pieces, 'elem', split_axis=0, concat_axis=0, tiled=True)  11.2 us
    pallas_call x1, Pallas kernels, partial_coefficients(): pl.pallas_call(coefficient_kernel, out_shape=jax.ShapeDtypeStruct((width,...  10 us
    ppermute x3, waiting for transfers between devices, swapped(): return lax.ppermute(block, axis, [(i, i ^ bit) for i in devices])  8.85 us
    ppermute x2, waiting for transfers between devices, passed_along(): return lax.ppermute(block, axis, route)  5.17 us
    ppermute x2, starting transfers between devices, passed_along(): return lax.ppermute(block, axis, route)  4.94 us
    ppermute x3, starting transfers between devices, swapped(): return lax.ppermute(block, axis, [(i, i ^ bit) for i in devices])  3.48 us
    dot_general x3, matrix products, pair_block(): lax.dot_general(left_t, right_t, (((1,), (1,)), ((), ())), precision=lax....  1.77 us
    all_to_all x2, local copies, waits for them, and re-layouts, local(): lax.all_to_all(pieces, 'elem', split_axis=0, concat_axis=0, tiled=True)  1.25 us
  transfers between devices with their start and end apart: 5, of which 4 were waited for; matrix products, arithmetic and copies ran while one was open for 1% of the time, Pallas kernels for 0%

profile of v5, /device:TPU:0, one launch (start us, length us, event | category | flops | bytes accessed | tf_op | source)
XLA Modules:
  0.0 51.3 jit_solution(13117861682302542435)
XLA Ops:
  0.0 0.0 copy-start
  0.0 0.0 copy-start.2
  0.0 0.0 copy-start.1
  0.0 10.0 %shard_map.64 = f32[160,960]{1,0:T(8,128)} custom-call(f32[1,8192]{1,0:T(1,128)} %weight_ref.1, bf16[160,8192]{1,0:T(8,128)(2,1)} %bitcast.49, bf16[960,8192]{1,0:T(8,128)(2,1)} %bitcast.44), custom_call_target="tpu_custom_call" | custom-call | flops 2516582400 | bytes 18997248 | tf_op jit(solution)/shard_map/pallas_call | solution.py:66
  10.0 1.1 %select_bitcast_fusion.2 = f32[2,40,960]{2,1,0:T(8,128)S(1)} fusion(f32[2,2,40,960]{3,2,1,0:T(8,128)} %bitcast.47, pred[]{:T(512)S(6)} %ne.12), kind=kLoop, calls=%fused_computation.12 | loop fusion | flops 76800 | bytes 921601 | tf_op jit(solution)/shard_map/jit(_where)/select_n | solution.py:27
  11.1 0.5 %collective-permute-start = (f32[2,40,960]{2,1,0:T(8,128)S(1)}, f32[2,40,960]{2,1,0:T(8,128)S(1)}, u32[]{:S(2)}, u32[]{:S(2)}) collective-permute-start(f32[2,40,960]{2,1,0:T(8,128)S(1)} %select_bitcast_fusion.2), channel_id=1, source_target_pairs={{0,1},{1,0},{2,3},{3,2},{4,5},{5,4},{6,7},{7,6},{8,9},{9,8},{10,11... | collective-permute-start | bytes 921608 | tf_op jit(solution)/shard_map/ppermute | solution.py:17
  11.7 1.3 %collective-permute-done = f32[2,40,960]{2,1,0:T(8,128)S(1)} collective-permute-done((f32[2,40,960]{2,1,0:T(8,128)S(1)}, f32[2,40,960]{2,1,0:T(8,128)S(1)}, u32[]{:S(2)}, u32[]{:S(2)}) %collective-permute-start) | collective-permute-done | bytes 307232 | tf_op jit(solution)/shard_map/ppermute | solution.py:17
  12.9 1.1 %bitcast_add_fusion = f32[2,40,960]{2,1,0:T(8,128)S(1)} fusion(f32[2,40,960]{2,1,0:T(8,128)S(1)} %collective-permute-done, f32[2,2,40,960]{3,2,1,0:T(8,128)} %bitcast.48, pred[]{:T(512)S(6)} %ne.12), kind=kLoop, calls=%fused_computation.9 | loop fusion | flops 153600 | bytes 1228801 | tf_op jit(solution)/shard_map/add | solution.py:28
  14.1 3.0 %collective-permute-start.1 = (f32[2,40,960]{2,1,0:T(8,128)S(1)}, f32[2,40,960]{2,1,0:T(8,128)S(1)}, u32[]{:S(2)}, u32[]{:S(2)}) collective-permute-start(f32[2,40,960]{2,1,0:T(8,128)S(1)} %bitcast_add_fusion), channel_id=1, source_target_pairs={{0,2},{1,3},{2,0},{3,1},{4,6},{5,7},{6,4},{7,5},{8,10},{9,11},{10,... | collective-permute-start | bytes 921608 | tf_op jit(solution)/shard_map/ppermute | solution.py:17
  17.0 0.0 copy-done
  17.0 0.0 copy-done.2
  17.0 0.0 copy-done.1
  17.0 0.2 convolution_select_fusion
  17.2 0.1 copy.23
  17.3 0.1 reshape.41
  17.4 7.6 %collective-permute-done.1 = f32[2,40,960]{2,1,0:T(8,128)S(1)} collective-permute-done((f32[2,40,960]{2,1,0:T(8,128)S(1)}, f32[2,40,960]{2,1,0:T(8,128)S(1)}, u32[]{:S(2)}, u32[]{:S(2)}) %collective-permute-start.1) | collective-permute-done | bytes 307232 | tf_op jit(solution)/shard_map/ppermute | solution.py:17
  25.1 0.1 fusion.12
  25.2 1.8 %collective-permute-start.3 = (f32[41,640]{1,0:T(8,128)S(1)}, f32[41,640]{1,0:T(8,128)S(1)}, u32[]{:S(2)}, u32[]{:S(2)}) collective-permute-start(f32[41,640]{1,0:T(8,128)S(1)} %get-tuple-element.9), channel_id=1, source_target_pairs={{28,0},{0,4},{4,8},{8,12},{12,16},{16,20},{20,24},{24,28},{29,1},{... | collective-permute-start | bytes 314888 | tf_op jit(solution)/shard_map/ppermute | solution.py:12
  27.0 0.0 collective-permute-start.2
  27.0 3.2 %collective-permute-start.4 = (f32[41,640]{1,0:T(8,128)S(1)}, f32[41,640]{1,0:T(8,128)S(1)}, u32[]{:S(2)}, u32[]{:S(2)}) collective-permute-start(f32[41,640]{1,0:T(8,128)S(1)} %get-tuple-element.10), channel_id=1, source_target_pairs={{4,0},{8,4},{12,8},{16,12},{20,16},{24,20},{28,24},{0,28},{5,1},{9... | collective-permute-start | bytes 314888 | tf_op jit(solution)/shard_map/ppermute | solution.py:12
  30.2 2.8 %collective-permute-done.3 = f32[41,640]{1,0:T(8,128)S(1)} collective-permute-done((f32[41,640]{1,0:T(8,128)S(1)}, f32[41,640]{1,0:T(8,128)S(1)}, u32[]{:S(2)}, u32[]{:S(2)}) %collective-permute-start.3) | collective-permute-done | bytes 104992 | tf_op jit(solution)/shard_map/ppermute | solution.py:12
  33.0 2.4 %collective-permute-done.4 = f32[41,640]{1,0:T(8,128)S(1)} collective-permute-done((f32[41,640]{1,0:T(8,128)S(1)}, f32[41,640]{1,0:T(8,128)S(1)}, u32[]{:S(2)}, u32[]{:S(2)}) %collective-permute-start.4) | collective-permute-done | bytes 104992 | tf_op jit(solution)/shard_map/ppermute | solution.py:12
  35.4 0.1 pad_maximum_fusion.4
  35.5 0.1 pad_maximum_fusion.3
  35.5 0.0 collective-permute-done.2
  35.5 0.1 select_bitcast_fusion.1
  35.6 0.1 pad_maximum_fusion
  35.7 0.1 reshape.42
  35.7 0.5 fusion.2
  36.2 0.5 %fusion = f32[160,40]{1,0:T(8,128)S(1)} fusion(f32[160,960]{1,0:T(8,128)S(1)} %bitcast.46, f32[41,640]{1,0:T(8,128)S(1)} %collective-permute-done.4, f32[640]{0:T(1024)S(1)} %get-tuple-element.12), kind=kOutput, calls=%fused_computation.3 | convolution fusion | flops 49177600 | bytes 541696 | tf_op jit(solution)/shard_map/dot_general | solution.py:87
  36.8 0.8 %convolution_bitcast_fusion = f32[1,8,20,40]{3,2,1,0:T(8,128)S(1)} fusion(f32[8,20,960]{2,1,0:T(8,128)S(1)} %reshape.42, f32[2,40,960]{2,1,0:T(8,128)S(1)} %add.14, s32[]{:T(128)S(6)} %select_n.46, f32[960]{0:T(1024)S(1)} %pad_maximum_fusion.4), kind=kOutput, calls=%fused_computation | convolution fusion | flops 73766400 | bytes 979972 | tf_op jit(solution)/shard_map/dot_general | solution.py:87
  37.6 0.2 reshape.46
  37.9 11.2 %all_to_all.5 = f32[8,1,2400]{2,1,0:T(1,128)S(1)} all-to-all(f32[8,1,2400]{2,1,0:T(1,128)S(1)} %reshape.46), channel_id=1, replica_groups=mesh['elem'=8,'cuts'=4] {'elem'}, dimensions={0} | all-to-all | bytes 153600 | tf_op jit(solution)/shard_map/all_to_all | solution.py:126
  49.1 0.5 broadcast.20
  49.6 0.8 %reduce.4 = f32[8,2400]{1,0:T(8,128)S(1)} reduce(f32[8,1,2400]{2,1,0:T(1,128)S(1)} %all_to_all.5, f32[]{:T(128)} %broadcast.20), dimensions={1}, to_apply=%all_to_all.3.reduce_sub_computation | reduce | bytes 153604 | tf_op jit(solution)/shard_map/all_to_all | solution.py:126
  50.4 0.1 reshape.47
  50.6 0.7 %copy.27 = f32[8,3,20,40]{3,0,2,1:T(8,128)} copy(f32[8,3,20,40]{3,2,1,0:T(8,128)S(1)} %reshape.47) | data formatting | bytes 153600 | tf_op jit(solution)/shard_map/all_to_all | solution.py:126
  (11 shorter events, 0.2 us)
Async XLA Ops:
  0.0 17.0 %copy-start = (f32[4,16]{1,0:T(4,128)S(1)}, f32[4,16]{1,0:T(4,128)}, u32[]{:S(2)}) copy-start(f32[4,16]{1,0:T(4,128)} %param.11) | copy-start | bytes 772
  0.0 17.0 %copy-start.2 = (s32[1,20]{1,0:T(1,128)S(1)}, s32[1,20]{1,0:T(1,128)}, u32[]{:S(2)}) copy-start(s32[1,20]{1,0:T(1,128)} %param.10) | copy-start | bytes 244
  0.0 17.0 %copy-start.1 = (s32[1,20]{1,0:T(1,128)S(1)}, s32[1,20]{1,0:T(1,128)}, u32[]{:S(2)}) copy-start(s32[1,20]{1,0:T(1,128)} %param.9) | copy-start | bytes 244
  11.1 1.8 %collective-permute-start = (f32[2,40,960]{2,1,0:T(8,128)S(1)}, f32[2,40,960]{2,1,0:T(8,128)S(1)}, u32[]{:S(2)}, u32[]{:S(2)}) collective-permute-start(f32[2,40,960]{2,1,0:T(8,128)S(1)} %select_bitcast_fusion.2), channel_id=1, source_target_pairs={{0,1},{1,0},{2,3},{3,2},{4,5},{5,4},{6,7},{7,6},{8,9},{9,8},{10,11... | collective-permute-start | bytes 921608 | tf_op jit(solution)/shard_map/ppermute | solution.py:17
  14.1 11.0 %collective-permute-start.1 = (f32[2,40,960]{2,1,0:T(8,128)S(1)}, f32[2,40,960]{2,1,0:T(8,128)S(1)}, u32[]{:S(2)}, u32[]{:S(2)}) collective-permute-start(f32[2,40,960]{2,1,0:T(8,128)S(1)} %bitcast_add_fusion), channel_id=1, source_target_pairs={{0,2},{1,3},{2,0},{3,1},{4,6},{5,7},{6,4},{7,5},{8,10},{9,11},{10,... | collective-permute-start | bytes 921608 | tf_op jit(solution)/shard_map/ppermute | solution.py:17
  25.2 7.7 %collective-permute-start.3 = (f32[41,640]{1,0:T(8,128)S(1)}, f32[41,640]{1,0:T(8,128)S(1)}, u32[]{:S(2)}, u32[]{:S(2)}) collective-permute-start(f32[41,640]{1,0:T(8,128)S(1)} %get-tuple-element.9), channel_id=1, source_target_pairs={{28,0},{0,4},{4,8},{8,12},{12,16},{16,20},{20,24},{24,28},{29,1},{... | collective-permute-start | bytes 314888 | tf_op jit(solution)/shard_map/ppermute | solution.py:12
  27.0 8.5 %collective-permute-start.2 = (f32[2,40,960]{2,1,0:T(8,128)S(1)}, f32[2,40,960]{2,1,0:T(8,128)S(1)}, u32[]{:S(2)}, u32[]{:S(2)}) collective-permute-start(f32[2,40,960]{2,1,0:T(8,128)S(1)} %add.14), channel_id=1, source_target_pairs={{0,1},{1,0},{2,3},{3,2},{4,5},{5,4},{6,7},{7,6},{8,9},{9,8},{10,11... | collective-permute-start | bytes 921608 | tf_op jit(solution)/shard_map/ppermute | solution.py:17
  27.0 8.4 %collective-permute-start.4 = (f32[41,640]{1,0:T(8,128)S(1)}, f32[41,640]{1,0:T(8,128)S(1)}, u32[]{:S(2)}, u32[]{:S(2)}) collective-permute-start(f32[41,640]{1,0:T(8,128)S(1)} %get-tuple-element.10), channel_id=1, source_target_pairs={{4,0},{8,4},{12,8},{16,12},{20,16},{24,20},{28,24},{0,28},{5,1},{9... | collective-permute-start | bytes 314888 | tf_op jit(solution)/shard_map/ppermute | solution.py:12

commit v6 on v5

--- a/solution.py
+++ b/solution.py
@@ -1,3 +1,5 @@
+import functools
+
 import jax
 import jax.numpy as jnp
 from jax import lax
@@ -17,21 +19,27 @@
     return lax.ppermute(block, axis, [(i, i ^ bit) for i in devices])
 
 
-def summed_rows(partial_t, axis, quarter):
-    columns = partial_t.shape[1]
+def summed_rows(keep, send, axis):
     size = lax.axis_size(axis)
     me = lax.axis_index(axis)
-    pairs = partial_t.reshape(size // 2, 2, quarter, columns)
-    odd = (me & 1) != 0
-    keep = jnp.where(odd, pairs[:, 1], pairs[:, 0])
-    send = jnp.where(odd, pairs[:, 0], pairs[:, 1])
-    half = keep + swapped(send, axis, 1)
+    count = size // 2
+    quarter = keep.shape[0] // count
+    half = (keep + swapped(send, axis, 1)).reshape(count, quarter, keep.shape[1])
+    mine = me // 2
+    if count == 2:
+        theirs = 1 - mine
+        share = lax.dynamic_index_in_dim(half, mine, 0, keepdims=False) + swapped(
+            lax.dynamic_index_in_dim(half, theirs, 0, keepdims=False), axis, 2
+        )
+        other = swapped(share, axis, 2)
+        first = jnp.where(mine == 0, share, other)
+        second = jnp.where(mine == 0, other, share)
+        return jnp.stack([first, second]), share
     bit = 2
     while bit < size:
         half = half + swapped(half, axis, bit)
         bit *= 2
-    share = lax.dynamic_index_in_dim(half, me // 2, 0, keepdims=False)
-    return half, share
+    return half, lax.dynamic_index_in_dim(half, mine, 0, keepdims=False)
 
 
 def gathered_rows(half, axis):
@@ -43,7 +51,7 @@
     return jnp.stack([low, high], axis=1).reshape(count * 2 * quarter, columns)
 
 
-def coefficient_kernel(weight_ref, basis_ref, projector_ref, out_ref):
+def coefficient_kernel(quarter, parity_ref, weight_ref, basis_ref, projector_ref, keep_ref, send_ref, total_ref):
     step = pl.program_id(0)
     scaled = (basis_ref[...].astype(jnp.float32) * weight_ref[...]).astype(jnp.bfloat16)
     product = lax.dot_general(
@@ -52,35 +60,53 @@
 
     @pl.when(step == 0)
     def _():
-        out_ref[...] = product
+        total_ref[...] = product
 
     @pl.when(step > 0)
     def _():
-        out_ref[...] += product
+        total_ref[...] += product
+
+    @pl.when(step == pl.num_programs(0) - 1)
+    def _():
+        count = keep_ref.shape[0] // quarter
+        odd = parity_ref[0]
+        for t in range(count):
+            kept = pl.multiple_of((2 * t + odd) * quarter, 8)
+            sent = pl.multiple_of((2 * t + 1 - odd) * quarter, 8)
+            keep_ref[t * quarter : (t + 1) * quarter, :] = total_ref[pl.ds(kept, quarter), :]
+            send_ref[t * quarter : (t + 1) * quarter, :] = total_ref[pl.ds(sent, quarter), :]
 
 
-def partial_coefficients(flat_projectors, basis_t, weight):
+def partial_coefficients(flat_projectors, basis_t, weight, parity, quarter):
     rows, points = flat_projectors.shape
     width = basis_t.shape[0]
-    depth = min(points, 2048)
-    transposed = pl.pallas_call(
-        coefficient_kernel,
-        out_shape=jax.ShapeDtypeStruct((width, rows), jnp.float32),
+    depth = min(points, 4096)
+    half = jax.ShapeDtypeStruct((width // 2, rows), jnp.float32)
+    grid_spec = pltpu.PrefetchScalarGridSpec(
+        num_scalar_prefetch=1,
         grid=(points // depth,),
         in_specs=[
-            pl.BlockSpec((1, depth), lambda k: (0, k)),
-            pl.BlockSpec((width, depth), lambda k: (0, k)),
-            pl.BlockSpec((rows, depth), lambda k: (0, k)),
+            pl.BlockSpec((1, depth), lambda k, p: (0, k)),
+            pl.BlockSpec((width, depth), lambda k, p: (0, k)),
+            pl.BlockSpec((rows, depth), lambda k, p: (0, k)),
         ],
-        out_specs=pl.BlockSpec((width, rows), lambda k: (0, 0)),
+        out_specs=[
+            pl.BlockSpec((width // 2, rows), lambda k, p: (0, 0)),
+            pl.BlockSpec((width // 2, rows), lambda k, p: (0, 0)),
+        ],
+        scratch_shapes=[pltpu.VMEM((width, rows), jnp.float32)],
+    )
+    return pl.pallas_call(
+        functools.partial(coefficient_kernel, quarter),
+        out_shape=(half, half),
+        grid_spec=grid_spec,
         compiler_params=pltpu.CompilerParams(dimension_semantics=("arbitrary",)),
         cost_estimate=pl.CostEstimate(
             flops=2 * rows * points * width,
             bytes_accessed=2 * rows * points + 2 * points * width + 4 * points + 4 * rows * width,
             transcendentals=0,
         ),
-    )(weight.reshape(1, points), basis_t, flat_projectors)
-    return transposed
+    )(parity, weight.reshape(1, points), basis_t, flat_projectors)
 
 
 def pair_block(left_t, right_t):
@@ -94,8 +120,9 @@
     groups, atoms, slots, points = projectors.shape[1:]
     span = atoms * slots
     quarter = width // lax.axis_size("cuts")
-    partial_t = partial_coefficients(
-        projectors[0].reshape(groups * span, points), basis[0].T, quad_weight[0]
+    parity = (lax.axis_index("cuts") % 2).astype(jnp.int32).reshape(1)
+    keep, send = partial_coefficients(
+        projectors[0].reshape(groups * span, points), basis[0].T, quad_weight[0], parity, quarter
     )
     onehot = (
         species[0][:, None] == jnp.arange(gamma_table.shape[0], dtype=jnp.int32)[None, :]
@@ -104,7 +131,7 @@
     active = (jnp.arange(slots, dtype=jnp.int32)[None, :] < counts[0][:, None]).astype(jnp.float32)
     energy = (table * active).reshape(span)
 
-    half, share = summed_rows(partial_t, "cuts", quarter)
+    half, share = summed_rows(keep, send, "cuts")
     energy_row = jnp.pad(energy, (0, span))[None]
     to_right = jnp.concatenate([share[:, span:], energy_row], axis=0)
     to_left = jnp.concatenate([share[:, : 2 * span], energy_row], axis=0)

time: 51.5 us -> 47.5 us (0.922)
  waiting for transfers between devices: 14 us -> 8.76 us
  starting transfers between devices: 8.42 us -> 10 us
  other arithmetic: 3.43 us -> 2.24 us
  blocking collectives: 11.2 us -> 12.3 us
    ppermute x3 -> x4, waiting for transfers between devices: 8.85 us -> 5.56 us  [swapped(): return lax.ppermute(block, axis, [(i, i ^ bit) for i in devices])]
    ppermute x2, waiting for transfers between devices: 5.17 us -> 3.2 us  [passed_along(): return lax.ppermute(block, axis, route)]
    ppermute x3 -> x4, starting transfers between devices: 3.48 us -> 5 us  [swapped(): return lax.ppermute(block, axis, [(i, i ^ bit) for i in devices])]
    select_n x1 -> x0, other arithmetic: 1.11 us -> none  [summed_rows(): send = jnp.where(odd, pairs[:, 0], pairs[:, 1])]
    all_to_all x1, blocking collectives: 11.2 us -> 12.3 us  [local(): lax.all_to_all(pieces, 'elem', split_axis=0, concat_axis=0, tiled=True)]
  transfers between devices with their start and end apart: 5 -> 6, of which waited for: 4 -> 4; matrix products, arithmetic and copies ran while one was open for 1% -> 1% of each run, Pallas kernels for 0% -> 0%
where the time goes in v6:
time: 47.5 us; the launch traced here: 47.3 us
  blocking collectives  12.3 us (26%)
  starting transfers between devices  10 us (21%)
  Pallas kernels  9.84 us (21%)
  waiting for transfers between devices  8.76 us (18%)
  other arithmetic  2.24 us (5%)
  local copies, waits for them, and re-layouts  2.05 us (4%)
  matrix products  1.97 us (4%)
    all_to_all x1, blocking collectives, local(): lax.all_to_all(pieces, 'elem', split_axis=0, concat_axis=0, tiled=True)  12.3 us
    pallas_call x1, Pallas kernels, partial_coefficients(): pl.pallas_call(functools.partial(coefficient_kernel, quarter), out_shape=...  9.84 us
    ppermute x4, waiting for transfers between devices, swapped(): return lax.ppermute(block, axis, [(i, i ^ bit) for i in devices])  5.56 us
    ppermute x4, starting transfers between devices, swapped(): return lax.ppermute(block, axis, [(i, i ^ bit) for i in devices])  5 us
    ppermute x2, starting transfers between devices, passed_along(): return lax.ppermute(block, axis, route)  5 us
    ppermute x2, waiting for transfers between devices, passed_along(): return lax.ppermute(block, axis, route)  3.2 us
    dot_general x3, matrix products, pair_block(): lax.dot_general(left_t, right_t, (((1,), (1,)), ((), ())), precision=lax....  1.76 us
    all_to_all x2, local copies, waits for them, and re-layouts, local(): lax.all_to_all(pieces, 'elem', split_axis=0, concat_axis=0, tiled=True)  1.25 us
  transfers between devices with their start and end apart: 6, of which 4 were waited for; matrix products, arithmetic and copies ran while one was open for 1% of the time, Pallas kernels for 0%

profile of v6, /device:TPU:0, one launch (start us, length us, event | category | flops | bytes accessed | tf_op | source)
XLA Modules:
  0.0 47.3 jit_solution(3645749636761049076)
XLA Ops:
  0.0 0.0 copy-start
  0.0 0.0 copy-start.2
  0.0 0.0 copy-start.1
  0.0 9.8 %shard_map.64 = (f32[80,960]{1,0:T(8,128)}, f32[80,960]{1,0:T(8,128)}) custom-call(s32[1]{0:T(128)} %bitcast.parity_ref, f32[1,8192]{1,0:T(1,128)} %weight_ref.1, bf16[160,8192]{1,0:T(8,128)(2,1)} %bitcast.37, bf16[960,8192]{1,0:T(8,128)(2,1)} %bitcast.34), custom_call_target="tpu_custom_call" | custom-call | flops 2516582400 | bytes 18997248 | tf_op jit(solution)/shard_map/pallas_call | solution.py:99
  9.8 0.5 collective-permute-start
  10.3 1.5 %collective-permute-done = f32[80,960]{1,0:T(8,128)S(1)} collective-permute-done((f32[80,960]{1,0:T(8,128)}, f32[80,960]{1,0:T(8,128)S(1)}, u32[]{:S(2)}, u32[]{:S(2)}) %collective-permute-start) | collective-permute-done | bytes 307232 | tf_op jit(solution)/shard_map/ppermute | solution.py:19
  11.8 1.0 %add.22 = f32[80,960]{1,0:T(8,128)S(1)} add(f32[80,960]{1,0:T(8,128)} %get-tuple-element.7, f32[80,960]{1,0:T(8,128)S(1)} %collective-permute-done) | non-fusion elementwise | flops 76800 | bytes 921600 | tf_op jit(solution)/shard_map/add | solution.py:27
  12.8 3.0 %collective-permute-start.1 = (f32[40,960]{1,0:T(8,128)S(1)}, f32[40,960]{1,0:T(8,128)S(1)}, u32[]{:S(2)}, u32[]{:S(2)}) collective-permute-start(f32[40,960]{1,0:T(8,128)S(1)} %dynamic-slice_bitcast_fusion), channel_id=1, source_target_pairs={{0,2},{1,3},{2,0},{3,1},{4,6},{5,7},{6,4},{7,5},{8,10},{9,11},{10,... | collective-permute-start | bytes 460808 | tf_op jit(solution)/shard_map/ppermute | solution.py:19
  15.8 0.0 copy-done
  15.8 0.0 copy-done.2
  15.8 0.0 copy-done.1
  15.8 0.2 convolution_select_fusion
  16.0 0.1 copy.17
  16.1 0.1 reshape.34
  16.2 4.1 %collective-permute-done.1 = f32[40,960]{1,0:T(8,128)S(1)} collective-permute-done((f32[40,960]{1,0:T(8,128)S(1)}, f32[40,960]{1,0:T(8,128)S(1)}, u32[]{:S(2)}, u32[]{:S(2)}) %collective-permute-start.1) | collective-permute-done | bytes 153632 | tf_op jit(solution)/shard_map/ppermute | solution.py:19
  20.3 0.1 fusion.10
  20.4 1.8 %collective-permute-start.4 = (f32[41,640]{1,0:T(8,128)S(1)}, f32[41,640]{1,0:T(8,128)S(1)}, u32[]{:S(2)}, u32[]{:S(2)}) collective-permute-start(f32[41,640]{1,0:T(8,128)S(1)} %get-tuple-element.15), channel_id=1, source_target_pairs={{28,0},{0,4},{4,8},{8,12},{12,16},{16,20},{20,24},{24,28},{29,1},{... | collective-permute-start | bytes 314888 | tf_op jit(solution)/shard_map/ppermute | solution.py:14
  22.2 1.5 %collective-permute-start.2 = (f32[40,960]{1,0:T(8,128)S(1)}, f32[40,960]{1,0:T(8,128)S(1)}, u32[]{:S(2)}, u32[]{:S(2)}) collective-permute-start(f32[40,960]{1,0:T(8,128)S(1)} %bitcast_add_fusion), channel_id=1, source_target_pairs={{0,2},{1,3},{2,0},{3,1},{4,6},{5,7},{6,4},{7,5},{8,10},{9,11},{10,... | collective-permute-start | bytes 460808 | tf_op jit(solution)/shard_map/ppermute | solution.py:19
  23.7 3.2 %collective-permute-start.5 = (f32[41,640]{1,0:T(8,128)S(1)}, f32[41,640]{1,0:T(8,128)S(1)}, u32[]{:S(2)}, u32[]{:S(2)}) collective-permute-start(f32[41,640]{1,0:T(8,128)S(1)} %get-tuple-element.16), channel_id=1, source_target_pairs={{4,0},{8,4},{12,8},{16,12},{20,16},{24,20},{28,24},{0,28},{5,1},{9... | collective-permute-start | bytes 314888 | tf_op jit(solution)/shard_map/ppermute | solution.py:14
  26.9 1.2 %collective-permute-done.4 = f32[41,640]{1,0:T(8,128)S(1)} collective-permute-done((f32[41,640]{1,0:T(8,128)S(1)}, f32[41,640]{1,0:T(8,128)S(1)}, u32[]{:S(2)}, u32[]{:S(2)}) %collective-permute-start.4) | collective-permute-done | bytes 104992 | tf_op jit(solution)/shard_map/ppermute | solution.py:14
  28.2 0.0 collective-permute-done.2
  28.2 0.1 collective-permute-start.3
  28.3 2.0 %collective-permute-done.5 = f32[41,640]{1,0:T(8,128)S(1)} collective-permute-done((f32[41,640]{1,0:T(8,128)S(1)}, f32[41,640]{1,0:T(8,128)S(1)}, u32[]{:S(2)}, u32[]{:S(2)}) %collective-permute-start.5) | collective-permute-done | bytes 104992 | tf_op jit(solution)/shard_map/ppermute | solution.py:14
  30.3 0.1 pad_maximum_fusion.5
  30.4 0.1 pad_maximum_fusion.4
  30.5 0.0 collective-permute-done.3
  30.5 0.1 select_bitcast_fusion.1
  30.6 0.1 pad_maximum_fusion
  30.6 0.1 reshape.35
  30.7 0.5 fusion.2
  31.2 0.5 %fusion = f32[160,40]{1,0:T(8,128)S(1)} fusion(f32[160,960]{1,0:T(8,128)S(1)} %bitcast.36, f32[41,640]{1,0:T(8,128)S(1)} %collective-permute-done.5, f32[640]{0:T(1024)S(1)} %get-tuple-element.18), kind=kOutput, calls=%fused_computation.3 | convolution fusion | flops 49177600 | bytes 541696 | tf_op jit(solution)/shard_map/dot_general | solution.py:113
  31.8 0.8 %convolution_bitcast_fusion = f32[1,8,20,40]{3,2,1,0:T(8,128)S(1)} fusion(f32[8,20,960]{2,1,0:T(8,128)S(1)} %reshape.35, f32[40,960]{1,0:T(8,128)S(1)} %bitcast_add_fusion, f32[960]{0:T(1024)S(1)} %pad_maximum_fusion.5), kind=kOutput, calls=%fused_computation | convolution fusion | flops 73766400 | bytes 797440 | tf_op jit(solution)/shard_map/dot_general | solution.py:113
  32.6 0.2 reshape.39
  32.8 12.3 %all_to_all.5 = f32[8,1,2400]{2,1,0:T(1,128)S(1)} all-to-all(f32[8,1,2400]{2,1,0:T(1,128)S(1)} %reshape.39), channel_id=1, replica_groups=mesh['elem'=8,'cuts'=4] {'elem'}, dimensions={0} | all-to-all | bytes 153600 | tf_op jit(solution)/shard_map/all_to_all | solution.py:153
  45.1 0.5 %broadcast.14 = f32[]{:T(128)} broadcast(f32[]{:T(128)} %constant.80), dimensions={} | broadcast | bytes 8 | tf_op jit(solution)/shard_map/all_to_all | solution.py:153
  45.6 0.8 %reduce.4 = f32[8,2400]{1,0:T(8,128)S(1)} reduce(f32[8,1,2400]{2,1,0:T(1,128)S(1)} %all_to_all.5, f32[]{:T(128)} %broadcast.14), dimensions={1}, to_apply=%all_to_all.3.reduce_sub_computation | reduce | bytes 153604 | tf_op jit(solution)/shard_map/all_to_all | solution.py:153
  46.4 0.1 reshape.40
  46.6 0.7 %copy.21 = f32[8,3,20,40]{3,0,2,1:T(8,128)} copy(f32[8,3,20,40]{3,2,1,0:T(8,128)S(1)} %reshape.40) | data formatting | bytes 153600 | tf_op jit(solution)/shard_map/all_to_all | solution.py:153
  (13 shorter events, 0.2 us)
Async XLA Ops:
  0.0 15.8 %copy-start = (f32[4,16]{1,0:T(4,128)S(1)}, f32[4,16]{1,0:T(4,128)}, u32[]{:S(2)}) copy-start(f32[4,16]{1,0:T(4,128)} %param.11) | copy-start | bytes 772
  0.0 15.8 %copy-start.2 = (s32[1,20]{1,0:T(1,128)S(1)}, s32[1,20]{1,0:T(1,128)}, u32[]{:S(2)}) copy-start(s32[1,20]{1,0:T(1,128)} %param.10) | copy-start | bytes 244
  0.0 15.8 %copy-start.1 = (s32[1,20]{1,0:T(1,128)S(1)}, s32[1,20]{1,0:T(1,128)}, u32[]{:S(2)}) copy-start(s32[1,20]{1,0:T(1,128)} %param.9) | copy-start | bytes 244
  9.8 1.9 %collective-permute-start = (f32[80,960]{1,0:T(8,128)}, f32[80,960]{1,0:T(8,128)S(1)}, u32[]{:S(2)}, u32[]{:S(2)}) collective-permute-start(f32[80,960]{1,0:T(8,128)} %get-tuple-element.8), channel_id=1, source_target_pairs={{0,1},{1,0},{2,3},{3,2},{4,5},{5,4},{6,7},{7,6},{8,9},{9,8},{10,11... | collective-permute-start | bytes 921608 | tf_op jit(solution)/shard_map/ppermute | solution.py:19
  12.8 7.5 %collective-permute-start.1 = (f32[40,960]{1,0:T(8,128)S(1)}, f32[40,960]{1,0:T(8,128)S(1)}, u32[]{:S(2)}, u32[]{:S(2)}) collective-permute-start(f32[40,960]{1,0:T(8,128)S(1)} %dynamic-slice_bitcast_fusion), channel_id=1, source_target_pairs={{0,2},{1,3},{2,0},{3,1},{4,6},{5,7},{6,4},{7,5},{8,10},{9,11},{10,... | collective-permute-start | bytes 460808 | tf_op jit(solution)/shard_map/ppermute | solution.py:19
  20.4 7.7 %collective-permute-start.4 = (f32[41,640]{1,0:T(8,128)S(1)}, f32[41,640]{1,0:T(8,128)S(1)}, u32[]{:S(2)}, u32[]{:S(2)}) collective-permute-start(f32[41,640]{1,0:T(8,128)S(1)} %get-tuple-element.15), channel_id=1, source_target_pairs={{28,0},{0,4},{4,8},{8,12},{12,16},{16,20},{20,24},{24,28},{29,1},{... | collective-permute-start | bytes 314888 | tf_op jit(solution)/shard_map/ppermute | solution.py:14
  22.2 6.0 %collective-permute-start.2 = (f32[40,960]{1,0:T(8,128)S(1)}, f32[40,960]{1,0:T(8,128)S(1)}, u32[]{:S(2)}, u32[]{:S(2)}) collective-permute-start(f32[40,960]{1,0:T(8,128)S(1)} %bitcast_add_fusion), channel_id=1, source_target_pairs={{0,2},{1,3},{2,0},{3,1},{4,6},{5,7},{6,4},{7,5},{8,10},{9,11},{10,... | collective-permute-start | bytes 460808 | tf_op jit(solution)/shard_map/ppermute | solution.py:19
  23.7 6.6 %collective-permute-start.5 = (f32[41,640]{1,0:T(8,128)S(1)}, f32[41,640]{1,0:T(8,128)S(1)}, u32[]{:S(2)}, u32[]{:S(2)}) collective-permute-start(f32[41,640]{1,0:T(8,128)S(1)} %get-tuple-element.16), channel_id=1, source_target_pairs={{4,0},{8,4},{12,8},{16,12},{20,16},{24,20},{28,24},{0,28},{5,1},{9... | collective-permute-start | bytes 314888 | tf_op jit(solution)/shard_map/ppermute | solution.py:14
  28.2 2.3 %collective-permute-start.3 = (f32[2,40,960]{2,1,0:T(8,128)S(1)}, f32[2,40,960]{2,1,0:T(8,128)S(1)}, u32[]{:S(2)}, u32[]{:S(2)}) collective-permute-start(f32[2,40,960]{2,1,0:T(8,128)S(1)} %pad_maximum_fusion.1), channel_id=1, source_target_pairs={{0,1},{1,0},{2,3},{3,2},{4,5},{5,4},{6,7},{7,6},{8,9},{9,8},{10,11... | collective-permute-start | bytes 921608 | tf_op jit(solution)/shard_map/ppermute | solution.py:19

commit v7 on v6

--- a/solution.py
+++ b/solution.py
@@ -19,7 +19,7 @@
     return lax.ppermute(block, axis, [(i, i ^ bit) for i in devices])
 
 
-def summed_rows(keep, send, axis):
+def chip_reduced(keep, send, axis):
     size = lax.axis_size(axis)
     me = lax.axis_index(axis)
     count = size // 2
@@ -27,19 +27,23 @@
     half = (keep + swapped(send, axis, 1)).reshape(count, quarter, keep.shape[1])
     mine = me // 2
     if count == 2:
-        theirs = 1 - mine
         share = lax.dynamic_index_in_dim(half, mine, 0, keepdims=False) + swapped(
-            lax.dynamic_index_in_dim(half, theirs, 0, keepdims=False), axis, 2
+            lax.dynamic_index_in_dim(half, 1 - mine, 0, keepdims=False), axis, 2
         )
-        other = swapped(share, axis, 2)
-        first = jnp.where(mine == 0, share, other)
-        second = jnp.where(mine == 0, other, share)
-        return jnp.stack([first, second]), share
+        return share, None
     bit = 2
     while bit < size:
         half = half + swapped(half, axis, bit)
         bit *= 2
-    return half, lax.dynamic_index_in_dim(half, mine, 0, keepdims=False)
+    return lax.dynamic_index_in_dim(half, mine, 0, keepdims=False), half
+
+
+def chip_gathered(share, half, axis):
+    if half is not None:
+        return half
+    first_here = (lax.axis_index(axis) // 2) == 0
+    other = swapped(share, axis, 2)
+    return jnp.stack([jnp.where(first_here, share, other), jnp.where(first_here, other, share)])
 
 
 def gathered_rows(half, axis):
@@ -77,8 +81,8 @@
             send_ref[t * quarter : (t + 1) * quarter, :] = total_ref[pl.ds(sent, quarter), :]
 
 
-def partial_coefficients(flat_projectors, basis_t, weight, parity, quarter):
-    rows, points = flat_projectors.shape
+def partial_coefficients(flat_projectors, basis_t, weight, parity, quarter, rows, row_index):
+    points = flat_projectors.shape[1]
     width = basis_t.shape[0]
     depth = min(points, 4096)
     half = jax.ShapeDtypeStruct((width // 2, rows), jnp.float32)
@@ -88,7 +92,7 @@
         in_specs=[
             pl.BlockSpec((1, depth), lambda k, p: (0, k)),
             pl.BlockSpec((width, depth), lambda k, p: (0, k)),
-            pl.BlockSpec((rows, depth), lambda k, p: (0, k)),
+            pl.BlockSpec((rows, depth), lambda k, p: (row_index, k)),
         ],
         out_specs=[
             pl.BlockSpec((width // 2, rows), lambda k, p: (0, 0)),
@@ -120,10 +124,6 @@
     groups, atoms, slots, points = projectors.shape[1:]
     span = atoms * slots
     quarter = width // lax.axis_size("cuts")
-    parity = (lax.axis_index("cuts") % 2).astype(jnp.int32).reshape(1)
-    keep, send = partial_coefficients(
-        projectors[0].reshape(groups * span, points), basis[0].T, quad_weight[0], parity, quarter
-    )
     onehot = (
         species[0][:, None] == jnp.arange(gamma_table.shape[0], dtype=jnp.int32)[None, :]
     ).astype(jnp.float32)
@@ -131,13 +131,25 @@
     active = (jnp.arange(slots, dtype=jnp.int32)[None, :] < counts[0][:, None]).astype(jnp.float32)
     energy = (table * active).reshape(span)
 
-    half, share = summed_rows(keep, send, "cuts")
+    parity = (lax.axis_index("cuts") % 2).astype(jnp.int32).reshape(1)
+    flat = projectors[0].reshape(groups * span, points)
+    keep_first, send_first = partial_coefficients(
+        flat, basis[0].T, quad_weight[0], parity, quarter, 2 * span, 0
+    )
+    keep_first, send_first, parity = lax.optimization_barrier((keep_first, send_first, parity))
+    keep_last, send_last = partial_coefficients(
+        flat, basis[0].T, quad_weight[0], parity, quarter, span, 2
+    )
+    share_first, half_first = chip_reduced(keep_first, send_first, "cuts")
     energy_row = jnp.pad(energy, (0, span))[None]
+    to_left = jnp.concatenate([share_first, energy_row], axis=0)
+    from_right = passed_along(to_left, "elem", -1)
+    share_last, half_last = chip_reduced(keep_last, send_last, "cuts")
+    share = jnp.concatenate([share_first, share_last], axis=1)
     to_right = jnp.concatenate([share[:, span:], energy_row], axis=0)
-    to_left = jnp.concatenate([share[:, : 2 * span], energy_row], axis=0)
     from_left = passed_along(to_right, "elem", 1)
-    from_right = passed_along(to_left, "elem", -1)
-    full_t = gathered_rows(half, "cuts")
+    half = None if half_first is None else jnp.concatenate([half_first, half_last], axis=2)
+    full_t = gathered_rows(chip_gathered(share, half, "cuts"), "cuts")
 
     left_energy = from_left[quarter, :span]
     right_energy = from_right[quarter, :span]

time: 47.5 us -> 50.4 us (1.061)
  Pallas kernels: 9.84 us -> 12.7 us
  waiting for transfers between devices: 8.76 us -> 9.28 us
    pallas_call x1 -> x2, Pallas kernels: 9.84 us -> 12.7 us  [partial_coefficients(): pl.pallas_call(functools.partial(coefficient_kernel, quarter), out_shape=...]
    ppermute x4 -> x6, waiting for transfers between devices: 5.56 us -> 5.86 us  [swapped(): return lax.ppermute(block, axis, [(i, i ^ bit) for i in devices])]
    add x2 -> x4, other arithmetic: 1.04 us -> 0.97 us  [the longest x2 0.94 us: chip_reduced(): keep + swapped(send, axis, 1)]
    ppermute x4 -> x6, starting transfers between devices: 5 us -> 4.98 us  [swapped(): return lax.ppermute(block, axis, [(i, i ^ bit) for i in devices])]
  transfers between devices with their start and end apart: 6 -> 8, of which waited for: 4 -> 5; matrix products, arithmetic and copies ran while one was open for 1% -> 3% of each run, Pallas kernels for 0% -> 10%
where the time goes in v7:
time: 50.4 us; the launch traced here: 50.2 us
  Pallas kernels  12.7 us (25%)
  blocking collectives  12 us (24%)
  starting transfers between devices  9.76 us (19%)
  waiting for transfers between devices  9.28 us (18%)
  other arithmetic  2.27 us (5%)
  local copies, waits for them, and re-layouts  1.98 us (4%)
  matrix products  1.97 us (4%)
    pallas_call x2, Pallas kernels, partial_coefficients(): pl.pallas_call(functools.partial(coefficient_kernel, quarter), out_shape=...  12.7 us
    all_to_all x1, blocking collectives, local(): lax.all_to_all(pieces, 'elem', split_axis=0, concat_axis=0, tiled=True)  12 us
    ppermute x6, waiting for transfers between devices, swapped(): return lax.ppermute(block, axis, [(i, i ^ bit) for i in devices])  5.86 us
    ppermute x6, starting transfers between devices, swapped(): return lax.ppermute(block, axis, [(i, i ^ bit) for i in devices])  4.98 us
    ppermute x2, starting transfers between devices, passed_along(): return lax.ppermute(block, axis, route)  4.78 us
    ppermute x2, waiting for transfers between devices, passed_along(): return lax.ppermute(block, axis, route)  3.42 us
    dot_general x3, matrix products, pair_block(): lax.dot_general(left_t, right_t, (((1,), (1,)), ((), ())), precision=lax....  1.77 us
    all_to_all x2, local copies, waits for them, and re-layouts, local(): lax.all_to_all(pieces, 'elem', split_axis=0, concat_axis=0, tiled=True)  1.25 us
  transfers between devices with their start and end apart: 8, of which 5 were waited for; matrix products, arithmetic and copies ran while one was open for 3% of the time, Pallas kernels for 10%

profile of v7, /device:TPU:0, one launch (start us, length us, event | category | flops | bytes accessed | tf_op | source)
XLA Modules:
  0.0 50.2 jit_solution(921329623372442407)
XLA Ops:
  0.0 0.0 copy-start
  0.0 0.0 copy-start.2
  0.0 0.0 copy-start.3
  0.0 7.5 %shard_map.64 = (f32[80,640]{1,0:T(8,128)}, f32[80,640]{1,0:T(8,128)}) custom-call(s32[1]{0:T(128)} %bitcast.parity_ref, f32[1,8192]{1,0:T(1,128)} %weight_ref.3, bf16[160,8192]{1,0:T(8,128)(2,1)} %bitcast.41, bf16[960,8192]{1,0:T(8,128)(2,1)} %bitcast.39), custom_call_target="tpu_custom_call" | custom-call | flops 1677721600 | bytes 13549568 | tf_op jit(solution)/shard_map/pallas_call | solution.py:103
  7.5 0.0 copy-start.1
  7.5 0.5 collective-permute-start
  7.9 5.2 %shard_map.65 = (f32[80,320]{1,0:T(8,128)}, f32[80,320]{1,0:T(8,128)}) custom-call(s32[1]{0:T(128)} %bitcast.parity_ref, f32[1,8192]{1,0:T(1,128)} %weight_ref.3, bf16[160,8192]{1,0:T(8,128)(2,1)} %bitcast.42, bf16[960,8192]{1,0:T(8,128)(2,1)} %bitcast.40), custom_call_target="tpu_custom_call" | custom-call | flops 838860800 | bytes 8101888 | tf_op jit(solution)/shard_map/pallas_call | solution.py:103
  13.1 0.1 collective-permute-start.2
  13.2 0.0 copy-done
  13.2 0.0 copy-done.2
  13.2 0.0 copy-done.3
  13.2 0.2 convolution_select_fusion
  13.4 0.1 copy.17
  13.5 0.1 reshape.38
  13.7 1.0 %collective-permute-done.2 = f32[80,320]{1,0:T(8,128)S(1)} collective-permute-done((f32[80,320]{1,0:T(8,128)}, f32[80,320]{1,0:T(8,128)S(1)}, u32[]{:S(2)}, u32[]{:S(2)}) %collective-permute-start.2) | collective-permute-done | bytes 102432 | tf_op jit(solution)/shard_map/ppermute | solution.py:19
  14.7 0.9 %add.35 = f32[80,320]{1,0:T(8,128)S(1)} add(f32[80,320]{1,0:T(8,128)} %get-tuple-element.17, f32[80,320]{1,0:T(8,128)S(1)} %collective-permute-done.2) | non-fusion elementwise | flops 25600 | bytes 307200 | tf_op jit(solution)/shard_map/add | solution.py:27
  15.6 2.7 %collective-permute-start.3 = (f32[40,320]{1,0:T(8,128)S(1)}, f32[40,320]{1,0:T(8,128)S(1)}, u32[]{:S(2)}, u32[]{:S(2)}) collective-permute-start(f32[40,320]{1,0:T(8,128)S(1)} %dynamic-slice_bitcast_fusion.1), channel_id=1, source_target_pairs={{0,2},{1,3},{2,0},{3,1},{4,6},{5,7},{6,4},{7,5},{8,10},{9,11},{10,... | collective-permute-start | bytes 153608 | tf_op jit(solution)/shard_map/ppermute | solution.py:19
  18.4 0.0 collective-permute-done
  18.4 0.0 copy-done.1
  18.4 0.1 collective-permute-start.1
  18.5 2.4 %collective-permute-done.3 = f32[40,320]{1,0:T(8,128)S(1)} collective-permute-done((f32[40,320]{1,0:T(8,128)S(1)}, f32[40,320]{1,0:T(8,128)S(1)}, u32[]{:S(2)}, u32[]{:S(2)}) %collective-permute-start.3) | collective-permute-done | bytes 51232 | tf_op jit(solution)/shard_map/ppermute | solution.py:19
  20.9 2.5 %collective-permute-done.1 = f32[40,640]{1,0:T(8,128)S(1)} collective-permute-done((f32[40,640]{1,0:T(8,128)S(1)}, f32[40,640]{1,0:T(8,128)S(1)}, u32[]{:S(2)}, u32[]{:S(2)}) %collective-permute-start.1) | collective-permute-done | bytes 102432 | tf_op jit(solution)/shard_map/ppermute | solution.py:19
  23.4 0.1 fusion.6
  23.5 1.5 %collective-permute-start.6 = (f32[41,640]{1,0:T(8,128)S(1)}, f32[41,640]{1,0:T(8,128)S(1)}, u32[]{:S(2)}, u32[]{:S(2)}) collective-permute-start(f32[41,640]{1,0:T(8,128)S(1)} %get-tuple-element.23), channel_id=1, source_target_pairs={{28,0},{0,4},{4,8},{8,12},{12,16},{16,20},{20,24},{24,28},{29,1},{... | collective-permute-start | bytes 314888 | tf_op jit(solution)/shard_map/ppermute | solution.py:14
  25.1 1.5 %collective-permute-start.4 = (f32[40,960]{1,0:T(8,128)S(1)}, f32[40,960]{1,0:T(8,128)S(1)}, u32[]{:S(2)}, u32[]{:S(2)}) collective-permute-start(f32[40,960]{1,0:T(8,128)S(1)} %pad_maximum_fusion.2), channel_id=1, source_target_pairs={{0,2},{1,3},{2,0},{3,1},{4,6},{5,7},{6,4},{7,5},{8,10},{9,11},{10,... | collective-permute-start | bytes 460808 | tf_op jit(solution)/shard_map/ppermute | solution.py:19
  26.6 3.2 %collective-permute-start.7 = (f32[41,640]{1,0:T(8,128)S(1)}, f32[41,640]{1,0:T(8,128)S(1)}, u32[]{:S(2)}, u32[]{:S(2)}) collective-permute-start(f32[41,640]{1,0:T(8,128)S(1)} %get-tuple-element.24), channel_id=1, source_target_pairs={{4,0},{8,4},{12,8},{16,12},{20,16},{24,20},{28,24},{0,28},{5,1},{9... | collective-permute-start | bytes 314888 | tf_op jit(solution)/shard_map/ppermute | solution.py:14
  29.8 1.4 %collective-permute-done.6 = f32[41,640]{1,0:T(8,128)S(1)} collective-permute-done((f32[41,640]{1,0:T(8,128)S(1)}, f32[41,640]{1,0:T(8,128)S(1)}, u32[]{:S(2)}, u32[]{:S(2)}) %collective-permute-start.6) | collective-permute-done | bytes 104992 | tf_op jit(solution)/shard_map/ppermute | solution.py:14
  31.2 0.0 collective-permute-done.4
  31.3 0.1 collective-permute-start.5
  31.4 2.1 %collective-permute-done.7 = f32[41,640]{1,0:T(8,128)S(1)} collective-permute-done((f32[41,640]{1,0:T(8,128)S(1)}, f32[41,640]{1,0:T(8,128)S(1)}, u32[]{:S(2)}, u32[]{:S(2)}) %collective-permute-start.7) | collective-permute-done | bytes 104992 | tf_op jit(solution)/shard_map/ppermute | solution.py:14
  33.4 0.1 pad_maximum_fusion.6
  33.5 0.1 pad_maximum_fusion.5
  33.6 0.0 collective-permute-done.5
  33.6 0.1 select_bitcast_fusion.1
  33.7 0.1 pad_maximum_fusion
  33.7 0.1 reshape.39
  33.8 0.5 fusion.2
  34.3 0.5 %fusion = f32[160,40]{1,0:T(8,128)S(1)} fusion(f32[160,960]{1,0:T(8,128)S(1)} %bitcast.44, f32[41,640]{1,0:T(8,128)S(1)} %collective-permute-done.7, f32[640]{0:T(1024)S(1)} %get-tuple-element.26), kind=kOutput, calls=%fused_computation.3 | convolution fusion | flops 49177600 | bytes 541696 | tf_op jit(solution)/shard_map/dot_general | solution.py:117
  34.9 0.8 %convolution_bitcast_fusion = f32[1,8,20,40]{3,2,1,0:T(8,128)S(1)} fusion(f32[8,20,960]{2,1,0:T(8,128)S(1)} %reshape.39, f32[960]{0:T(1024)S(1)} %pad_maximum_fusion.6, f32[40,320]{1,0:T(8,128)S(1)} %bitcast_add_fusion.1, f32[40,640]{1,0:T(8,128)S(1)} %bitcast_add_fusion), kind=kOutput, calls=%fused_computation | convolution fusion | flops 73804800 | bytes 797440 | tf_op jit(solution)/shard_map/dot_general | solution.py:117
  35.7 0.2 reshape.43
  35.9 12.0 %all_to_all.5 = f32[8,1,2400]{2,1,0:T(1,128)S(1)} all-to-all(f32[8,1,2400]{2,1,0:T(1,128)S(1)} %reshape.43), channel_id=1, replica_groups=mesh['elem'=8,'cuts'=4] {'elem'}, dimensions={0} | all-to-all | bytes 153600 | tf_op jit(solution)/shard_map/all_to_all | solution.py:165
  48.0 0.5 %broadcast.14 = f32[]{:T(128)} broadcast(f32[]{:T(128)} %constant.105), dimensions={} | broadcast | bytes 8 | tf_op jit(solution)/shard_map/all_to_all | solution.py:165
  48.5 0.8 %reduce.4 = f32[8,2400]{1,0:T(8,128)S(1)} reduce(f32[8,1,2400]{2,1,0:T(1,128)S(1)} %all_to_all.5, f32[]{:T(128)} %broadcast.14), dimensions={1}, to_apply=%all_to_all.3.reduce_sub_computation | reduce | bytes 153604 | tf_op jit(solution)/shard_map/all_to_all | solution.py:165
  49.3 0.1 reshape.44
  49.5 0.7 %copy.21 = f32[8,3,20,40]{3,0,2,1:T(8,128)} copy(f32[8,3,20,40]{3,2,1,0:T(8,128)S(1)} %reshape.44) | data formatting | bytes 153600 | tf_op jit(solution)/shard_map/all_to_all | solution.py:165
  (17 shorter events, 0.3 us)
Async XLA Ops:
  0.0 13.2 %copy-start = (f32[4,16]{1,0:T(4,128)S(1)}, f32[4,16]{1,0:T(4,128)}, u32[]{:S(2)}) copy-start(f32[4,16]{1,0:T(4,128)} %param.11) | copy-start | bytes 772
  0.0 13.2 %copy-start.2 = (s32[1,20]{1,0:T(1,128)S(1)}, s32[1,20]{1,0:T(1,128)}, u32[]{:S(2)}) copy-start(s32[1,20]{1,0:T(1,128)} %param.9) | copy-start | bytes 244
  0.0 13.2 %copy-start.3 = (s32[1,20]{1,0:T(1,128)S(1)}, s32[1,20]{1,0:T(1,128)}, u32[]{:S(2)}) copy-start(s32[1,20]{1,0:T(1,128)} %param.10) | copy-start | bytes 244
  7.5 10.9 %copy-start.1 = (f32[80,640]{1,0:T(8,128)S(1)}, f32[80,640]{1,0:T(8,128)}, u32[]{:S(2)}) copy-start(f32[80,640]{1,0:T(8,128)} %get-tuple-element.14) | copy-start | bytes 614404
  7.5 10.9 %collective-permute-start = (f32[80,640]{1,0:T(8,128)}, f32[80,640]{1,0:T(8,128)S(1)}, u32[]{:S(2)}, u32[]{:S(2)}) collective-permute-start(f32[80,640]{1,0:T(8,128)} %get-tuple-element.15), channel_id=1, source_target_pairs={{0,1},{1,0},{2,3},{3,2},{4,5},{5,4},{6,7},{7,6},{8,9},{9,8},{10,11... | collective-permute-start | bytes 614408 | tf_op jit(solution)/shard_map/ppermute | solution.py:19
  13.1 1.5 %collective-permute-start.2 = (f32[80,320]{1,0:T(8,128)}, f32[80,320]{1,0:T(8,128)S(1)}, u32[]{:S(2)}, u32[]{:S(2)}) collective-permute-start(f32[80,320]{1,0:T(8,128)} %get-tuple-element.18), channel_id=1, source_target_pairs={{0,1},{1,0},{2,3},{3,2},{4,5},{5,4},{6,7},{7,6},{8,9},{9,8},{10,11... | collective-permute-start | bytes 307208 | tf_op jit(solution)/shard_map/ppermute | solution.py:19
  15.6 5.3 %collective-permute-start.3 = (f32[40,320]{1,0:T(8,128)S(1)}, f32[40,320]{1,0:T(8,128)S(1)}, u32[]{:S(2)}, u32[]{:S(2)}) collective-permute-start(f32[40,320]{1,0:T(8,128)S(1)} %dynamic-slice_bitcast_fusion.1), channel_id=1, source_target_pairs={{0,2},{1,3},{2,0},{3,1},{4,6},{5,7},{6,4},{7,5},{8,10},{9,11},{10,... | collective-permute-start | bytes 153608 | tf_op jit(solution)/shard_map/ppermute | solution.py:19
  18.4 4.9 %collective-permute-start.1 = (f32[40,640]{1,0:T(8,128)S(1)}, f32[40,640]{1,0:T(8,128)S(1)}, u32[]{:S(2)}, u32[]{:S(2)}) collective-permute-start(f32[40,640]{1,0:T(8,128)S(1)} %dynamic-slice_bitcast_fusion), channel_id=1, source_target_pairs={{0,2},{1,3},{2,0},{3,1},{4,6},{5,7},{6,4},{7,5},{8,10},{9,11},{10,... | collective-permute-start | bytes 307208 | tf_op jit(solution)/shard_map/ppermute | solution.py:19
  23.5 7.7 %collective-permute-start.6 = (f32[41,640]{1,0:T(8,128)S(1)}, f32[41,640]{1,0:T(8,128)S(1)}, u32[]{:S(2)}, u32[]{:S(2)}) collective-permute-start(f32[41,640]{1,0:T(8,128)S(1)} %get-tuple-element.23), channel_id=1, source_target_pairs={{28,0},{0,4},{4,8},{8,12},{12,16},{16,20},{20,24},{24,28},{29,1},{... | collective-permute-start | bytes 314888 | tf_op jit(solution)/shard_map/ppermute | solution.py:14
  25.1 6.2 %collective-permute-start.4 = (f32[40,960]{1,0:T(8,128)S(1)}, f32[40,960]{1,0:T(8,128)S(1)}, u32[]{:S(2)}, u32[]{:S(2)}) collective-permute-start(f32[40,960]{1,0:T(8,128)S(1)} %pad_maximum_fusion.2), channel_id=1, source_target_pairs={{0,2},{1,3},{2,0},{3,1},{4,6},{5,7},{6,4},{7,5},{8,10},{9,11},{10,... | collective-permute-start | bytes 460808 | tf_op jit(solution)/shard_map/ppermute | solution.py:19
  26.6 6.8 %collective-permute-start.7 = (f32[41,640]{1,0:T(8,128)S(1)}, f32[41,640]{1,0:T(8,128)S(1)}, u32[]{:S(2)}, u32[]{:S(2)}) collective-permute-start(f32[41,640]{1,0:T(8,128)S(1)} %get-tuple-element.24), channel_id=1, source_target_pairs={{4,0},{8,4},{12,8},{16,12},{20,16},{24,20},{28,24},{0,28},{5,1},{9... | collective-permute-start | bytes 314888 | tf_op jit(solution)/shard_map/ppermute | solution.py:14
  31.3 2.3 %collective-permute-start.5 = (f32[2,40,960]{2,1,0:T(8,128)S(1)}, f32[2,40,960]{2,1,0:T(8,128)S(1)}, u32[]{:S(2)}, u32[]{:S(2)}) collective-permute-start(f32[2,40,960]{2,1,0:T(8,128)S(1)} %pad_maximum_fusion.1), channel_id=1, source_target_pairs={{0,1},{1,0},{2,3},{3,2},{4,5},{5,4},{6,7},{7,6},{8,9},{9,8},{10,11... | collective-permute-start | bytes 921608 | tf_op jit(solution)/shard_map/ppermute | solution.py:19

commit v8 on v6

--- a/solution.py
+++ b/solution.py
@@ -24,17 +24,23 @@
     me = lax.axis_index(axis)
     count = size // 2
     quarter = keep.shape[0] // count
-    half = (keep + swapped(send, axis, 1)).reshape(count, quarter, keep.shape[1])
     mine = me // 2
     if count == 2:
         theirs = 1 - mine
-        share = lax.dynamic_index_in_dim(half, mine, 0, keepdims=False) + swapped(
-            lax.dynamic_index_in_dim(half, theirs, 0, keepdims=False), axis, 2
-        )
+        received = swapped(send, axis, 1).reshape(count, quarter, keep.shape[1])
+        kept = keep.reshape(count, quarter, keep.shape[1])
+
+        def summed(index):
+            return lax.dynamic_index_in_dim(kept, index, 0, keepdims=False) + lax.dynamic_index_in_dim(
+                received, index, 0, keepdims=False
+            )
+
+        share = summed(mine) + swapped(summed(theirs), axis, 2)
         other = swapped(share, axis, 2)
         first = jnp.where(mine == 0, share, other)
         second = jnp.where(mine == 0, other, share)
         return jnp.stack([first, second]), share
+    half = (keep + swapped(send, axis, 1)).reshape(count, quarter, keep.shape[1])
     bit = 2
     while bit < size:
         half = half + swapped(half, axis, bit)
@@ -111,7 +117,7 @@
 
 def pair_block(left_t, right_t):
     return lax.dot_general(
-        left_t, right_t, (((1,), (1,)), ((), ())), precision=lax.Precision.HIGHEST
+        left_t, right_t, (((1,), (1,)), ((), ())), precision=lax.Precision.HIGH
     )
 
 

time: 47.5 us -> 47.7 us (level)
  other arithmetic: 2.24 us -> 3.09 us
  matrix products: 1.97 us -> 1.39 us
    add x2, other arithmetic: 1.04 us -> 1.89 us  [the longest x1 0.95 us: summed_rows(): share = summed(mine) + swapped(summed(theirs), axis, 2)]
    dot_general x3, matrix products: 1.76 us -> 1.18 us  [pair_block(): lax.dot_general(left_t, right_t, (((1,), (1,)), ((), ())), precision=lax....]
where the time goes in v8:
time: 47.7 us; the launch traced here: 47.5 us
  blocking collectives  12.3 us (26%)
  starting transfers between devices  10 us (21%)
  Pallas kernels  9.84 us (21%)
  waiting for transfers between devices  8.76 us (18%)
  other arithmetic  3.09 us (6%)
  local copies, waits for them, and re-layouts  2.03 us (4%)
  matrix products  1.39 us (3%)
    all_to_all x1, blocking collectives, local(): lax.all_to_all(pieces, 'elem', split_axis=0, concat_axis=0, tiled=True)  12.3 us
    pallas_call x1, Pallas kernels, partial_coefficients(): pl.pallas_call(functools.partial(coefficient_kernel, quarter), out_shape=...  9.84 us
    ppermute x4, waiting for transfers between devices, swapped(): return lax.ppermute(block, axis, [(i, i ^ bit) for i in devices])  5.56 us
    ppermute x4, starting transfers between devices, swapped(): return lax.ppermute(block, axis, [(i, i ^ bit) for i in devices])  5 us
    ppermute x2, starting transfers between devices, passed_along(): return lax.ppermute(block, axis, route)  5 us
    ppermute x2, waiting for transfers between devices, passed_along(): return lax.ppermute(block, axis, route)  3.2 us
    all_to_all x2, local copies, waits for them, and re-layouts, local(): lax.all_to_all(pieces, 'elem', split_axis=0, concat_axis=0, tiled=True)  1.25 us
    dot_general x3, matrix products, pair_block(): lax.dot_general(left_t, right_t, (((1,), (1,)), ((), ())), precision=lax....  1.18 us
  transfers between devices with their start and end apart: 6, of which 4 were waited for; matrix products, arithmetic and copies ran while one was open for 1% of the time, Pallas kernels for 0%

profile of v8, /device:TPU:0, one launch (start us, length us, event | category | flops | bytes accessed | tf_op | source)
XLA Modules:
  0.0 47.5 jit_solution(8412459657747786484)
XLA Ops:
  0.0 0.0 copy-start
  0.0 0.0 copy-start.2
  0.0 0.0 copy-start.1
  0.0 9.8 %shard_map.64 = (f32[80,960]{1,0:T(8,128)}, f32[80,960]{1,0:T(8,128)}) custom-call(s32[1]{0:T(128)} %bitcast.parity_ref, f32[1,8192]{1,0:T(1,128)} %weight_ref.1, bf16[160,8192]{1,0:T(8,128)(2,1)} %bitcast.38, bf16[960,8192]{1,0:T(8,128)(2,1)} %bitcast.35), custom_call_target="tpu_custom_call" | custom-call | flops 2516582400 | bytes 18997248 | tf_op jit(solution)/shard_map/pallas_call | solution.py:105
  9.8 0.5 collective-permute-start
  10.3 1.5 %collective-permute-done = f32[80,960]{1,0:T(8,128)S(1)} collective-permute-done((f32[80,960]{1,0:T(8,128)}, f32[80,960]{1,0:T(8,128)S(1)}, u32[]{:S(2)}, u32[]{:S(2)}) %collective-permute-start) | collective-permute-done | bytes 307232 | tf_op jit(solution)/shard_map/ppermute | solution.py:19
  11.8 0.9 %add_bitcast_fusion = f32[40,960]{1,0:T(8,128)S(1)} fusion(f32[2,40,960]{2,1,0:T(8,128)S(1)} %bitcast.41, s32[]{:T(128)S(6)} %select_n.49, f32[2,40,960]{2,1,0:T(8,128)} %bitcast.39), kind=kLoop, calls=%fused_computation.18 | loop fusion | flops 38400 | bytes 460804 | tf_op jit(solution)/shard_map/add | solution.py:34
  12.7 3.0 %collective-permute-start.1 = (f32[40,960]{1,0:T(8,128)S(1)}, f32[40,960]{1,0:T(8,128)S(1)}, u32[]{:S(2)}, u32[]{:S(2)}) collective-permute-start(f32[40,960]{1,0:T(8,128)S(1)} %add_bitcast_fusion), channel_id=1, source_target_pairs={{0,2},{1,3},{2,0},{3,1},{4,6},{5,7},{6,4},{7,5},{8,10},{9,11},{10,... | collective-permute-start | bytes 460808 | tf_op jit(solution)/shard_map/ppermute | solution.py:19
  15.7 0.0 copy-done
  15.7 0.0 copy-done.2
  15.7 0.0 copy-done.1
  15.7 0.2 convolution_select_fusion
  15.9 0.1 copy.17
  16.0 0.1 reshape.40
  16.1 4.1 %collective-permute-done.1 = f32[40,960]{1,0:T(8,128)S(1)} collective-permute-done((f32[40,960]{1,0:T(8,128)S(1)}, f32[40,960]{1,0:T(8,128)S(1)}, u32[]{:S(2)}, u32[]{:S(2)}) %collective-permute-start.1) | collective-permute-done | bytes 153632 | tf_op jit(solution)/shard_map/ppermute | solution.py:19
  20.2 0.9 %bitcast_add_fusion = f32[40,960]{1,0:T(8,128)S(1)} fusion(f32[40,960]{1,0:T(8,128)S(1)} %collective-permute-done.1, f32[2,40,960]{2,1,0:T(8,128)S(1)} %bitcast.42, s32[]{:T(128)S(6)} %select_n.48, f32[2,40,960]{2,1,0:T(8,128)} %bitcast.40), kind=kLoop, calls=%fused_computation.14 | loop fusion | flops 76800 | bytes 614404 | tf_op jit(solution)/shard_map/add | solution.py:38
  21.1 0.1 fusion.10
  21.2 1.8 %collective-permute-start.4 = (f32[41,640]{1,0:T(8,128)S(1)}, f32[41,640]{1,0:T(8,128)S(1)}, u32[]{:S(2)}, u32[]{:S(2)}) collective-permute-start(f32[41,640]{1,0:T(8,128)S(1)} %get-tuple-element.15), channel_id=1, source_target_pairs={{28,0},{0,4},{4,8},{8,12},{12,16},{16,20},{20,24},{24,28},{29,1},{... | collective-permute-start | bytes 314888 | tf_op jit(solution)/shard_map/ppermute | solution.py:14
  23.0 1.5 %collective-permute-start.2 = (f32[40,960]{1,0:T(8,128)S(1)}, f32[40,960]{1,0:T(8,128)S(1)}, u32[]{:S(2)}, u32[]{:S(2)}) collective-permute-start(f32[40,960]{1,0:T(8,128)S(1)} %bitcast_add_fusion), channel_id=1, source_target_pairs={{0,2},{1,3},{2,0},{3,1},{4,6},{5,7},{6,4},{7,5},{8,10},{9,11},{10,... | collective-permute-start | bytes 460808 | tf_op jit(solution)/shard_map/ppermute | solution.py:19
  24.5 3.2 %collective-permute-start.5 = (f32[41,640]{1,0:T(8,128)S(1)}, f32[41,640]{1,0:T(8,128)S(1)}, u32[]{:S(2)}, u32[]{:S(2)}) collective-permute-start(f32[41,640]{1,0:T(8,128)S(1)} %get-tuple-element.16), channel_id=1, source_target_pairs={{4,0},{8,4},{12,8},{16,12},{20,16},{24,20},{28,24},{0,28},{5,1},{9... | collective-permute-start | bytes 314888 | tf_op jit(solution)/shard_map/ppermute | solution.py:14
  27.8 1.2 %collective-permute-done.4 = f32[41,640]{1,0:T(8,128)S(1)} collective-permute-done((f32[41,640]{1,0:T(8,128)S(1)}, f32[41,640]{1,0:T(8,128)S(1)}, u32[]{:S(2)}, u32[]{:S(2)}) %collective-permute-start.4) | collective-permute-done | bytes 104992 | tf_op jit(solution)/shard_map/ppermute | solution.py:14
  29.0 0.0 collective-permute-done.2
  29.1 0.1 collective-permute-start.3
  29.1 2.0 %collective-permute-done.5 = f32[41,640]{1,0:T(8,128)S(1)} collective-permute-done((f32[41,640]{1,0:T(8,128)S(1)}, f32[41,640]{1,0:T(8,128)S(1)}, u32[]{:S(2)}, u32[]{:S(2)}) %collective-permute-start.5) | collective-permute-done | bytes 104992 | tf_op jit(solution)/shard_map/ppermute | solution.py:14
  31.2 0.1 pad_maximum_fusion.5
  31.2 0.1 pad_maximum_fusion.4
  31.3 0.0 collective-permute-done.3
  31.3 0.1 select_bitcast_fusion.1
  31.4 0.1 pad_maximum_fusion
  31.4 0.1 reshape.41
  31.5 0.3 fusion.2
  31.9 0.4 fusion
  32.3 0.5 convolution_bitcast_fusion
  32.8 0.2 reshape.45
  33.0 12.3 %all_to_all.5 = f32[8,1,2400]{2,1,0:T(1,128)S(1)} all-to-all(f32[8,1,2400]{2,1,0:T(1,128)S(1)} %reshape.45), channel_id=1, replica_groups=mesh['elem'=8,'cuts'=4] {'elem'}, dimensions={0} | all-to-all | bytes 153600 | tf_op jit(solution)/shard_map/all_to_all | solution.py:159
  45.3 0.5 %broadcast.14 = f32[]{:T(128)} broadcast(f32[]{:T(128)} %constant.84), dimensions={} | broadcast | bytes 8 | tf_op jit(solution)/shard_map/all_to_all | solution.py:159
  45.8 0.8 %reduce.4 = f32[8,2400]{1,0:T(8,128)S(1)} reduce(f32[8,1,2400]{2,1,0:T(1,128)S(1)} %all_to_all.5, f32[]{:T(128)} %broadcast.14), dimensions={1}, to_apply=%all_to_all.3.reduce_sub_computation | reduce | bytes 153604 | tf_op jit(solution)/shard_map/all_to_all | solution.py:159
  46.7 0.1 reshape.46
  46.8 0.7 %copy.21 = f32[8,3,20,40]{3,0,2,1:T(8,128)} copy(f32[8,3,20,40]{3,2,1,0:T(8,128)S(1)} %reshape.46) | data formatting | bytes 153600 | tf_op jit(solution)/shard_map/all_to_all | solution.py:159
  (11 shorter events, 0.2 us)
Async XLA Ops:
  0.0 15.7 %copy-start = (f32[4,16]{1,0:T(4,128)S(1)}, f32[4,16]{1,0:T(4,128)}, u32[]{:S(2)}) copy-start(f32[4,16]{1,0:T(4,128)} %param.11) | copy-start | bytes 772
  0.0 15.7 %copy-start.2 = (s32[1,20]{1,0:T(1,128)S(1)}, s32[1,20]{1,0:T(1,128)}, u32[]{:S(2)}) copy-start(s32[1,20]{1,0:T(1,128)} %param.10) | copy-start | bytes 244
  0.0 15.7 %copy-start.1 = (s32[1,20]{1,0:T(1,128)S(1)}, s32[1,20]{1,0:T(1,128)}, u32[]{:S(2)}) copy-start(s32[1,20]{1,0:T(1,128)} %param.9) | copy-start | bytes 244
  9.8 1.9 %collective-permute-start = (f32[80,960]{1,0:T(8,128)}, f32[80,960]{1,0:T(8,128)S(1)}, u32[]{:S(2)}, u32[]{:S(2)}) collective-permute-start(f32[80,960]{1,0:T(8,128)} %get-tuple-element.8), channel_id=1, source_target_pairs={{0,1},{1,0},{2,3},{3,2},{4,5},{5,4},{6,7},{7,6},{8,9},{9,8},{10,11... | collective-permute-start | bytes 921608 | tf_op jit(solution)/shard_map/ppermute | solution.py:19
  12.7 7.5 %collective-permute-start.1 = (f32[40,960]{1,0:T(8,128)S(1)}, f32[40,960]{1,0:T(8,128)S(1)}, u32[]{:S(2)}, u32[]{:S(2)}) collective-permute-start(f32[40,960]{1,0:T(8,128)S(1)} %add_bitcast_fusion), channel_id=1, source_target_pairs={{0,2},{1,3},{2,0},{3,1},{4,6},{5,7},{6,4},{7,5},{8,10},{9,11},{10,... | collective-permute-start | bytes 460808 | tf_op jit(solution)/shard_map/ppermute | solution.py:19
  21.2 7.7 %collective-permute-start.4 = (f32[41,640]{1,0:T(8,128)S(1)}, f32[41,640]{1,0:T(8,128)S(1)}, u32[]{:S(2)}, u32[]{:S(2)}) collective-permute-start(f32[41,640]{1,0:T(8,128)S(1)} %get-tuple-element.15), channel_id=1, source_target_pairs={{28,0},{0,4},{4,8},{8,12},{12,16},{16,20},{20,24},{24,28},{29,1},{... | collective-permute-start | bytes 314888 | tf_op jit(solution)/shard_map/ppermute | solution.py:14
  23.0 6.0 %collective-permute-start.2 = (f32[40,960]{1,0:T(8,128)S(1)}, f32[40,960]{1,0:T(8,128)S(1)}, u32[]{:S(2)}, u32[]{:S(2)}) collective-permute-start(f32[40,960]{1,0:T(8,128)S(1)} %bitcast_add_fusion), channel_id=1, source_target_pairs={{0,2},{1,3},{2,0},{3,1},{4,6},{5,7},{6,4},{7,5},{8,10},{9,11},{10,... | collective-permute-start | bytes 460808 | tf_op jit(solution)/shard_map/ppermute | solution.py:19
  24.5 6.6 %collective-permute-start.5 = (f32[41,640]{1,0:T(8,128)S(1)}, f32[41,640]{1,0:T(8,128)S(1)}, u32[]{:S(2)}, u32[]{:S(2)}) collective-permute-start(f32[41,640]{1,0:T(8,128)S(1)} %get-tuple-element.16), channel_id=1, source_target_pairs={{4,0},{8,4},{12,8},{16,12},{20,16},{24,20},{28,24},{0,28},{5,1},{9... | collective-permute-start | bytes 314888 | tf_op jit(solution)/shard_map/ppermute | solution.py:14
  29.1 2.3 %collective-permute-start.3 = (f32[2,40,960]{2,1,0:T(8,128)S(1)}, f32[2,40,960]{2,1,0:T(8,128)S(1)}, u32[]{:S(2)}, u32[]{:S(2)}) collective-permute-start(f32[2,40,960]{2,1,0:T(8,128)S(1)} %pad_maximum_fusion.1), channel_id=1, source_target_pairs={{0,1},{1,0},{2,3},{3,2},{4,5},{5,4},{6,7},{7,6},{8,9},{9,8},{10,11... | collective-permute-start | bytes 921608 | tf_op jit(solution)/shard_map/ppermute | solution.py:19

commit v9 on v8

--- a/solution.py
+++ b/solution.py
@@ -156,7 +156,8 @@
     owners = lax.axis_size("elem")
     stacked = jnp.stack([block_left, block_diag, block_right], axis=0)
     pieces = stacked.reshape(3, owners, width // owners, quarter).transpose(1, 0, 2, 3)
-    return lax.all_to_all(pieces, "elem", split_axis=0, concat_axis=0, tiled=True)
+    received = lax.all_to_all(pieces.reshape(owners, -1), "elem", split_axis=0, concat_axis=0, tiled=True)
+    return received.reshape(pieces.shape)
 
 
 def solution(mesh):

time: 47.7 us -> 46.6 us (0.977)
  other arithmetic: 3.09 us -> 2.44 us
  local copies, waits for them, and re-layouts: 2.03 us -> 1.52 us
    all_to_all x2 -> x1, local copies, waits for them, and re-layouts: 1.25 us -> 0.22 us  [local(): lax.all_to_all(pieces.reshape(owners, -1), 'elem', split_axis=0, concat_a...]
    reshape x0 -> x2, local copies, waits for them, and re-layouts: none -> 0.88 us  [local(): return received.reshape(pieces.shape)]
    all_to_all x1, other arithmetic: 0.83 us -> 0.19 us  [local(): lax.all_to_all(pieces.reshape(owners, -1), 'elem', split_axis=0, concat_a...]
where the time goes in v9:
time: 46.6 us; the launch traced here: 46.4 us
  blocking collectives  12.3 us (26%)
  starting transfers between devices  10 us (21%)
  Pallas kernels  9.84 us (21%)
  waiting for transfers between devices  8.76 us (19%)
  other arithmetic  2.44 us (5%)
  local copies, waits for them, and re-layouts  1.52 us (3%)
  matrix products  1.39 us (3%)
    all_to_all x1, blocking collectives, local(): lax.all_to_all(pieces.reshape(owners, -1), 'elem', split_axis=0, concat_a...  12.3 us
    pallas_call x1, Pallas kernels, partial_coefficients(): pl.pallas_call(functools.partial(coefficient_kernel, quarter), out_shape=...  9.84 us
    ppermute x4, waiting for transfers between devices, swapped(): return lax.ppermute(block, axis, [(i, i ^ bit) for i in devices])  5.56 us
    ppermute x4, starting transfers between devices, swapped(): return lax.ppermute(block, axis, [(i, i ^ bit) for i in devices])  5 us
    ppermute x2, starting transfers between devices, passed_along(): return lax.ppermute(block, axis, route)  5 us
    ppermute x2, waiting for transfers between devices, passed_along(): return lax.ppermute(block, axis, route)  3.2 us
    dot_general x3, matrix products, pair_block(): lax.dot_general(left_t, right_t, (((1,), (1,)), ((), ())), precision=lax....  1.18 us
    add x1, other arithmetic, summed_rows(): share = summed(mine) + swapped(summed(theirs), axis, 2)  0.95 us
  transfers between devices with their start and end apart: 6, of which 4 were waited for; matrix products, arithmetic and copies ran while one was open for 1% of the time, Pallas kernels for 0%

profile of v9, /device:TPU:0, one launch (start us, length us, event | category | flops | bytes accessed | tf_op | source)
XLA Modules:
  0.0 46.4 jit_solution(16226323013925211113)
XLA Ops:
  0.0 0.0 copy-start
  0.0 0.0 copy-start.2
  0.0 0.0 copy-start.1
  0.0 9.8 %shard_map.64 = (f32[80,960]{1,0:T(8,128)}, f32[80,960]{1,0:T(8,128)}) custom-call(s32[1]{0:T(128)} %bitcast.parity_ref, f32[1,8192]{1,0:T(1,128)} %weight_ref.1, bf16[160,8192]{1,0:T(8,128)(2,1)} %bitcast.38, bf16[960,8192]{1,0:T(8,128)(2,1)} %bitcast.35), custom_call_target="tpu_custom_call" | custom-call | flops 2516582400 | bytes 18997248 | tf_op jit(solution)/shard_map/pallas_call | solution.py:105
  9.8 0.5 collective-permute-start
  10.3 1.5 %collective-permute-done = f32[80,960]{1,0:T(8,128)S(1)} collective-permute-done((f32[80,960]{1,0:T(8,128)}, f32[80,960]{1,0:T(8,128)S(1)}, u32[]{:S(2)}, u32[]{:S(2)}) %collective-permute-start) | collective-permute-done | bytes 307232 | tf_op jit(solution)/shard_map/ppermute | solution.py:19
  11.8 0.9 %add_bitcast_fusion = f32[40,960]{1,0:T(8,128)S(1)} fusion(f32[2,40,960]{2,1,0:T(8,128)S(1)} %bitcast.41, s32[]{:T(128)S(6)} %select_n.49, f32[2,40,960]{2,1,0:T(8,128)} %bitcast.39), kind=kLoop, calls=%fused_computation.18 | loop fusion | flops 38400 | bytes 460804 | tf_op jit(solution)/shard_map/add | solution.py:34
  12.7 3.0 %collective-permute-start.1 = (f32[40,960]{1,0:T(8,128)S(1)}, f32[40,960]{1,0:T(8,128)S(1)}, u32[]{:S(2)}, u32[]{:S(2)}) collective-permute-start(f32[40,960]{1,0:T(8,128)S(1)} %add_bitcast_fusion), channel_id=1, source_target_pairs={{0,2},{1,3},{2,0},{3,1},{4,6},{5,7},{6,4},{7,5},{8,10},{9,11},{10,... | collective-permute-start | bytes 460808 | tf_op jit(solution)/shard_map/ppermute | solution.py:19
  15.7 0.0 copy-done
  15.7 0.0 copy-done.2
  15.7 0.0 copy-done.1
  15.7 0.2 convolution_select_fusion
  15.9 0.1 copy.17
  16.0 0.1 reshape.48
  16.1 4.1 %collective-permute-done.1 = f32[40,960]{1,0:T(8,128)S(1)} collective-permute-done((f32[40,960]{1,0:T(8,128)S(1)}, f32[40,960]{1,0:T(8,128)S(1)}, u32[]{:S(2)}, u32[]{:S(2)}) %collective-permute-start.1) | collective-permute-done | bytes 153632 | tf_op jit(solution)/shard_map/ppermute | solution.py:19
  20.2 0.9 %bitcast_add_fusion = f32[40,960]{1,0:T(8,128)S(1)} fusion(f32[40,960]{1,0:T(8,128)S(1)} %collective-permute-done.1, f32[2,40,960]{2,1,0:T(8,128)S(1)} %bitcast.42, s32[]{:T(128)S(6)} %select_n.48, f32[2,40,960]{2,1,0:T(8,128)} %bitcast.40), kind=kLoop, calls=%fused_computation.14 | loop fusion | flops 76800 | bytes 614404 | tf_op jit(solution)/shard_map/add | solution.py:38
  21.1 0.1 fusion.10
  21.2 1.8 %collective-permute-start.4 = (f32[41,640]{1,0:T(8,128)S(1)}, f32[41,640]{1,0:T(8,128)S(1)}, u32[]{:S(2)}, u32[]{:S(2)}) collective-permute-start(f32[41,640]{1,0:T(8,128)S(1)} %get-tuple-element.15), channel_id=1, source_target_pairs={{28,0},{0,4},{4,8},{8,12},{12,16},{16,20},{20,24},{24,28},{29,1},{... | collective-permute-start | bytes 314888 | tf_op jit(solution)/shard_map/ppermute | solution.py:14
  23.0 1.5 %collective-permute-start.2 = (f32[40,960]{1,0:T(8,128)S(1)}, f32[40,960]{1,0:T(8,128)S(1)}, u32[]{:S(2)}, u32[]{:S(2)}) collective-permute-start(f32[40,960]{1,0:T(8,128)S(1)} %bitcast_add_fusion), channel_id=1, source_target_pairs={{0,2},{1,3},{2,0},{3,1},{4,6},{5,7},{6,4},{7,5},{8,10},{9,11},{10,... | collective-permute-start | bytes 460808 | tf_op jit(solution)/shard_map/ppermute | solution.py:19
  24.5 3.2 %collective-permute-start.5 = (f32[41,640]{1,0:T(8,128)S(1)}, f32[41,640]{1,0:T(8,128)S(1)}, u32[]{:S(2)}, u32[]{:S(2)}) collective-permute-start(f32[41,640]{1,0:T(8,128)S(1)} %get-tuple-element.16), channel_id=1, source_target_pairs={{4,0},{8,4},{12,8},{16,12},{20,16},{24,20},{28,24},{0,28},{5,1},{9... | collective-permute-start | bytes 314888 | tf_op jit(solution)/shard_map/ppermute | solution.py:14
  27.8 1.2 %collective-permute-done.4 = f32[41,640]{1,0:T(8,128)S(1)} collective-permute-done((f32[41,640]{1,0:T(8,128)S(1)}, f32[41,640]{1,0:T(8,128)S(1)}, u32[]{:S(2)}, u32[]{:S(2)}) %collective-permute-start.4) | collective-permute-done | bytes 104992 | tf_op jit(solution)/shard_map/ppermute | solution.py:14
  29.0 0.0 collective-permute-done.2
  29.1 0.1 collective-permute-start.3
  29.1 2.0 %collective-permute-done.5 = f32[41,640]{1,0:T(8,128)S(1)} collective-permute-done((f32[41,640]{1,0:T(8,128)S(1)}, f32[41,640]{1,0:T(8,128)S(1)}, u32[]{:S(2)}, u32[]{:S(2)}) %collective-permute-start.5) | collective-permute-done | bytes 104992 | tf_op jit(solution)/shard_map/ppermute | solution.py:14
  31.2 0.1 pad_maximum_fusion.5
  31.2 0.1 pad_maximum_fusion.4
  31.3 0.0 collective-permute-done.3
  31.3 0.1 select_bitcast_fusion.1
  31.4 0.1 pad_maximum_fusion
  31.4 0.1 reshape.49
  31.5 0.3 fusion.2
  31.9 0.4 fusion
  32.3 0.5 %convolution_bitcast_fusion = f32[1,8,20,40]{3,2,1,0:T(8,128)S(1)} fusion(f32[8,20,960]{2,1,0:T(8,128)S(1)} %reshape.49, f32[40,960]{1,0:T(8,128)S(1)} %bitcast_add_fusion, f32[960]{0:T(1024)S(1)} %pad_maximum_fusion.5), kind=kOutput, calls=%fused_computation | convolution fusion | flops 36902400 | bytes 797440 | tf_op jit(solution)/shard_map/dot_general | solution.py:119
  32.8 0.2 all_to_all.8
  33.0 12.3 %all_to_all.10 = f32[8,1,2400]{2,1,0:T(1,128)S(1)} all-to-all(f32[8,1,2400]{2,1,0:T(1,128)S(1)} %all_to_all.8), channel_id=1, replica_groups=mesh['elem'=8,'cuts'=4] {'elem'}, dimensions={0} | all-to-all | bytes 153600 | tf_op jit(solution)/shard_map/all_to_all | solution.py:159
  45.3 0.2 reduce.2
  45.5 0.1 reshape.50
  45.6 0.7 %copy.22 = f32[8,3,20,40]{3,0,2,1:T(8,128)} copy(f32[8,3,20,40]{3,2,1,0:T(8,128)S(1)} %reshape.50) | data formatting | bytes 153600 | tf_op jit(solution)/shard_map/reshape | solution.py:160
  (11 shorter events, 0.2 us)
Async XLA Ops:
  0.0 15.7 %copy-start = (f32[4,16]{1,0:T(4,128)S(1)}, f32[4,16]{1,0:T(4,128)}, u32[]{:S(2)}) copy-start(f32[4,16]{1,0:T(4,128)} %param.11) | copy-start | bytes 772
  0.0 15.7 %copy-start.2 = (s32[1,20]{1,0:T(1,128)S(1)}, s32[1,20]{1,0:T(1,128)}, u32[]{:S(2)}) copy-start(s32[1,20]{1,0:T(1,128)} %param.10) | copy-start | bytes 244
  0.0 15.7 %copy-start.1 = (s32[1,20]{1,0:T(1,128)S(1)}, s32[1,20]{1,0:T(1,128)}, u32[]{:S(2)}) copy-start(s32[1,20]{1,0:T(1,128)} %param.9) | copy-start | bytes 244
  9.8 1.9 %collective-permute-start = (f32[80,960]{1,0:T(8,128)}, f32[80,960]{1,0:T(8,128)S(1)}, u32[]{:S(2)}, u32[]{:S(2)}) collective-permute-start(f32[80,960]{1,0:T(8,128)} %get-tuple-element.8), channel_id=1, source_target_pairs={{0,1},{1,0},{2,3},{3,2},{4,5},{5,4},{6,7},{7,6},{8,9},{9,8},{10,11... | collective-permute-start | bytes 921608 | tf_op jit(solution)/shard_map/ppermute | solution.py:19
  12.7 7.5 %collective-permute-start.1 = (f32[40,960]{1,0:T(8,128)S(1)}, f32[40,960]{1,0:T(8,128)S(1)}, u32[]{:S(2)}, u32[]{:S(2)}) collective-permute-start(f32[40,960]{1,0:T(8,128)S(1)} %add_bitcast_fusion), channel_id=1, source_target_pairs={{0,2},{1,3},{2,0},{3,1},{4,6},{5,7},{6,4},{7,5},{8,10},{9,11},{10,... | collective-permute-start | bytes 460808 | tf_op jit(solution)/shard_map/ppermute | solution.py:19
  21.2 7.7 %collective-permute-start.4 = (f32[41,640]{1,0:T(8,128)S(1)}, f32[41,640]{1,0:T(8,128)S(1)}, u32[]{:S(2)}, u32[]{:S(2)}) collective-permute-start(f32[41,640]{1,0:T(8,128)S(1)} %get-tuple-element.15), channel_id=1, source_target_pairs={{28,0},{0,4},{4,8},{8,12},{12,16},{16,20},{20,24},{24,28},{29,1},{... | collective-permute-start | bytes 314888 | tf_op jit(solution)/shard_map/ppermute | solution.py:14
  23.0 6.0 %collective-permute-start.2 = (f32[40,960]{1,0:T(8,128)S(1)}, f32[40,960]{1,0:T(8,128)S(1)}, u32[]{:S(2)}, u32[]{:S(2)}) collective-permute-start(f32[40,960]{1,0:T(8,128)S(1)} %bitcast_add_fusion), channel_id=1, source_target_pairs={{0,2},{1,3},{2,0},{3,1},{4,6},{5,7},{6,4},{7,5},{8,10},{9,11},{10,... | collective-permute-start | bytes 460808 | tf_op jit(solution)/shard_map/ppermute | solution.py:19
  24.5 6.6 %collective-permute-start.5 = (f32[41,640]{1,0:T(8,128)S(1)}, f32[41,640]{1,0:T(8,128)S(1)}, u32[]{:S(2)}, u32[]{:S(2)}) collective-permute-start(f32[41,640]{1,0:T(8,128)S(1)} %get-tuple-element.16), channel_id=1, source_target_pairs={{4,0},{8,4},{12,8},{16,12},{20,16},{24,20},{28,24},{0,28},{5,1},{9... | collective-permute-start | bytes 314888 | tf_op jit(solution)/shard_map/ppermute | solution.py:14
  29.1 2.3 %collective-permute-start.3 = (f32[2,40,960]{2,1,0:T(8,128)S(1)}, f32[2,40,960]{2,1,0:T(8,128)S(1)}, u32[]{:S(2)}, u32[]{:S(2)}) collective-permute-start(f32[2,40,960]{2,1,0:T(8,128)S(1)} %pad_maximum_fusion.1), channel_id=1, source_target_pairs={{0,1},{1,0},{2,3},{3,2},{4,5},{5,4},{6,7},{7,6},{8,9},{9,8},{10,11... | collective-permute-start | bytes 921608 | tf_op jit(solution)/shard_map/ppermute | solution.py:19

commit v10 on v9

--- a/solution.py
+++ b/solution.py
@@ -26,16 +26,9 @@
     quarter = keep.shape[0] // count
     mine = me // 2
     if count == 2:
-        theirs = 1 - mine
         received = swapped(send, axis, 1).reshape(count, quarter, keep.shape[1])
         kept = keep.reshape(count, quarter, keep.shape[1])
-
-        def summed(index):
-            return lax.dynamic_index_in_dim(kept, index, 0, keepdims=False) + lax.dynamic_index_in_dim(
-                received, index, 0, keepdims=False
-            )
-
-        share = summed(mine) + swapped(summed(theirs), axis, 2)
+        share = (kept[0] + received[0]) + swapped(kept[1] + received[1], axis, 2)
         other = swapped(share, axis, 2)
         first = jnp.where(mine == 0, share, other)
         second = jnp.where(mine == 0, other, share)
@@ -76,9 +69,10 @@
     def _():
         count = keep_ref.shape[0] // quarter
         odd = parity_ref[0]
+        first = parity_ref[1]
         for t in range(count):
-            kept = pl.multiple_of((2 * t + odd) * quarter, 8)
-            sent = pl.multiple_of((2 * t + 1 - odd) * quarter, 8)
+            kept = pl.multiple_of((2 * (t ^ first) + odd) * quarter, 8)
+            sent = pl.multiple_of((2 * (t ^ first) + 1 - odd) * quarter, 8)
             keep_ref[t * quarter : (t + 1) * quarter, :] = total_ref[pl.ds(kept, quarter), :]
             send_ref[t * quarter : (t + 1) * quarter, :] = total_ref[pl.ds(sent, quarter), :]
 
@@ -126,7 +120,9 @@
     groups, atoms, slots, points = projectors.shape[1:]
     span = atoms * slots
     quarter = width // lax.axis_size("cuts")
-    parity = (lax.axis_index("cuts") % 2).astype(jnp.int32).reshape(1)
+    cut = lax.axis_index("cuts")
+    first = cut // 2 if lax.axis_size("cuts") == 4 else 0
+    parity = jnp.stack([cut % 2, first]).astype(jnp.int32)
     keep, send = partial_coefficients(
         projectors[0].reshape(groups * span, points), basis[0].T, quad_weight[0], parity, quarter
     )

time: 46.6 us -> 47.9 us (1.028)
  Pallas kernels: 9.84 us -> 10.5 us
  other arithmetic: 2.44 us -> 3 us
    pallas_call x1, Pallas kernels: 9.84 us -> 10.5 us  [partial_coefficients(): pl.pallas_call(functools.partial(coefficient_kernel, quarter), out_shape=...]
    another operation x0 -> x1, other arithmetic: none -> 0.55 us  [local(): parity = jnp.stack([cut % 2, first]).astype(jnp.int32)]
where the time goes in v10:
time: 47.9 us; the launch traced here: 47.7 us
  blocking collectives  12.3 us (26%)
  Pallas kernels  10.5 us (22%)
  starting transfers between devices  10 us (21%)
  waiting for transfers between devices  8.76 us (18%)
  other arithmetic  3 us (6%)
  local copies, waits for them, and re-layouts  1.58 us (3%)
  matrix products  1.38 us (3%)
    all_to_all x1, blocking collectives, local(): lax.all_to_all(pieces.reshape(owners, -1), 'elem', split_axis=0, concat_a...  12.3 us
    pallas_call x1, Pallas kernels, partial_coefficients(): pl.pallas_call(functools.partial(coefficient_kernel, quarter), out_shape=...  10.5 us
    ppermute x4, waiting for transfers between devices, swapped(): return lax.ppermute(block, axis, [(i, i ^ bit) for i in devices])  5.56 us
    ppermute x4, starting transfers between devices, swapped(): return lax.ppermute(block, axis, [(i, i ^ bit) for i in devices])  5.02 us
    ppermute x2, starting transfers between devices, passed_along(): return lax.ppermute(block, axis, route)  5 us
    ppermute x2, waiting for transfers between devices, passed_along(): return lax.ppermute(block, axis, route)  3.2 us
    add x2, other arithmetic, summed_rows(): share = kept[0] + received[0] + swapped(kept[1] + received[1], axis, 2)  1.89 us
    dot_general x3, matrix products, pair_block(): lax.dot_general(left_t, right_t, (((1,), (1,)), ((), ())), precision=lax....  1.17 us
  transfers between devices with their start and end apart: 6, of which 4 were waited for; matrix products, arithmetic and copies ran while one was open for 1% of the time, Pallas kernels for 0%

profile of v10, /device:TPU:0, one launch (start us, length us, event | category | flops | bytes accessed | tf_op | source)
XLA Modules:
  0.0 47.7 jit_solution(13989064232278025604)
XLA Ops:
  0.0 0.0 copy-start
  0.0 0.0 copy-start.2
  0.0 0.0 copy-start.1
  0.0 0.6 %pad_add_fusion.parity_ref = s32[2]{0:T(128)} fusion(s32[1]{0:T(128)} %bitcast.1, s32[1]{0:T(128)} %bitcast), kind=kLoop, calls=%fused_computation.33 | loop fusion | flops 2 | bytes 16 | tf_op jit(solution)/shard_map/stack | solution.py:125
  0.6 10.5 %shard_map.64 = (f32[80,960]{1,0:T(8,128)}, f32[80,960]{1,0:T(8,128)}) custom-call(s32[2]{0:T(128)} %pad_add_fusion.parity_ref, f32[1,8192]{1,0:T(1,128)} %weight_ref.1, bf16[160,8192]{1,0:T(8,128)(2,1)} %bitcast.31, bf16[960,8192]{1,0:T(8,128)(2,1)} %bitcast.28), custom_call_target="tpu_custom_call" | custom-call | flops 2516582400 | bytes 18997248 | tf_op jit(solution)/shard_map/pallas_call | solution.py:99
  11.0 0.5 %collective-permute-start = (f32[80,960]{1,0:T(8,128)}, f32[80,960]{1,0:T(8,128)S(1)}, u32[]{:S(2)}, u32[]{:S(2)}) collective-permute-start(f32[80,960]{1,0:T(8,128)} %get-tuple-element.8), channel_id=1, source_target_pairs={{0,1},{1,0},{2,3},{3,2},{4,5},{5,4},{6,7},{7,6},{8,9},{9,8},{10,11... | collective-permute-start | bytes 921608 | tf_op jit(solution)/shard_map/ppermute | solution.py:19
  11.5 1.5 %collective-permute-done = f32[80,960]{1,0:T(8,128)S(1)} collective-permute-done((f32[80,960]{1,0:T(8,128)}, f32[80,960]{1,0:T(8,128)S(1)}, u32[]{:S(2)}, u32[]{:S(2)}) %collective-permute-start) | collective-permute-done | bytes 307232 | tf_op jit(solution)/shard_map/ppermute | solution.py:19
  13.0 0.9 %slice_add_fusion = f32[40,960]{1,0:T(8,128)S(1)} fusion(f32[80,960]{1,0:T(8,128)S(1)} %collective-permute-done, f32[80,960]{1,0:T(8,128)} %get-tuple-element.7), kind=kLoop, calls=%fused_computation.13 | loop fusion | flops 38400 | bytes 460800 | tf_op jit(solution)/shard_map/add | solution.py:31
  13.9 3.0 %collective-permute-start.1 = (f32[40,960]{1,0:T(8,128)S(1)}, f32[40,960]{1,0:T(8,128)S(1)}, u32[]{:S(2)}, u32[]{:S(2)}) collective-permute-start(f32[40,960]{1,0:T(8,128)S(1)} %slice_add_fusion), channel_id=1, source_target_pairs={{0,2},{1,3},{2,0},{3,1},{4,6},{5,7},{6,4},{7,5},{8,10},{9,11},{10,... | collective-permute-start | bytes 460808 | tf_op jit(solution)/shard_map/ppermute | solution.py:19
  16.9 0.0 copy-done
  16.9 0.0 copy-done.2
  16.9 0.0 copy-done.1
  16.9 0.2 convolution_select_fusion
  17.1 0.1 copy.17
  17.2 0.1 reshape.44
  17.3 4.1 %collective-permute-done.1 = f32[40,960]{1,0:T(8,128)S(1)} collective-permute-done((f32[40,960]{1,0:T(8,128)S(1)}, f32[40,960]{1,0:T(8,128)S(1)}, u32[]{:S(2)}, u32[]{:S(2)}) %collective-permute-start.1) | collective-permute-done | bytes 153632 | tf_op jit(solution)/shard_map/ppermute | solution.py:19
  21.4 1.0 %fusion.4 = f32[40,960]{1,0:T(8,128)S(1)} fusion(f32[40,960]{1,0:T(8,128)S(1)} %collective-permute-done.1, f32[80,960]{1,0:T(8,128)S(1)} %collective-permute-done, f32[80,960]{1,0:T(8,128)} %get-tuple-element.7), kind=kLoop, calls=%fused_computation.15 | loop fusion | flops 76800 | bytes 614400 | tf_op jit(solution)/shard_map/add | solution.py:31
  22.3 0.1 fusion.11
  22.5 1.8 %collective-permute-start.4 = (f32[41,640]{1,0:T(8,128)S(1)}, f32[41,640]{1,0:T(8,128)S(1)}, u32[]{:S(2)}, u32[]{:S(2)}) collective-permute-start(f32[41,640]{1,0:T(8,128)S(1)} %get-tuple-element.15), channel_id=1, source_target_pairs={{28,0},{0,4},{4,8},{8,12},{12,16},{16,20},{20,24},{24,28},{29,1},{... | collective-permute-start | bytes 314888 | tf_op jit(solution)/shard_map/ppermute | solution.py:14
  24.2 1.5 %collective-permute-start.2 = (f32[40,960]{1,0:T(8,128)S(1)}, f32[40,960]{1,0:T(8,128)S(1)}, u32[]{:S(2)}, u32[]{:S(2)}) collective-permute-start(f32[40,960]{1,0:T(8,128)S(1)} %fusion.4), channel_id=1, source_target_pairs={{0,2},{1,3},{2,0},{3,1},{4,6},{5,7},{6,4},{7,5},{8,10},{9,11},{10,... | collective-permute-start | bytes 460808 | tf_op jit(solution)/shard_map/ppermute | solution.py:19
  25.7 3.2 %collective-permute-start.5 = (f32[41,640]{1,0:T(8,128)S(1)}, f32[41,640]{1,0:T(8,128)S(1)}, u32[]{:S(2)}, u32[]{:S(2)}) collective-permute-start(f32[41,640]{1,0:T(8,128)S(1)} %get-tuple-element.16), channel_id=1, source_target_pairs={{4,0},{8,4},{12,8},{16,12},{20,16},{24,20},{28,24},{0,28},{5,1},{9... | collective-permute-start | bytes 314888 | tf_op jit(solution)/shard_map/ppermute | solution.py:14
  29.0 1.2 %collective-permute-done.4 = f32[41,640]{1,0:T(8,128)S(1)} collective-permute-done((f32[41,640]{1,0:T(8,128)S(1)}, f32[41,640]{1,0:T(8,128)S(1)}, u32[]{:S(2)}, u32[]{:S(2)}) %collective-permute-start.4) | collective-permute-done | bytes 104992 | tf_op jit(solution)/shard_map/ppermute | solution.py:14
  30.2 0.0 collective-permute-done.2
  30.3 0.1 collective-permute-start.3
  30.3 2.0 %collective-permute-done.5 = f32[41,640]{1,0:T(8,128)S(1)} collective-permute-done((f32[41,640]{1,0:T(8,128)S(1)}, f32[41,640]{1,0:T(8,128)S(1)}, u32[]{:S(2)}, u32[]{:S(2)}) %collective-permute-start.5) | collective-permute-done | bytes 104992 | tf_op jit(solution)/shard_map/ppermute | solution.py:14
  32.4 0.1 pad_maximum_fusion.5
  32.4 0.1 pad_maximum_fusion.4
  32.5 0.0 collective-permute-done.3
  32.5 0.1 select_bitcast_fusion.1
  32.6 0.1 pad_maximum_fusion
  32.7 0.1 copy.16
  32.7 0.1 reshape.45
  32.8 0.3 fusion.2
  33.1 0.4 fusion
  33.6 0.5 convolution_bitcast_fusion
  34.1 0.2 all_to_all.8
  34.3 12.3 %all_to_all.10 = f32[8,1,2400]{2,1,0:T(1,128)S(1)} all-to-all(f32[8,1,2400]{2,1,0:T(1,128)S(1)} %all_to_all.8), channel_id=1, replica_groups=mesh['elem'=8,'cuts'=4] {'elem'}, dimensions={0} | all-to-all | bytes 153600 | tf_op jit(solution)/shard_map/all_to_all | solution.py:155
  46.6 0.2 reduce.2
  46.8 0.1 reshape.46
  46.9 0.7 %copy.23 = f32[8,3,20,40]{3,0,2,1:T(8,128)} copy(f32[8,3,20,40]{3,2,1,0:T(8,128)S(1)} %reshape.46) | data formatting | bytes 153600 | tf_op jit(solution)/shard_map/reshape | solution.py:156
  (11 shorter events, 0.2 us)
Async XLA Ops:
  0.0 16.9 %copy-start = (f32[4,16]{1,0:T(4,128)S(1)}, f32[4,16]{1,0:T(4,128)}, u32[]{:S(2)}) copy-start(f32[4,16]{1,0:T(4,128)} %param.11) | copy-start | bytes 772
  0.0 16.9 %copy-start.2 = (s32[1,20]{1,0:T(1,128)S(1)}, s32[1,20]{1,0:T(1,128)}, u32[]{:S(2)}) copy-start(s32[1,20]{1,0:T(1,128)} %param.10) | copy-start | bytes 244
  0.0 16.9 %copy-start.1 = (s32[1,20]{1,0:T(1,128)S(1)}, s32[1,20]{1,0:T(1,128)}, u32[]{:S(2)}) copy-start(s32[1,20]{1,0:T(1,128)} %param.9) | copy-start | bytes 244
  11.0 1.9 %collective-permute-start = (f32[80,960]{1,0:T(8,128)}, f32[80,960]{1,0:T(8,128)S(1)}, u32[]{:S(2)}, u32[]{:S(2)}) collective-permute-start(f32[80,960]{1,0:T(8,128)} %get-tuple-element.8), channel_id=1, source_target_pairs={{0,1},{1,0},{2,3},{3,2},{4,5},{5,4},{6,7},{7,6},{8,9},{9,8},{10,11... | collective-permute-start | bytes 921608 | tf_op jit(solution)/shard_map/ppermute | solution.py:19
  13.9 7.5 %collective-permute-start.1 = (f32[40,960]{1,0:T(8,128)S(1)}, f32[40,960]{1,0:T(8,128)S(1)}, u32[]{:S(2)}, u32[]{:S(2)}) collective-permute-start(f32[40,960]{1,0:T(8,128)S(1)} %slice_add_fusion), channel_id=1, source_target_pairs={{0,2},{1,3},{2,0},{3,1},{4,6},{5,7},{6,4},{7,5},{8,10},{9,11},{10,... | collective-permute-start | bytes 460808 | tf_op jit(solution)/shard_map/ppermute | solution.py:19
  22.5 7.7 %collective-permute-start.4 = (f32[41,640]{1,0:T(8,128)S(1)}, f32[41,640]{1,0:T(8,128)S(1)}, u32[]{:S(2)}, u32[]{:S(2)}) collective-permute-start(f32[41,640]{1,0:T(8,128)S(1)} %get-tuple-element.15), channel_id=1, source_target_pairs={{28,0},{0,4},{4,8},{8,12},{12,16},{16,20},{20,24},{24,28},{29,1},{... | collective-permute-start | bytes 314888 | tf_op jit(solution)/shard_map/ppermute | solution.py:14
  24.2 6.0 %collective-permute-start.2 = (f32[40,960]{1,0:T(8,128)S(1)}, f32[40,960]{1,0:T(8,128)S(1)}, u32[]{:S(2)}, u32[]{:S(2)}) collective-permute-start(f32[40,960]{1,0:T(8,128)S(1)} %fusion.4), channel_id=1, source_target_pairs={{0,2},{1,3},{2,0},{3,1},{4,6},{5,7},{6,4},{7,5},{8,10},{9,11},{10,... | collective-permute-start | bytes 460808 | tf_op jit(solution)/shard_map/ppermute | solution.py:19
  25.7 6.6 %collective-permute-start.5 = (f32[41,640]{1,0:T(8,128)S(1)}, f32[41,640]{1,0:T(8,128)S(1)}, u32[]{:S(2)}, u32[]{:S(2)}) collective-permute-start(f32[41,640]{1,0:T(8,128)S(1)} %get-tuple-element.16), channel_id=1, source_target_pairs={{4,0},{8,4},{12,8},{16,12},{20,16},{24,20},{28,24},{0,28},{5,1},{9... | collective-permute-start | bytes 314888 | tf_op jit(solution)/shard_map/ppermute | solution.py:14
  30.3 2.3 %collective-permute-start.3 = (f32[2,40,960]{2,1,0:T(8,128)S(1)}, f32[2,40,960]{2,1,0:T(8,128)S(1)}, u32[]{:S(2)}, u32[]{:S(2)}) collective-permute-start(f32[2,40,960]{2,1,0:T(8,128)S(1)} %pad_maximum_fusion.1), channel_id=1, source_target_pairs={{0,1},{1,0},{2,3},{3,2},{4,5},{5,4},{6,7},{7,6},{8,9},{9,8},{10,11... | collective-permute-start | bytes 921608 | tf_op jit(solution)/shard_map/ppermute | solution.py:19

commit v11 on v9

--- a/solution.py
+++ b/solution.py
@@ -36,10 +36,7 @@
             )
 
         share = summed(mine) + swapped(summed(theirs), axis, 2)
-        other = swapped(share, axis, 2)
-        first = jnp.where(mine == 0, share, other)
-        second = jnp.where(mine == 0, other, share)
-        return jnp.stack([first, second]), share
+        return None, share
     half = (keep + swapped(send, axis, 1)).reshape(count, quarter, keep.shape[1])
     bit = 2
     while bit < size:
@@ -48,7 +45,19 @@
     return half, lax.dynamic_index_in_dim(half, mine, 0, keepdims=False)
 
 
-def gathered_rows(half, axis):
+def gathered_rows(half, share, axis):
+    if half is None:
+        me = lax.axis_index(axis)
+        odd = (me & 1) != 0
+        high = (me // 2) != 0
+        beside = swapped(share, axis, 1)
+        across = swapped(share, axis, 2)
+        relayed = swapped(across, axis, 1)
+        here = jnp.stack([jnp.where(odd, beside, share), jnp.where(odd, share, beside)])
+        there = jnp.stack([jnp.where(odd, relayed, across), jnp.where(odd, across, relayed)])
+        return jnp.where(high, jnp.stack([there, here]), jnp.stack([here, there])).reshape(
+            4 * share.shape[0], share.shape[1]
+        )
     count, quarter, columns = half.shape
     odd = (lax.axis_index(axis) & 1) != 0
     other = swapped(half, axis, 1)
@@ -143,7 +152,7 @@
     to_left = jnp.concatenate([share[:, : 2 * span], energy_row], axis=0)
     from_left = passed_along(to_right, "elem", 1)
     from_right = passed_along(to_left, "elem", -1)
-    full_t = gathered_rows(half, "cuts")
+    full_t = gathered_rows(half, share, "cuts")
 
     left_energy = from_left[quarter, :span]
     right_energy = from_right[quarter, :span]

time: 46.6 us -> 48.6 us (1.043)
  waiting for transfers between devices: 8.76 us -> 10.6 us
    ppermute x4 -> x5, waiting for transfers between devices: 5.56 us -> 6.89 us  [swapped(): return lax.ppermute(block, axis, [(i, i ^ bit) for i in devices])]
    ppermute x2, waiting for transfers between devices: 3.2 us -> 3.7 us  [passed_along(): return lax.ppermute(block, axis, route)]
    ppermute x4 -> x5, starting transfers between devices: 5 us -> 4.95 us  [swapped(): return lax.ppermute(block, axis, [(i, i ^ bit) for i in devices])]
  transfers between devices with their start and end apart: 6 -> 7, of which waited for: 4 -> 5; matrix products, arithmetic and copies ran while one was open for 1% -> 1% of each run, Pallas kernels for 0% -> 0%
where the time goes in v11:
time: 48.6 us; the launch traced here: 48.4 us
  blocking collectives  12.5 us (26%)
  waiting for transfers between devices  10.6 us (22%)
  starting transfers between devices  9.95 us (20%)
  Pallas kernels  9.84 us (20%)
  other arithmetic  2.44 us (5%)
  local copies, waits for them, and re-layouts  1.52 us (3%)
  matrix products  1.39 us (3%)
    all_to_all x1, blocking collectives, local(): lax.all_to_all(pieces.reshape(owners, -1), 'elem', split_axis=0, concat_a...  12.5 us
    pallas_call x1, Pallas kernels, partial_coefficients(): pl.pallas_call(functools.partial(coefficient_kernel, quarter), out_shape=...  9.84 us
    ppermute x5, waiting for transfers between devices, swapped(): return lax.ppermute(block, axis, [(i, i ^ bit) for i in devices])  6.89 us
    ppermute x2, starting transfers between devices, passed_along(): return lax.ppermute(block, axis, route)  5 us
    ppermute x5, starting transfers between devices, swapped(): return lax.ppermute(block, axis, [(i, i ^ bit) for i in devices])  4.95 us
    ppermute x2, waiting for transfers between devices, passed_along(): return lax.ppermute(block, axis, route)  3.7 us
    dot_general x3, matrix products, pair_block(): lax.dot_general(left_t, right_t, (((1,), (1,)), ((), ())), precision=lax....  1.18 us
  transfers between devices with their start and end apart: 7, of which 5 were waited for; matrix products, arithmetic and copies ran while one was open for 1% of the time, Pallas kernels for 0%

profile of v11, /device:TPU:0, one launch (start us, length us, event | category | flops | bytes accessed | tf_op | source)
XLA Modules:
  0.0 48.4 jit_solution(6625023078786288388)
XLA Ops:
  0.0 0.0 copy-start
  0.0 0.0 copy-start.2
  0.0 0.0 copy-start.1
  0.0 9.8 %shard_map.64 = (f32[80,960]{1,0:T(8,128)}, f32[80,960]{1,0:T(8,128)}) custom-call(s32[1]{0:T(128)} %bitcast.parity_ref, f32[1,8192]{1,0:T(1,128)} %weight_ref.1, bf16[160,8192]{1,0:T(8,128)(2,1)} %bitcast.40, bf16[960,8192]{1,0:T(8,128)(2,1)} %bitcast.37), custom_call_target="tpu_custom_call" | custom-call | flops 2516582400 | bytes 18997248 | tf_op jit(solution)/shard_map/pallas_call | solution.py:114
  9.8 0.5 collective-permute-start
  10.3 1.5 %collective-permute-done = f32[80,960]{1,0:T(8,128)S(1)} collective-permute-done((f32[80,960]{1,0:T(8,128)}, f32[80,960]{1,0:T(8,128)S(1)}, u32[]{:S(2)}, u32[]{:S(2)}) %collective-permute-start) | collective-permute-done | bytes 307232 | tf_op jit(solution)/shard_map/ppermute | solution.py:19
  11.8 0.9 %add_bitcast_fusion = f32[40,960]{1,0:T(8,128)S(1)} fusion(f32[2,40,960]{2,1,0:T(8,128)S(1)} %bitcast.43, s32[]{:T(128)S(6)} %select_n.65, f32[2,40,960]{2,1,0:T(8,128)} %bitcast.41), kind=kLoop, calls=%fused_computation.19 | loop fusion | flops 38400 | bytes 460804 | tf_op jit(solution)/shard_map/add | solution.py:34
  12.7 3.0 %collective-permute-start.1 = (f32[40,960]{1,0:T(8,128)S(1)}, f32[40,960]{1,0:T(8,128)S(1)}, u32[]{:S(2)}, u32[]{:S(2)}) collective-permute-start(f32[40,960]{1,0:T(8,128)S(1)} %add_bitcast_fusion), channel_id=1, source_target_pairs={{0,2},{1,3},{2,0},{3,1},{4,6},{5,7},{6,4},{7,5},{8,10},{9,11},{10,... | collective-permute-start | bytes 460808 | tf_op jit(solution)/shard_map/ppermute | solution.py:19
  15.7 0.0 copy-done
  15.7 0.0 copy-done.2
  15.7 0.0 copy-done.1
  15.7 0.2 convolution_select_fusion
  15.9 0.1 copy.14
  16.0 0.1 reshape.56
  16.1 4.1 %collective-permute-done.1 = f32[40,960]{1,0:T(8,128)S(1)} collective-permute-done((f32[40,960]{1,0:T(8,128)S(1)}, f32[40,960]{1,0:T(8,128)S(1)}, u32[]{:S(2)}, u32[]{:S(2)}) %collective-permute-start.1) | collective-permute-done | bytes 153632 | tf_op jit(solution)/shard_map/ppermute | solution.py:19
  20.2 0.9 %bitcast_add_fusion = f32[40,960]{1,0:T(8,128)S(1)} fusion(f32[40,960]{1,0:T(8,128)S(1)} %collective-permute-done.1, f32[2,40,960]{2,1,0:T(8,128)S(1)} %bitcast.44, s32[]{:T(128)S(6)} %select_n.64, f32[2,40,960]{2,1,0:T(8,128)} %bitcast.42), kind=kLoop, calls=%fused_computation.13 | loop fusion | flops 76800 | bytes 614404 | tf_op jit(solution)/shard_map/add | solution.py:38
  21.1 0.1 fusion.10
  21.2 1.8 %collective-permute-start.5 = (f32[41,640]{1,0:T(8,128)S(1)}, f32[41,640]{1,0:T(8,128)S(1)}, u32[]{:S(2)}, u32[]{:S(2)}) collective-permute-start(f32[41,640]{1,0:T(8,128)S(1)} %get-tuple-element.15), channel_id=1, source_target_pairs={{28,0},{0,4},{4,8},{8,12},{12,16},{16,20},{20,24},{24,28},{29,1},{... | collective-permute-start | bytes 314888 | tf_op jit(solution)/shard_map/ppermute | solution.py:14
  23.0 0.0 collective-permute-start.4
  23.0 1.5 %collective-permute-start.2 = (f32[40,960]{1,0:T(8,128)S(1)}, f32[40,960]{1,0:T(8,128)S(1)}, u32[]{:S(2)}, u32[]{:S(2)}) collective-permute-start(f32[40,960]{1,0:T(8,128)S(1)} %bitcast_add_fusion), channel_id=1, source_target_pairs={{0,2},{1,3},{2,0},{3,1},{4,6},{5,7},{6,4},{7,5},{8,10},{9,11},{10,... | collective-permute-start | bytes 460808 | tf_op jit(solution)/shard_map/ppermute | solution.py:19
  24.5 3.2 %collective-permute-start.6 = (f32[41,640]{1,0:T(8,128)S(1)}, f32[41,640]{1,0:T(8,128)S(1)}, u32[]{:S(2)}, u32[]{:S(2)}) collective-permute-start(f32[41,640]{1,0:T(8,128)S(1)} %get-tuple-element.16), channel_id=1, source_target_pairs={{4,0},{8,4},{12,8},{16,12},{20,16},{24,20},{28,24},{0,28},{5,1},{9... | collective-permute-start | bytes 314888 | tf_op jit(solution)/shard_map/ppermute | solution.py:14
  27.8 1.2 %collective-permute-done.5 = f32[41,640]{1,0:T(8,128)S(1)} collective-permute-done((f32[41,640]{1,0:T(8,128)S(1)}, f32[41,640]{1,0:T(8,128)S(1)}, u32[]{:S(2)}, u32[]{:S(2)}) %collective-permute-start.5) | collective-permute-done | bytes 104992 | tf_op jit(solution)/shard_map/ppermute | solution.py:14
  29.0 2.5 %collective-permute-done.6 = f32[41,640]{1,0:T(8,128)S(1)} collective-permute-done((f32[41,640]{1,0:T(8,128)S(1)}, f32[41,640]{1,0:T(8,128)S(1)}, u32[]{:S(2)}, u32[]{:S(2)}) %collective-permute-start.6) | collective-permute-done | bytes 104992 | tf_op jit(solution)/shard_map/ppermute | solution.py:14
  31.5 0.1 pad_maximum_fusion.3
  31.6 0.1 pad_maximum_fusion.2
  31.7 0.0 collective-permute-done.2
  31.7 0.0 collective-permute-start.3
  31.7 0.0 collective-permute-done.4
  31.7 1.3 %collective-permute-done.3 = f32[40,960]{1,0:T(8,128)S(1)} collective-permute-done((f32[40,960]{1,0:T(8,128)S(1)}, f32[40,960]{1,0:T(8,128)S(1)}, u32[]{:S(2)}, u32[]{:S(2)}) %collective-permute-start.3) | collective-permute-done | bytes 153632 | tf_op jit(solution)/shard_map/ppermute | solution.py:19
  33.1 0.1 maximum_bitcast_fusion
  33.2 0.1 maximum_select_fusion
  33.2 0.1 select_n.72
  33.3 0.3 fusion.2
  33.6 0.4 fusion
  34.1 0.5 convolution_bitcast_fusion
  34.6 0.2 all_to_all.8
  34.8 12.5 %all_to_all.10 = f32[8,1,2400]{2,1,0:T(1,128)S(1)} all-to-all(f32[8,1,2400]{2,1,0:T(1,128)S(1)} %all_to_all.8), channel_id=1, replica_groups=mesh['elem'=8,'cuts'=4] {'elem'}, dimensions={0} | all-to-all | bytes 153600 | tf_op jit(solution)/shard_map/all_to_all | solution.py:168
  47.3 0.2 reduce.2
  47.5 0.1 reshape.57
  47.6 0.7 %copy.19 = f32[8,3,20,40]{3,0,2,1:T(8,128)} copy(f32[8,3,20,40]{3,2,1,0:T(8,128)S(1)} %reshape.57) | data formatting | bytes 153600 | tf_op jit(solution)/shard_map/reshape | solution.py:169
  (11 shorter events, 0.2 us)
Async XLA Ops:
  0.0 15.7 %copy-start = (f32[4,16]{1,0:T(4,128)S(1)}, f32[4,16]{1,0:T(4,128)}, u32[]{:S(2)}) copy-start(f32[4,16]{1,0:T(4,128)} %param.11) | copy-start | bytes 772
  0.0 15.7 %copy-start.2 = (s32[1,20]{1,0:T(1,128)S(1)}, s32[1,20]{1,0:T(1,128)}, u32[]{:S(2)}) copy-start(s32[1,20]{1,0:T(1,128)} %param.10) | copy-start | bytes 244
  0.0 15.7 %copy-start.1 = (s32[1,20]{1,0:T(1,128)S(1)}, s32[1,20]{1,0:T(1,128)}, u32[]{:S(2)}) copy-start(s32[1,20]{1,0:T(1,128)} %param.9) | copy-start | bytes 244
  9.8 1.9 %collective-permute-start = (f32[80,960]{1,0:T(8,128)}, f32[80,960]{1,0:T(8,128)S(1)}, u32[]{:S(2)}, u32[]{:S(2)}) collective-permute-start(f32[80,960]{1,0:T(8,128)} %get-tuple-element.8), channel_id=1, source_target_pairs={{0,1},{1,0},{2,3},{3,2},{4,5},{5,4},{6,7},{7,6},{8,9},{9,8},{10,11... | collective-permute-start | bytes 921608 | tf_op jit(solution)/shard_map/ppermute | solution.py:19
  12.7 7.5 %collective-permute-start.1 = (f32[40,960]{1,0:T(8,128)S(1)}, f32[40,960]{1,0:T(8,128)S(1)}, u32[]{:S(2)}, u32[]{:S(2)}) collective-permute-start(f32[40,960]{1,0:T(8,128)S(1)} %add_bitcast_fusion), channel_id=1, source_target_pairs={{0,2},{1,3},{2,0},{3,1},{4,6},{5,7},{6,4},{7,5},{8,10},{9,11},{10,... | collective-permute-start | bytes 460808 | tf_op jit(solution)/shard_map/ppermute | solution.py:19
  21.2 7.7 %collective-permute-start.5 = (f32[41,640]{1,0:T(8,128)S(1)}, f32[41,640]{1,0:T(8,128)S(1)}, u32[]{:S(2)}, u32[]{:S(2)}) collective-permute-start(f32[41,640]{1,0:T(8,128)S(1)} %get-tuple-element.15), channel_id=1, source_target_pairs={{28,0},{0,4},{4,8},{8,12},{12,16},{16,20},{20,24},{24,28},{29,1},{... | collective-permute-start | bytes 314888 | tf_op jit(solution)/shard_map/ppermute | solution.py:14
  23.0 8.7 %collective-permute-start.4 = (f32[40,960]{1,0:T(8,128)S(1)}, f32[40,960]{1,0:T(8,128)S(1)}, u32[]{:S(2)}, u32[]{:S(2)}) collective-permute-start(f32[40,960]{1,0:T(8,128)S(1)} %bitcast_add_fusion), channel_id=1, source_target_pairs={{0,1},{1,0},{2,3},{3,2},{4,5},{5,4},{6,7},{7,6},{8,9},{9,8},{10,11... | collective-permute-start | bytes 460808 | tf_op jit(solution)/shard_map/ppermute | solution.py:19
  23.0 8.6 %collective-permute-start.2 = (f32[40,960]{1,0:T(8,128)S(1)}, f32[40,960]{1,0:T(8,128)S(1)}, u32[]{:S(2)}, u32[]{:S(2)}) collective-permute-start(f32[40,960]{1,0:T(8,128)S(1)} %bitcast_add_fusion), channel_id=1, source_target_pairs={{0,2},{1,3},{2,0},{3,1},{4,6},{5,7},{6,4},{7,5},{8,10},{9,11},{10,... | collective-permute-start | bytes 460808 | tf_op jit(solution)/shard_map/ppermute | solution.py:19
  24.5 7.0 %collective-permute-start.6 = (f32[41,640]{1,0:T(8,128)S(1)}, f32[41,640]{1,0:T(8,128)S(1)}, u32[]{:S(2)}, u32[]{:S(2)}) collective-permute-start(f32[41,640]{1,0:T(8,128)S(1)} %get-tuple-element.16), channel_id=1, source_target_pairs={{4,0},{8,4},{12,8},{16,12},{20,16},{24,20},{28,24},{0,28},{5,1},{9... | collective-permute-start | bytes 314888 | tf_op jit(solution)/shard_map/ppermute | solution.py:14
  31.7 1.4 %collective-permute-start.3 = (f32[40,960]{1,0:T(8,128)S(1)}, f32[40,960]{1,0:T(8,128)S(1)}, u32[]{:S(2)}, u32[]{:S(2)}) collective-permute-start(f32[40,960]{1,0:T(8,128)S(1)} %collective-permute-done.2), channel_id=1, source_target_pairs={{0,1},{1,0},{2,3},{3,2},{4,5},{5,4},{6,7},{7,6},{8,9},{9,8},{10,11... | collective-permute-start | bytes 460808 | tf_op jit(solution)/shard_map/ppermute | solution.py:19

commit v12 on v9

--- a/solution.py
+++ b/solution.py
@@ -150,12 +150,18 @@
     weight_left = jnp.concatenate([left_energy, energy])
     weight_diag = jnp.concatenate([left_energy, energy, right_energy])
     weight_right = jnp.concatenate([energy, right_energy])
-    block_left = pair_block(full_t[:, : 2 * span], from_left[:quarter] * weight_left[None])
-    block_diag = pair_block(full_t, share * weight_diag[None])
-    block_right = pair_block(full_t[:, span:], from_right[:quarter] * weight_right[None])
+    gap = jnp.zeros((quarter, span), jnp.float32)
+    right_t = jnp.concatenate(
+        [
+            jnp.concatenate([from_left[:quarter] * weight_left[None], gap], axis=1),
+            share * weight_diag[None],
+            jnp.concatenate([gap, from_right[:quarter] * weight_right[None]], axis=1),
+        ],
+        axis=0,
+    )
     owners = lax.axis_size("elem")
-    stacked = jnp.stack([block_left, block_diag, block_right], axis=0)
-    pieces = stacked.reshape(3, owners, width // owners, quarter).transpose(1, 0, 2, 3)
+    stacked = pair_block(full_t, right_t).reshape(owners, width // owners, 3, quarter)
+    pieces = stacked.transpose(0, 2, 1, 3)
     received = lax.all_to_all(pieces.reshape(owners, -1), "elem", split_axis=0, concat_axis=0, tiled=True)
     return received.reshape(pieces.shape)
 

time: 46.6 us -> 48.9 us (1.049)
  waiting for transfers between devices: 8.76 us -> 14.6 us
  blocking collectives: 12.3 us -> 9.37 us
    ppermute x2, waiting for transfers between devices: 3.2 us -> 7.55 us  [passed_along(): return lax.ppermute(block, axis, route)]
    all_to_all x1, blocking collectives: 12.3 us -> 9.37 us  [local(): lax.all_to_all(pieces.reshape(owners, -1), 'elem', split_axis=0, concat_a...]
    ppermute x4, waiting for transfers between devices: 5.56 us -> 7.04 us  [swapped(): return lax.ppermute(block, axis, [(i, i ^ bit) for i in devices])]
    dot_general x3 -> x1, matrix products: 1.18 us -> 0.77 us  [pair_block(): lax.dot_general(left_t, right_t, (((1,), (1,)), ((), ())), precision=lax....]
  transfers between devices with their start and end apart: 6 -> 6, of which waited for: 4 -> 5; matrix products, arithmetic and copies ran while one was open for 1% -> 1% of each run, Pallas kernels for 0% -> 0%
where the time goes in v12:
time: 48.9 us; the launch traced here: 48.7 us
  waiting for transfers between devices  14.6 us (30%)
  Pallas kernels  9.83 us (20%)
  starting transfers between devices  9.8 us (20%)
  blocking collectives  9.37 us (19%)
  other arithmetic  2.55 us (5%)
  local copies, waits for them, and re-layouts  1.48 us (3%)
  matrix products  0.97 us (2%)
    pallas_call x1, Pallas kernels, partial_coefficients(): pl.pallas_call(functools.partial(coefficient_kernel, quarter), out_shape=...  9.83 us
    all_to_all x1, blocking collectives, local(): lax.all_to_all(pieces.reshape(owners, -1), 'elem', split_axis=0, concat_a...  9.37 us
    ppermute x2, waiting for transfers between devices, passed_along(): return lax.ppermute(block, axis, route)  7.55 us
    ppermute x4, waiting for transfers between devices, swapped(): return lax.ppermute(block, axis, [(i, i ^ bit) for i in devices])  7.04 us
    ppermute x4, starting transfers between devices, swapped(): return lax.ppermute(block, axis, [(i, i ^ bit) for i in devices])  5 us
    ppermute x2, starting transfers between devices, passed_along(): return lax.ppermute(block, axis, route)  4.8 us
  transfers between devices with their start and end apart: 6, of which 5 were waited for; matrix products, arithmetic and copies ran while one was open for 1% of the time, Pallas kernels for 0%

profile of v12, /device:TPU:0, one launch (start us, length us, event | category | flops | bytes accessed | tf_op | source)
XLA Modules:
  0.0 48.7 jit_solution(2583556122438555386)
XLA Ops:
  0.0 0.0 copy-start
  0.0 0.0 copy-start.2
  0.0 0.0 copy-start.1
  0.0 9.8 %shard_map.64 = (f32[80,960]{1,0:T(8,128)}, f32[80,960]{1,0:T(8,128)}) custom-call(s32[1]{0:T(128)} %bitcast.parity_ref, f32[1,8192]{1,0:T(1,128)} %weight_ref.1, bf16[160,8192]{1,0:T(8,128)(2,1)} %bitcast.36, bf16[960,8192]{1,0:T(8,128)(2,1)} %bitcast.35), custom_call_target="tpu_custom_call" | custom-call | flops 2516582400 | bytes 18997248 | tf_op jit(solution)/shard_map/pallas_call | solution.py:105
  9.8 0.5 collective-permute-start
  10.3 1.5 %collective-permute-done = f32[80,960]{1,0:T(8,128)S(1)} collective-permute-done((f32[80,960]{1,0:T(8,128)}, f32[80,960]{1,0:T(8,128)S(1)}, u32[]{:S(2)}, u32[]{:S(2)}) %collective-permute-start) | collective-permute-done | bytes 307232 | tf_op jit(solution)/shard_map/ppermute | solution.py:19
  11.8 0.9 %add_bitcast_fusion = f32[40,960]{1,0:T(8,128)S(1)} fusion(f32[2,40,960]{2,1,0:T(8,128)S(1)} %bitcast.40, s32[]{:T(128)S(6)} %select_n.49, f32[2,40,960]{2,1,0:T(8,128)} %bitcast.38), kind=kLoop, calls=%fused_computation.16 | loop fusion | flops 38400 | bytes 460804 | tf_op jit(solution)/shard_map/add | solution.py:34
  12.7 3.0 %collective-permute-start.1 = (f32[40,960]{1,0:T(8,128)S(1)}, f32[40,960]{1,0:T(8,128)S(1)}, u32[]{:S(2)}, u32[]{:S(2)}) collective-permute-start(f32[40,960]{1,0:T(8,128)S(1)} %add_bitcast_fusion), channel_id=1, source_target_pairs={{0,2},{1,3},{2,0},{3,1},{4,6},{5,7},{6,4},{7,5},{8,10},{9,11},{10,... | collective-permute-start | bytes 460808 | tf_op jit(solution)/shard_map/ppermute | solution.py:19
  15.7 0.0 copy-done
  15.7 0.0 copy-done.2
  15.7 0.0 copy-done.1
  15.7 0.2 convolution_select_fusion
  15.9 0.1 copy.12
  16.0 0.1 reshape.35
  16.1 4.1 %collective-permute-done.1 = f32[40,960]{1,0:T(8,128)S(1)} collective-permute-done((f32[40,960]{1,0:T(8,128)S(1)}, f32[40,960]{1,0:T(8,128)S(1)}, u32[]{:S(2)}, u32[]{:S(2)}) %collective-permute-start.1) | collective-permute-done | bytes 153632 | tf_op jit(solution)/shard_map/ppermute | solution.py:19
  20.2 0.9 %bitcast_add_fusion = f32[40,960]{1,0:T(8,128)S(1)} fusion(f32[40,960]{1,0:T(8,128)S(1)} %collective-permute-done.1, f32[2,40,960]{2,1,0:T(8,128)S(1)} %bitcast.41, s32[]{:T(128)S(6)} %select_n.48, f32[2,40,960]{2,1,0:T(8,128)} %bitcast.39), kind=kLoop, calls=%fused_computation.13 | loop fusion | flops 76800 | bytes 614404 | tf_op jit(solution)/shard_map/add | solution.py:38
  21.1 0.1 fusion.2
  21.2 4.8 %collective-permute-start.5 = (f32[41,640]{1,0:T(8,128)S(1)}, f32[41,640]{1,0:T(8,128)S(1)}, u32[]{:S(2)}, u32[]{:S(2)}) collective-permute-start(f32[41,640]{1,0:T(8,128)S(1)} %get-tuple-element.17), channel_id=1, source_target_pairs={{4,0},{8,4},{12,8},{16,12},{20,16},{24,20},{28,24},{0,28},{5,1},{9... | collective-permute-start | bytes 314888 | tf_op jit(solution)/shard_map/ppermute | solution.py:14
  26.0 1.5 %collective-permute-start.2 = (f32[40,960]{1,0:T(8,128)S(1)}, f32[40,960]{1,0:T(8,128)S(1)}, u32[]{:S(2)}, u32[]{:S(2)}) collective-permute-start(f32[40,960]{1,0:T(8,128)S(1)} %bitcast_add_fusion), channel_id=1, source_target_pairs={{0,2},{1,3},{2,0},{3,1},{4,6},{5,7},{6,4},{7,5},{8,10},{9,11},{10,... | collective-permute-start | bytes 460808 | tf_op jit(solution)/shard_map/ppermute | solution.py:19
  27.6 0.0 collective-permute-start.4
  27.6 0.9 %collective-permute-done.5 = f32[41,640]{1,0:T(8,128)S(1)} collective-permute-done((f32[41,640]{1,0:T(8,128)S(1)}, f32[41,640]{1,0:T(8,128)S(1)}, u32[]{:S(2)}, u32[]{:S(2)}) %collective-permute-start.5) | collective-permute-done | bytes 104992 | tf_op jit(solution)/shard_map/ppermute | solution.py:14
  28.5 6.6 %collective-permute-done.4 = f32[41,640]{1,0:T(8,128)S(1)} collective-permute-done((f32[41,640]{1,0:T(8,128)S(1)}, f32[41,640]{1,0:T(8,128)S(1)}, u32[]{:S(2)}, u32[]{:S(2)}) %collective-permute-start.4) | collective-permute-done | bytes 104992 | tf_op jit(solution)/shard_map/ppermute | solution.py:14
  35.2 0.1 pad_maximum_fusion.5
  35.2 0.1 pad_maximum_fusion.4
  35.3 0.0 collective-permute-done.2
  35.4 0.1 collective-permute-start.3
  35.5 0.1 select_maximum_fusion
  35.6 1.5 %collective-permute-done.3 = f32[2,40,960]{2,1,0:T(8,128)S(1)} collective-permute-done((f32[2,40,960]{2,1,0:T(8,128)S(1)}, f32[2,40,960]{2,1,0:T(8,128)S(1)}, u32[]{:S(2)}, u32[]{:S(2)}) %collective-permute-start.3) | collective-permute-done | bytes 307232 | tf_op jit(solution)/shard_map/ppermute | solution.py:19
  37.1 0.1 select_bitcast_fusion.1
  37.2 0.1 pad_maximum_fusion
  37.2 0.1 reshape.37
  37.3 0.8 %convolution_bitcast_fusion = f32[8,3,20,40]{3,2,1,0:T(8,128)S(1)} fusion(f32[3,40,960,1]{2,1,0,3:T(8,128)S(1)} %bitcast.37, f32[8,20,960,1]{2,1,0,3:T(8,128)S(1)} %reshape.37), kind=kOutput, calls=%fused_computation | convolution fusion | flops 110592000 | bytes 1152000 | tf_op jit(solution)/shard_map/dot_general | solution.py:119
  38.1 0.2 all_to_all.8
  38.3 9.4 %all_to_all.10 = f32[8,1,2400]{2,1,0:T(1,128)S(1)} all-to-all(f32[8,1,2400]{2,1,0:T(1,128)S(1)} %all_to_all.8), channel_id=1, replica_groups=mesh['elem'=8,'cuts'=4] {'elem'}, dimensions={0} | all-to-all | bytes 153600 | tf_op jit(solution)/shard_map/all_to_all | solution.py:165
  47.7 0.2 reduce.2
  47.9 0.1 reshape.36
  48.0 0.7 %copy.14 = f32[8,3,20,40]{3,0,2,1:T(8,128)} copy(f32[8,3,20,40]{3,2,1,0:T(8,128)S(1)} %reshape.36) | data formatting | bytes 153600 | tf_op jit(solution)/shard_map/reshape | solution.py:166
  (8 shorter events, 0.2 us)
Async XLA Ops:
  0.0 15.7 %copy-start = (f32[4,16]{1,0:T(4,128)S(1)}, f32[4,16]{1,0:T(4,128)}, u32[]{:S(2)}) copy-start(f32[4,16]{1,0:T(4,128)} %param.11) | copy-start | bytes 772
  0.0 15.7 %copy-start.2 = (s32[1,20]{1,0:T(1,128)S(1)}, s32[1,20]{1,0:T(1,128)}, u32[]{:S(2)}) copy-start(s32[1,20]{1,0:T(1,128)} %param.10) | copy-start | bytes 244
  0.0 15.7 %copy-start.1 = (s32[1,20]{1,0:T(1,128)S(1)}, s32[1,20]{1,0:T(1,128)}, u32[]{:S(2)}) copy-start(s32[1,20]{1,0:T(1,128)} %param.9) | copy-start | bytes 244
  9.8 1.9 %collective-permute-start = (f32[80,960]{1,0:T(8,128)}, f32[80,960]{1,0:T(8,128)S(1)}, u32[]{:S(2)}, u32[]{:S(2)}) collective-permute-start(f32[80,960]{1,0:T(8,128)} %get-tuple-element.8), channel_id=1, source_target_pairs={{0,1},{1,0},{2,3},{3,2},{4,5},{5,4},{6,7},{7,6},{8,9},{9,8},{10,11... | collective-permute-start | bytes 921608 | tf_op jit(solution)/shard_map/ppermute | solution.py:19
  12.7 7.5 %collective-permute-start.1 = (f32[40,960]{1,0:T(8,128)S(1)}, f32[40,960]{1,0:T(8,128)S(1)}, u32[]{:S(2)}, u32[]{:S(2)}) collective-permute-start(f32[40,960]{1,0:T(8,128)S(1)} %add_bitcast_fusion), channel_id=1, source_target_pairs={{0,2},{1,3},{2,0},{3,1},{4,6},{5,7},{6,4},{7,5},{8,10},{9,11},{10,... | collective-permute-start | bytes 460808 | tf_op jit(solution)/shard_map/ppermute | solution.py:19
  21.2 7.2 %collective-permute-start.5 = (f32[41,640]{1,0:T(8,128)S(1)}, f32[41,640]{1,0:T(8,128)S(1)}, u32[]{:S(2)}, u32[]{:S(2)}) collective-permute-start(f32[41,640]{1,0:T(8,128)S(1)} %get-tuple-element.17), channel_id=1, source_target_pairs={{4,0},{8,4},{12,8},{16,12},{20,16},{24,20},{28,24},{0,28},{5,1},{9... | collective-permute-start | bytes 314888 | tf_op jit(solution)/shard_map/ppermute | solution.py:14
  26.0 9.3 %collective-permute-start.2 = (f32[40,960]{1,0:T(8,128)S(1)}, f32[40,960]{1,0:T(8,128)S(1)}, u32[]{:S(2)}, u32[]{:S(2)}) collective-permute-start(f32[40,960]{1,0:T(8,128)S(1)} %bitcast_add_fusion), channel_id=1, source_target_pairs={{0,2},{1,3},{2,0},{3,1},{4,6},{5,7},{6,4},{7,5},{8,10},{9,11},{10,... | collective-permute-start | bytes 460808 | tf_op jit(solution)/shard_map/ppermute | solution.py:19
  27.6 7.6 %collective-permute-start.4 = (f32[41,640]{1,0:T(8,128)S(1)}, f32[41,640]{1,0:T(8,128)S(1)}, u32[]{:S(2)}, u32[]{:S(2)}) collective-permute-start(f32[41,640]{1,0:T(8,128)S(1)} %get-tuple-element.16), channel_id=1, source_target_pairs={{28,0},{0,4},{4,8},{8,12},{12,16},{16,20},{20,24},{24,28},{29,1},{... | collective-permute-start | bytes 314888 | tf_op jit(solution)/shard_map/ppermute | solution.py:14
  35.4 1.7 %collective-permute-start.3 = (f32[2,40,960]{2,1,0:T(8,128)S(1)}, f32[2,40,960]{2,1,0:T(8,128)S(1)}, u32[]{:S(2)}, u32[]{:S(2)}) collective-permute-start(f32[2,40,960]{2,1,0:T(8,128)S(1)} %pad_maximum_fusion.1), channel_id=1, source_target_pairs={{0,1},{1,0},{2,3},{3,2},{4,5},{5,4},{6,7},{7,6},{8,9},{9,8},{10,11... | collective-permute-start | bytes 921608 | tf_op jit(solution)/shard_map/ppermute | solution.py:19

commit v13 on v10

v13 whole, which is shorter than its diff:
```python
import functools

import jax
import jax.numpy as jnp
from jax import lax
from jax.experimental import pallas as pl
from jax.experimental.pallas import tpu as pltpu
from jax.sharding import PartitionSpec as P


def passed_along(block, axis, distance):
    devices = range(lax.axis_size(axis))
    route = [((i - distance) % len(devices), i) for i in devices]
    return lax.ppermute(block, axis, route)


def swapped(block, axis, bit):
    devices = range(lax.axis_size(axis))
    return lax.ppermute(block, axis, [(i, i ^ bit) for i in devices])


def summed_rows(pieces, axis):
    share = pieces[0]
    for distance in range(1, pieces.shape[0]):
        share = share + swapped(pieces[distance], axis, distance)
    return share


def gathered_rows(share, axis):
    quarter, columns = share.shape
    size = lax.axis_size(axis)
    me = lax.axis_index(axis)
    held = share[None]
    bit = size // 2
    while bit >= 1:
        other = swapped(held, axis, bit)
        mine = (me & bit) != 0
        low = jnp.where(mine, other, held)
        high = jnp.where(mine, held, other)
        held = jnp.stack([low, high], axis=1).reshape(held.shape[0] * 2, quarter, columns)
        bit //= 2
    return held.reshape(size * quarter, columns)


def coefficient_kernel(quarter, cut_ref, weight_ref, basis_ref, projector_ref, pieces_ref, total_ref):
    step = pl.program_id(0)
    scaled = (basis_ref[...].astype(jnp.float32) * weight_ref[...]).astype(jnp.bfloat16)
    product = lax.dot_general(
        scaled, projector_ref[...], (((1,), (1,)), ((), ())), preferred_element_type=jnp.float32
    )

    @pl.when(step == 0)
    def _():
        total_ref[...] = product

    @pl.when(step > 0)
    def _():
        total_ref[...] += product

    @pl.when(step == pl.num_programs(0) - 1)
    def _():
        me = cut_ref[0]
        for distance in range(pieces_ref.shape[0]):
            start = pl.multiple_of((me ^ distance) * quarter, 8)
            pieces_ref[distance] = total_ref[pl.ds(start, quarter), :]


def partial_coefficients(flat_projectors, basis_t, weight, cut, quarter):
    rows, points = flat_projectors.shape
    width = basis_t.shape[0]
    depth = min(points, 4096)
    size = width // quarter
    grid_spec = pltpu.PrefetchScalarGridSpec(
        num_scalar_prefetch=1,
        grid=(points // depth,),
        in_specs=[
            pl.BlockSpec((1, depth), lambda k, p: (0, k)),
            pl.BlockSpec((width, depth), lambda k, p: (0, k)),
            pl.BlockSpec((rows, depth), lambda k, p: (0, k)),
        ],
        out_specs=pl.BlockSpec((size, quarter, rows), lambda k, p: (0, 0, 0)),
        scratch_shapes=[pltpu.VMEM((width, rows), jnp.float32)],
    )
    return pl.pallas_call(
        functools.partial(coefficient_kernel, quarter),
        out_shape=jax.ShapeDtypeStruct((size, quarter, rows), jnp.float32),
        grid_spec=grid_spec,
        compiler_params=pltpu.CompilerParams(dimension_semantics=("arbitrary",)),
        cost_estimate=pl.CostEstimate(
            flops=2 * rows * points * width,
            bytes_accessed=2 * rows * points + 2 * points * width + 4 * points + 4 * rows * width,
            transcendentals=0,
        ),
    )(cut, weight.reshape(1, points), basis_t, flat_projectors)


def pair_block(left_t, right_t):
    return lax.dot_general(
        left_t, right_t, (((1,), (1,)), ((), ())), precision=lax.Precision.HIGH
    )


def local(basis, quad_weight, projectors, species, counts, gamma_table):
    width = basis.shape[2]
    groups, atoms, slots, points = projectors.shape[1:]
    span = atoms * slots
    quarter = width // lax.axis_size("cuts")
    cut = lax.axis_index("cuts").astype(jnp.int32).reshape(1)
    pieces = partial_coefficients(
        projectors[0].reshape(groups * span, points), basis[0].T, quad_weight[0], cut, quarter
    )
    onehot = (
        species[0][:, None] == jnp.arange(gamma_table.shape[0], dtype=jnp.int32)[None, :]
    ).astype(jnp.float32)
    table = jnp.dot(onehot, gamma_table, precision=lax.Precision.HIGHEST)
    active = (jnp.arange(slots, dtype=jnp.int32)[None, :] < counts[0][:, None]).astype(jnp.float32)
    energy = (table * active).reshape(span)

    share = summed_rows(pieces, "cuts")
    energy_row = jnp.pad(energy, (0, span))[None]
    to_right = jnp.concatenate([share[:, span:], energy_row], axis=0)
    to_left = jnp.concatenate([share[:, : 2 * span], energy_row], axis=0)
    from_left = passed_along(to_right, "elem", 1)
    from_right = passed_along(to_left, "elem", -1)
    full_t = gathered_rows(share, "cuts")

    left_energy = from_left[quarter, :span]
    right_energy = from_right[quarter, :span]
    weight_left = jnp.concatenate([left_energy, energy])
    weight_diag = jnp.concatenate([left_energy, energy, right_energy])
    weight_right = jnp.concatenate([energy, right_energy])
    block_left = pair_block(full_t[:, : 2 * span], from_left[:quarter] * weight_left[None])
    block_diag = pair_block(full_t, share * weight_diag[None])
    block_right = pair_block(full_t[:, span:], from_right[:quarter] * weight_right[None])
    owners = lax.axis_size("elem")
    stacked = jnp.stack([block_left, block_diag, block_right], axis=0)
    pieces = stacked.reshape(3, owners, width // owners, quarter).transpose(1, 0, 2, 3)
    received = lax.all_to_all(pieces.reshape(owners, -1), "elem", split_axis=0, concat_axis=0, tiled=True)
    return received.reshape(pieces.shape)


def solution(mesh):
    in_specs = (
        P("elem", "cuts", None),
        P("elem", "cuts"),
        P("elem", None, None, None, "cuts"),
        P("elem", None),
        P("elem", None),
        P(),
    )
    out_specs = P(None, None, "elem", "cuts")
    return jax.shard_map(local, mesh=mesh, in_specs=in_specs, out_specs=out_specs, check_vma=False)
```

time: 47.9 us -> 48.8 us (1.019)
  waiting for transfers between devices: 8.76 us -> 11.2 us
  other arithmetic: 3 us -> 1.52 us
  local copies, waits for them, and re-layouts: 1.58 us -> 2.68 us
  Pallas kernels: 10.5 us -> 9.83 us
    ppermute x4 -> x5, waiting for transfers between devices: 5.56 us -> 7.8 us  [swapped(): return lax.ppermute(block, axis, [(i, i ^ bit) for i in devices])]
    squeeze x0 -> x1, local copies, waits for them, and re-layouts: none -> 1.1 us  [summed_rows(): share = share + swapped(pieces[distance], axis, distance)]
    add x2 -> x1, other arithmetic: 1.89 us -> 0.96 us  [summed_rows(): share = share + swapped(pieces[distance], axis, distance)]
    pallas_call x1, Pallas kernels: 10.5 us -> 9.83 us  [partial_coefficients(): pl.pallas_call(functools.partial(coefficient_kernel, quarter), out_shape=...]
    another operation x5 -> x3, other arithmetic: 0.72 us -> 0.14 us  [gathered_rows(): jnp.stack([low, high], axis=1).reshape(held.shape[0] * 2, quarter, columns)]
    ppermute x4 -> x5, starting transfers between devices: 5.02 us -> 4.8 us  [swapped(): return lax.ppermute(block, axis, [(i, i ^ bit) for i in devices])]
  transfers between devices with their start and end apart: 6 -> 7, of which waited for: 4 -> 4; matrix products, arithmetic and copies ran while one was open for 1% -> 1% of each run, Pallas kernels for 0% -> 0%
where the time goes in v13:
time: 48.8 us; the launch traced here: 48.6 us
  blocking collectives  12 us (25%)
  waiting for transfers between devices  11.2 us (23%)
  Pallas kernels  9.83 us (20%)
  starting transfers between devices  9.76 us (20%)
  local copies, waits for them, and re-layouts  2.68 us (5%)
  other arithmetic  1.52 us (3%)
  matrix products  1.39 us (3%)
    all_to_all x1, blocking collectives, local(): lax.all_to_all(pieces.reshape(owners, -1), 'elem', split_axis=0, concat_a...  12 us
    pallas_call x1, Pallas kernels, partial_coefficients(): pl.pallas_call(functools.partial(coefficient_kernel, quarter), out_shape=...  9.83 us
    ppermute x5, waiting for transfers between devices, swapped(): return lax.ppermute(block, axis, [(i, i ^ bit) for i in devices])  7.8 us
    ppermute x2, starting transfers between devices, passed_along(): return lax.ppermute(block, axis, route)  4.96 us
    ppermute x5, starting transfers between devices, swapped(): return lax.ppermute(block, axis, [(i, i ^ bit) for i in devices])  4.8 us
    ppermute x2, waiting for transfers between devices, passed_along(): return lax.ppermute(block, axis, route)  3.43 us
    dot_general x3, matrix products, pair_block(): lax.dot_general(left_t, right_t, (((1,), (1,)), ((), ())), precision=lax....  1.18 us
    squeeze x1, local copies, waits for them, and re-layouts, summed_rows(): share = share + swapped(pieces[distance], axis, distance)  1.1 us
  transfers between devices with their start and end apart: 7, of which 4 were waited for; matrix products, arithmetic and copies ran while one was open for 1% of the time, Pallas kernels for 0%

profile of v13, /device:TPU:0, one launch (start us, length us, event | category | flops | bytes accessed | tf_op | source)
XLA Modules:
  0.0 48.6 jit_solution(10413884443211081740)
XLA Ops:
  0.0 0.0 copy-start
  0.0 0.0 copy-start.2
  0.0 0.0 copy-start.1
  0.0 9.8 %shard_map.64 = f32[4,40,960]{2,1,0:T(8,128)} custom-call(s32[1]{0:T(128)} %bitcast.cut_ref, f32[1,8192]{1,0:T(1,128)} %weight_ref.1, bf16[160,8192]{1,0:T(8,128)(2,1)} %bitcast.54, bf16[960,8192]{1,0:T(8,128)(2,1)} %bitcast.50), custom_call_target="tpu_custom_call" | custom-call | flops 2516582400 | bytes 18997248 | tf_op jit(solution)/shard_map/pallas_call | solution.py:84
  9.8 1.1 %slice_bitcast_fusion.2 = (f32[40,960]{1,0:T(8,128)S(1)}, f32[40,960]{1,0:T(8,128)S(1)}, f32[40,960]{1,0:T(8,128)S(1)}) fusion(f32[4,40,960]{2,1,0:T(8,128)} %shard_map.64), kind=kLoop, calls=%fused_computation.15 | loop fusion | bytes 921600 | tf_op jit(solution)/shard_map/squeeze | solution.py:25
  10.9 0.5 %collective-permute-start = (f32[40,960]{1,0:T(8,128)S(1)}, f32[40,960]{1,0:T(8,128)S(1)}, u32[]{:S(2)}, u32[]{:S(2)}) collective-permute-start(f32[40,960]{1,0:T(8,128)S(1)} %get-tuple-element.7), channel_id=1, source_target_pairs={{0,1},{1,0},{2,3},{3,2},{4,5},{5,4},{6,7},{7,6},{8,9},{9,8},{10,11... | collective-permute-start | bytes 460808 | tf_op jit(solution)/shard_map/ppermute | solution.py:19
  11.5 2.6 %collective-permute-start.2 = (f32[40,960]{1,0:T(8,128)S(1)}, f32[40,960]{1,0:T(8,128)S(1)}, u32[]{:S(2)}, u32[]{:S(2)}) collective-permute-start(f32[40,960]{1,0:T(8,128)S(1)} %get-tuple-element.8), channel_id=1, source_target_pairs={{0,3},{1,2},{2,1},{3,0},{4,7},{5,6},{6,5},{7,4},{8,11},{9,10},{10,... | collective-permute-start | bytes 460808 | tf_op jit(solution)/shard_map/ppermute | solution.py:19
  14.1 0.0 collective-permute-start.1
  14.2 0.0 copy-done
  14.2 0.0 copy-done.2
  14.2 0.0 copy-done.1
  14.2 0.2 convolution_select_fusion
  14.4 0.1 copy.17
  14.5 0.1 reshape.38
  14.6 0.0 collective-permute-done
  14.6 4.1 %collective-permute-done.2 = f32[40,960]{1,0:T(8,128)S(1)} collective-permute-done((f32[40,960]{1,0:T(8,128)S(1)}, f32[40,960]{1,0:T(8,128)S(1)}, u32[]{:S(2)}, u32[]{:S(2)}) %collective-permute-start.2) | collective-permute-done | bytes 153632 | tf_op jit(solution)/shard_map/ppermute | solution.py:19
  18.6 3.7 %collective-permute-done.1 = f32[40,960]{1,0:T(8,128)S(1)} collective-permute-done((f32[40,960]{1,0:T(8,128)S(1)}, f32[40,960]{1,0:T(8,128)S(1)}, u32[]{:S(2)}, u32[]{:S(2)}) %collective-permute-start.1) | collective-permute-done | bytes 153632 | tf_op jit(solution)/shard_map/ppermute | solution.py:19
  22.4 1.0 %fusion.6 = f32[40,960]{1,0:T(8,128)S(1)} fusion(f32[40,960]{1,0:T(8,128)S(1)} %collective-permute-done.2, f32[40,960]{1,0:T(8,128)S(1)} %collective-permute-done.1, f32[40,960]{1,0:T(8,128)S(1)} %collective-permute-done, f32[4,40,960]{2,1,0:T(8,128)} %shard_map.64), kind=kLoop, calls=%fused_computation.19 | loop fusion | flops 115200 | bytes 768000 | tf_op jit(solution)/shard_map/add | solution.py:25
  23.3 0.1 fusion.13
  23.5 1.7 %collective-permute-start.5 = (f32[41,640]{1,0:T(8,128)S(1)}, f32[41,640]{1,0:T(8,128)S(1)}, u32[]{:S(2)}, u32[]{:S(2)}) collective-permute-start(f32[41,640]{1,0:T(8,128)S(1)} %get-tuple-element.14), channel_id=1, source_target_pairs={{28,0},{0,4},{4,8},{8,12},{12,16},{16,20},{20,24},{24,28},{29,1},{... | collective-permute-start | bytes 314888 | tf_op jit(solution)/shard_map/ppermute | solution.py:14
  25.2 1.5 %collective-permute-start.3 = (f32[1,40,960]{2,1,0:T(8,128)S(1)}, f32[1,40,960]{2,1,0:T(8,128)S(1)}, u32[]{:S(2)}, u32[]{:S(2)}) collective-permute-start(f32[1,40,960]{2,1,0:T(8,128)S(1)} %bitcast.53), channel_id=1, source_target_pairs={{0,2},{1,3},{2,0},{3,1},{4,6},{5,7},{6,4},{7,5},{8,10},{9,11},{10,... | collective-permute-start | bytes 460808 | tf_op jit(solution)/shard_map/ppermute | solution.py:19
  26.7 3.2 %collective-permute-start.6 = (f32[41,640]{1,0:T(8,128)S(1)}, f32[41,640]{1,0:T(8,128)S(1)}, u32[]{:S(2)}, u32[]{:S(2)}) collective-permute-start(f32[41,640]{1,0:T(8,128)S(1)} %get-tuple-element.15), channel_id=1, source_target_pairs={{4,0},{8,4},{12,8},{16,12},{20,16},{24,20},{28,24},{0,28},{5,1},{9... | collective-permute-start | bytes 314888 | tf_op jit(solution)/shard_map/ppermute | solution.py:14
  29.9 1.4 %collective-permute-done.5 = f32[41,640]{1,0:T(8,128)S(1)} collective-permute-done((f32[41,640]{1,0:T(8,128)S(1)}, f32[41,640]{1,0:T(8,128)S(1)}, u32[]{:S(2)}, u32[]{:S(2)}) %collective-permute-start.5) | collective-permute-done | bytes 104992 | tf_op jit(solution)/shard_map/ppermute | solution.py:14
  31.4 0.0 collective-permute-done.3
  31.5 0.1 collective-permute-start.4
  31.6 2.0 %collective-permute-done.6 = f32[41,640]{1,0:T(8,128)S(1)} collective-permute-done((f32[41,640]{1,0:T(8,128)S(1)}, f32[41,640]{1,0:T(8,128)S(1)}, u32[]{:S(2)}, u32[]{:S(2)}) %collective-permute-start.6) | collective-permute-done | bytes 104992 | tf_op jit(solution)/shard_map/ppermute | solution.py:14
  33.6 0.1 pad_maximum_fusion.4
  33.6 0.1 pad_maximum_fusion.3
  33.7 0.0 collective-permute-done.4
  33.7 0.1 select_bitcast_fusion.1
  33.8 0.1 pad_maximum_fusion
  33.9 0.1 copy.16
  33.9 0.1 reshape.39
  34.0 0.3 fusion.2
  34.3 0.4 fusion
  34.8 0.5 convolution_bitcast_fusion
  35.3 0.2 all_to_all.8
  35.5 12.0 %all_to_all.10 = f32[8,1,2400]{2,1,0:T(1,128)S(1)} all-to-all(f32[8,1,2400]{2,1,0:T(1,128)S(1)} %all_to_all.8), channel_id=1, replica_groups=mesh['elem'=8,'cuts'=4] {'elem'}, dimensions={0} | all-to-all | bytes 153600 | tf_op jit(solution)/shard_map/all_to_all | solution.py:138
  47.6 0.2 reduce.2
  47.7 0.1 reshape.40
  47.9 0.7 %copy.23 = f32[8,3,20,40]{3,0,2,1:T(8,128)} copy(f32[8,3,20,40]{3,2,1,0:T(8,128)S(1)} %reshape.40) | data formatting | bytes 153600 | tf_op jit(solution)/shard_map/reshape | solution.py:139
  (11 shorter events, 0.2 us)
Async XLA Ops:
  0.0 14.2 %copy-start = (f32[4,16]{1,0:T(4,128)S(1)}, f32[4,16]{1,0:T(4,128)}, u32[]{:S(2)}) copy-start(f32[4,16]{1,0:T(4,128)} %param.11) | copy-start | bytes 772
  0.0 14.2 %copy-start.2 = (s32[1,20]{1,0:T(1,128)S(1)}, s32[1,20]{1,0:T(1,128)}, u32[]{:S(2)}) copy-start(s32[1,20]{1,0:T(1,128)} %param.10) | copy-start | bytes 244
  0.0 14.2 %copy-start.1 = (s32[1,20]{1,0:T(1,128)S(1)}, s32[1,20]{1,0:T(1,128)}, u32[]{:S(2)}) copy-start(s32[1,20]{1,0:T(1,128)} %param.9) | copy-start | bytes 244
  10.9 3.6 %collective-permute-start = (f32[40,960]{1,0:T(8,128)S(1)}, f32[40,960]{1,0:T(8,128)S(1)}, u32[]{:S(2)}, u32[]{:S(2)}) collective-permute-start(f32[40,960]{1,0:T(8,128)S(1)} %get-tuple-element.7), channel_id=1, source_target_pairs={{0,1},{1,0},{2,3},{3,2},{4,5},{5,4},{6,7},{7,6},{8,9},{9,8},{10,11... | collective-permute-start | bytes 460808 | tf_op jit(solution)/shard_map/ppermute | solution.py:19
  11.5 7.2 %collective-permute-start.2 = (f32[40,960]{1,0:T(8,128)S(1)}, f32[40,960]{1,0:T(8,128)S(1)}, u32[]{:S(2)}, u32[]{:S(2)}) collective-permute-start(f32[40,960]{1,0:T(8,128)S(1)} %get-tuple-element.8), channel_id=1, source_target_pairs={{0,3},{1,2},{2,1},{3,0},{4,7},{5,6},{6,5},{7,4},{8,11},{9,10},{10,... | collective-permute-start | bytes 460808 | tf_op jit(solution)/shard_map/ppermute | solution.py:19
  14.1 8.3 %collective-permute-start.1 = (f32[40,960]{1,0:T(8,128)S(1)}, f32[40,960]{1,0:T(8,128)S(1)}, u32[]{:S(2)}, u32[]{:S(2)}) collective-permute-start(f32[40,960]{1,0:T(8,128)S(1)} %get-tuple-element.9), channel_id=1, source_target_pairs={{0,2},{1,3},{2,0},{3,1},{4,6},{5,7},{6,4},{7,5},{8,10},{9,11},{10,... | collective-permute-start | bytes 460808 | tf_op jit(solution)/shard_map/ppermute | solution.py:19
  23.5 7.9 %collective-permute-start.5 = (f32[41,640]{1,0:T(8,128)S(1)}, f32[41,640]{1,0:T(8,128)S(1)}, u32[]{:S(2)}, u32[]{:S(2)}) collective-permute-start(f32[41,640]{1,0:T(8,128)S(1)} %get-tuple-element.14), channel_id=1, source_target_pairs={{28,0},{0,4},{4,8},{8,12},{12,16},{16,20},{20,24},{24,28},{29,1},{... | collective-permute-start | bytes 314888 | tf_op jit(solution)/shard_map/ppermute | solution.py:14
  25.2 6.2 %collective-permute-start.3 = (f32[1,40,960]{2,1,0:T(8,128)S(1)}, f32[1,40,960]{2,1,0:T(8,128)S(1)}, u32[]{:S(2)}, u32[]{:S(2)}) collective-permute-start(f32[1,40,960]{2,1,0:T(8,128)S(1)} %bitcast.53), channel_id=1, source_target_pairs={{0,2},{1,3},{2,0},{3,1},{4,6},{5,7},{6,4},{7,5},{8,10},{9,11},{10,... | collective-permute-start | bytes 460808 | tf_op jit(solution)/shard_map/ppermute | solution.py:19
  26.7 6.8 %collective-permute-start.6 = (f32[41,640]{1,0:T(8,128)S(1)}, f32[41,640]{1,0:T(8,128)S(1)}, u32[]{:S(2)}, u32[]{:S(2)}) collective-permute-start(f32[41,640]{1,0:T(8,128)S(1)} %get-tuple-element.15), channel_id=1, source_target_pairs={{4,0},{8,4},{12,8},{16,12},{20,16},{24,20},{28,24},{0,28},{5,1},{9... | collective-permute-start | bytes 314888 | tf_op jit(solution)/shard_map/ppermute | solution.py:14
  31.5 2.2 %collective-permute-start.4 = (f32[2,40,960]{2,1,0:T(8,128)S(1)}, f32[2,40,960]{2,1,0:T(8,128)S(1)}, u32[]{:S(2)}, u32[]{:S(2)}) collective-permute-start(f32[2,40,960]{2,1,0:T(8,128)S(1)} %maximum_bitcast_fusion), channel_id=1, source_target_pairs={{0,1},{1,0},{2,3},{3,2},{4,5},{5,4},{6,7},{7,6},{8,9},{9,8},{10,11... | collective-permute-start | bytes 921608 | tf_op jit(solution)/shard_map/ppermute | solution.py:19

commit v14 on v9

--- a/solution.py
+++ b/solution.py
@@ -57,53 +57,81 @@
     return jnp.stack([low, high], axis=1).reshape(count * 2 * quarter, columns)
 
 
-def coefficient_kernel(quarter, parity_ref, weight_ref, basis_ref, projector_ref, keep_ref, send_ref, total_ref):
-    step = pl.program_id(0)
-    scaled = (basis_ref[...].astype(jnp.float32) * weight_ref[...]).astype(jnp.bfloat16)
-    product = lax.dot_general(
-        scaled, projector_ref[...], (((1,), (1,)), ((), ())), preferred_element_type=jnp.float32
-    )
-
-    @pl.when(step == 0)
-    def _():
-        total_ref[...] = product
-
-    @pl.when(step > 0)
-    def _():
-        total_ref[...] += product
-
-    @pl.when(step == pl.num_programs(0) - 1)
-    def _():
-        count = keep_ref.shape[0] // quarter
-        odd = parity_ref[0]
-        for t in range(count):
-            kept = pl.multiple_of((2 * t + odd) * quarter, 8)
-            sent = pl.multiple_of((2 * t + 1 - odd) * quarter, 8)
-            keep_ref[t * quarter : (t + 1) * quarter, :] = total_ref[pl.ds(kept, quarter), :]
-            send_ref[t * quarter : (t + 1) * quarter, :] = total_ref[pl.ds(sent, quarter), :]
+def coefficient_kernel(
+    quarter, chunk, parity_ref, weight_ref, basis_hbm, projector_hbm, keep_ref, send_ref,
+    basis_buf, projector_buf, copies, total_ref,
+):
+    points = projector_hbm.shape[1]
+    chunks = points // chunk
+    slots = basis_buf.shape[0]
+
+    def fetch(index):
+        slot = index % slots
+        window = pl.ds(index * chunk, chunk)
+        return (
+            pltpu.make_async_copy(basis_hbm.at[:, window], basis_buf.at[slot], copies.at[0, slot]),
+            pltpu.make_async_copy(projector_hbm.at[:, window], projector_buf.at[slot], copies.at[1, slot]),
+        )
+
+    pending = {}
+    for index in range(min(slots, chunks)):
+        pending[index] = fetch(index)
+        for copy in pending[index]:
+            copy.start()
+    for index in range(chunks):
+        slot = index % slots
+        for copy in pending.pop(index):
+            copy.wait()
+        weight = weight_ref[:, index * chunk : (index + 1) * chunk]
+        scaled = (basis_buf[slot].astype(jnp.float32) * weight).astype(jnp.bfloat16)
+        product = lax.dot_general(
+            scaled, projector_buf[slot], (((1,), (1,)), ((), ())), preferred_element_type=jnp.float32
+        )
+        if index == 0:
+            total_ref[...] = product
+        else:
+            total_ref[...] += product
+        if index + slots < chunks:
+            pending[index + slots] = fetch(index + slots)
+            for copy in pending[index + slots]:
+                copy.start()
+
+    count = keep_ref.shape[0] // quarter
+    odd = parity_ref[0]
+    for t in range(count):
+        kept = pl.multiple_of((2 * t + odd) * quarter, 8)
+        sent = pl.multiple_of((2 * t + 1 - odd) * quarter, 8)
+        keep_ref[t * quarter : (t + 1) * quarter, :] = total_ref[pl.ds(kept, quarter), :]
+        send_ref[t * quarter : (t + 1) * quarter, :] = total_ref[pl.ds(sent, quarter), :]
 
 
 def partial_coefficients(flat_projectors, basis_t, weight, parity, quarter):
     rows, points = flat_projectors.shape
     width = basis_t.shape[0]
-    depth = min(points, 4096)
+    chunk = min(points, 1024)
+    slots = 3
     half = jax.ShapeDtypeStruct((width // 2, rows), jnp.float32)
     grid_spec = pltpu.PrefetchScalarGridSpec(
         num_scalar_prefetch=1,
-        grid=(points // depth,),
+        grid=(1,),
         in_specs=[
-            pl.BlockSpec((1, depth), lambda k, p: (0, k)),
-            pl.BlockSpec((width, depth), lambda k, p: (0, k)),
-            pl.BlockSpec((rows, depth), lambda k, p: (0, k)),
+            pl.BlockSpec((1, points), lambda k, p: (0, 0)),
+            pl.BlockSpec(memory_space=pl.ANY),
+            pl.BlockSpec(memory_space=pl.ANY),
         ],
         out_specs=[
             pl.BlockSpec((width // 2, rows), lambda k, p: (0, 0)),
             pl.BlockSpec((width // 2, rows), lambda k, p: (0, 0)),
         ],
-        scratch_shapes=[pltpu.VMEM((width, rows), jnp.float32)],
+        scratch_shapes=[
+            pltpu.VMEM((slots, width, chunk), basis_t.dtype),
+            pltpu.VMEM((slots, rows, chunk), flat_projectors.dtype),
+            pltpu.SemaphoreType.DMA((2, slots)),
+            pltpu.VMEM((width, rows), jnp.float32),
+        ],
     )
     return pl.pallas_call(
-        functools.partial(coefficient_kernel, quarter),
+        functools.partial(coefficient_kernel, quarter, chunk),
         out_shape=(half, half),
         grid_spec=grid_spec,
         compiler_params=pltpu.CompilerParams(dimension_semantics=("arbitrary",)),

time: 46.6 us -> 46.6 us (level)
  no operation moved by 1% of the time
where the time goes in v14:
time: 46.6 us; the launch traced here: 46.3 us
  blocking collectives  12.3 us (26%)
  starting transfers between devices  10.1 us (22%)
  Pallas kernels  9.71 us (21%)
  waiting for transfers between devices  8.77 us (19%)
  other arithmetic  2.44 us (5%)
  local copies, waits for them, and re-layouts  1.52 us (3%)
  matrix products  1.38 us (3%)
    all_to_all x1, blocking collectives, local(): lax.all_to_all(pieces.reshape(owners, -1), 'elem', split_axis=0, concat_a...  12.3 us
    pallas_call x1, Pallas kernels, partial_coefficients(): pl.pallas_call(functools.partial(coefficient_kernel, quarter, chunk), out...  9.71 us
    ppermute x4, waiting for transfers between devices, swapped(): return lax.ppermute(block, axis, [(i, i ^ bit) for i in devices])  5.56 us
    ppermute x4, starting transfers between devices, swapped(): return lax.ppermute(block, axis, [(i, i ^ bit) for i in devices])  5.06 us
    ppermute x2, starting transfers between devices, passed_along(): return lax.ppermute(block, axis, route)  5 us
    ppermute x2, waiting for transfers between devices, passed_along(): return lax.ppermute(block, axis, route)  3.21 us
    dot_general x3, matrix products, pair_block(): lax.dot_general(left_t, right_t, (((1,), (1,)), ((), ())), precision=lax....  1.18 us
    add x1, other arithmetic, summed_rows(): share = summed(mine) + swapped(summed(theirs), axis, 2)  0.95 us
  transfers between devices with their start and end apart: 6, of which 4 were waited for; matrix products, arithmetic and copies ran while one was open for 1% of the time, Pallas kernels for 0%

profile of v14, /device:TPU:0, one launch (start us, length us, event | category | flops | bytes accessed | tf_op | source)
XLA Modules:
  0.0 46.3 jit_solution(12760940085637020429)
XLA Ops:
  0.0 0.0 copy-start
  0.0 0.0 copy-start.2
  0.0 0.0 copy-start.1
  0.0 9.7 %shard_map.64 = (f32[80,960]{1,0:T(8,128)}, f32[80,960]{1,0:T(8,128)}) custom-call(s32[1]{0:T(128)} %bitcast.parity_ref, f32[1,8192]{1,0:T(1,128)} %weight_ref.1, bf16[160,8192]{1,0:T(8,128)(2,1)} %bitcast.38, bf16[960,8192]{1,0:T(8,128)(2,1)} %bitcast.35), custom_call_target="tpu_custom_call" | custom-call | flops 2516582400 | bytes 18997248 | tf_op jit(solution)/shard_map/pallas_call | solution.py:133
  9.7 0.5 %collective-permute-start = (f32[80,960]{1,0:T(8,128)}, f32[80,960]{1,0:T(8,128)S(1)}, u32[]{:S(2)}, u32[]{:S(2)}) collective-permute-start(f32[80,960]{1,0:T(8,128)} %get-tuple-element.8), channel_id=1, source_target_pairs={{0,1},{1,0},{2,3},{3,2},{4,5},{5,4},{6,7},{7,6},{8,9},{9,8},{10,11... | collective-permute-start | bytes 921608 | tf_op jit(solution)/shard_map/ppermute | solution.py:19
  10.3 1.5 %collective-permute-done = f32[80,960]{1,0:T(8,128)S(1)} collective-permute-done((f32[80,960]{1,0:T(8,128)}, f32[80,960]{1,0:T(8,128)S(1)}, u32[]{:S(2)}, u32[]{:S(2)}) %collective-permute-start) | collective-permute-done | bytes 307232 | tf_op jit(solution)/shard_map/ppermute | solution.py:19
  11.7 0.9 %add_bitcast_fusion = f32[40,960]{1,0:T(8,128)S(1)} fusion(f32[2,40,960]{2,1,0:T(8,128)S(1)} %bitcast.41, s32[]{:T(128)S(6)} %select_n.49, f32[2,40,960]{2,1,0:T(8,128)} %bitcast.39), kind=kLoop, calls=%fused_computation.18 | loop fusion | flops 38400 | bytes 460804 | tf_op jit(solution)/shard_map/add | solution.py:34
  12.7 2.9 %collective-permute-start.1 = (f32[40,960]{1,0:T(8,128)S(1)}, f32[40,960]{1,0:T(8,128)S(1)}, u32[]{:S(2)}, u32[]{:S(2)}) collective-permute-start(f32[40,960]{1,0:T(8,128)S(1)} %add_bitcast_fusion), channel_id=1, source_target_pairs={{0,2},{1,3},{2,0},{3,1},{4,6},{5,7},{6,4},{7,5},{8,10},{9,11},{10,... | collective-permute-start | bytes 460808 | tf_op jit(solution)/shard_map/ppermute | solution.py:19
  15.6 0.0 copy-done
  15.6 0.0 copy-done.2
  15.6 0.0 copy-done.1
  15.6 0.2 convolution_select_fusion
  15.8 0.1 copy.17
  15.9 0.1 reshape.48
  16.0 4.1 %collective-permute-done.1 = f32[40,960]{1,0:T(8,128)S(1)} collective-permute-done((f32[40,960]{1,0:T(8,128)S(1)}, f32[40,960]{1,0:T(8,128)S(1)}, u32[]{:S(2)}, u32[]{:S(2)}) %collective-permute-start.1) | collective-permute-done | bytes 153632 | tf_op jit(solution)/shard_map/ppermute | solution.py:19
  20.1 0.9 %bitcast_add_fusion = f32[40,960]{1,0:T(8,128)S(1)} fusion(f32[40,960]{1,0:T(8,128)S(1)} %collective-permute-done.1, f32[2,40,960]{2,1,0:T(8,128)S(1)} %bitcast.42, s32[]{:T(128)S(6)} %select_n.48, f32[2,40,960]{2,1,0:T(8,128)} %bitcast.40), kind=kLoop, calls=%fused_computation.14 | loop fusion | flops 76800 | bytes 614404 | tf_op jit(solution)/shard_map/add | solution.py:38
  21.1 0.1 fusion.10
  21.2 1.8 %collective-permute-start.4 = (f32[41,640]{1,0:T(8,128)S(1)}, f32[41,640]{1,0:T(8,128)S(1)}, u32[]{:S(2)}, u32[]{:S(2)}) collective-permute-start(f32[41,640]{1,0:T(8,128)S(1)} %get-tuple-element.15), channel_id=1, source_target_pairs={{28,0},{0,4},{4,8},{8,12},{12,16},{16,20},{20,24},{24,28},{29,1},{... | collective-permute-start | bytes 314888 | tf_op jit(solution)/shard_map/ppermute | solution.py:14
  23.0 1.5 %collective-permute-start.2 = (f32[40,960]{1,0:T(8,128)S(1)}, f32[40,960]{1,0:T(8,128)S(1)}, u32[]{:S(2)}, u32[]{:S(2)}) collective-permute-start(f32[40,960]{1,0:T(8,128)S(1)} %bitcast_add_fusion), channel_id=1, source_target_pairs={{0,2},{1,3},{2,0},{3,1},{4,6},{5,7},{6,4},{7,5},{8,10},{9,11},{10,... | collective-permute-start | bytes 460808 | tf_op jit(solution)/shard_map/ppermute | solution.py:19
  24.5 3.2 %collective-permute-start.5 = (f32[41,640]{1,0:T(8,128)S(1)}, f32[41,640]{1,0:T(8,128)S(1)}, u32[]{:S(2)}, u32[]{:S(2)}) collective-permute-start(f32[41,640]{1,0:T(8,128)S(1)} %get-tuple-element.16), channel_id=1, source_target_pairs={{4,0},{8,4},{12,8},{16,12},{20,16},{24,20},{28,24},{0,28},{5,1},{9... | collective-permute-start | bytes 314888 | tf_op jit(solution)/shard_map/ppermute | solution.py:14
  27.7 1.2 %collective-permute-done.4 = f32[41,640]{1,0:T(8,128)S(1)} collective-permute-done((f32[41,640]{1,0:T(8,128)S(1)}, f32[41,640]{1,0:T(8,128)S(1)}, u32[]{:S(2)}, u32[]{:S(2)}) %collective-permute-start.4) | collective-permute-done | bytes 104992 | tf_op jit(solution)/shard_map/ppermute | solution.py:14
  28.9 0.0 collective-permute-done.2
  29.0 0.1 collective-permute-start.3
  29.1 2.0 %collective-permute-done.5 = f32[41,640]{1,0:T(8,128)S(1)} collective-permute-done((f32[41,640]{1,0:T(8,128)S(1)}, f32[41,640]{1,0:T(8,128)S(1)}, u32[]{:S(2)}, u32[]{:S(2)}) %collective-permute-start.5) | collective-permute-done | bytes 104992 | tf_op jit(solution)/shard_map/ppermute | solution.py:14
  31.1 0.1 pad_maximum_fusion.5
  31.2 0.1 pad_maximum_fusion.4
  31.3 0.0 collective-permute-done.3
  31.3 0.1 select_bitcast_fusion.1
  31.3 0.1 pad_maximum_fusion
  31.4 0.1 reshape.49
  31.5 0.3 fusion.2
  31.8 0.4 fusion
  32.2 0.5 convolution_bitcast_fusion
  32.8 0.2 all_to_all.8
  33.0 12.3 %all_to_all.10 = f32[8,1,2400]{2,1,0:T(1,128)S(1)} all-to-all(f32[8,1,2400]{2,1,0:T(1,128)S(1)} %all_to_all.8), channel_id=1, replica_groups=mesh['elem'=8,'cuts'=4] {'elem'}, dimensions={0} | all-to-all | bytes 153600 | tf_op jit(solution)/shard_map/all_to_all | solution.py:187
  45.2 0.2 reduce.2
  45.4 0.1 reshape.50
  45.6 0.7 %copy.22 = f32[8,3,20,40]{3,0,2,1:T(8,128)} copy(f32[8,3,20,40]{3,2,1,0:T(8,128)S(1)} %reshape.50) | data formatting | bytes 153600 | tf_op jit(solution)/shard_map/reshape | solution.py:188
  (11 shorter events, 0.2 us)
Async XLA Ops:
  0.0 15.6 %copy-start = (f32[4,16]{1,0:T(4,128)S(1)}, f32[4,16]{1,0:T(4,128)}, u32[]{:S(2)}) copy-start(f32[4,16]{1,0:T(4,128)} %param.11) | copy-start | bytes 772
  0.0 15.6 %copy-start.2 = (s32[1,20]{1,0:T(1,128)S(1)}, s32[1,20]{1,0:T(1,128)}, u32[]{:S(2)}) copy-start(s32[1,20]{1,0:T(1,128)} %param.10) | copy-start | bytes 244
  0.0 15.6 %copy-start.1 = (s32[1,20]{1,0:T(1,128)S(1)}, s32[1,20]{1,0:T(1,128)}, u32[]{:S(2)}) copy-start(s32[1,20]{1,0:T(1,128)} %param.9) | copy-start | bytes 244
  9.7 2.0 %collective-permute-start = (f32[80,960]{1,0:T(8,128)}, f32[80,960]{1,0:T(8,128)S(1)}, u32[]{:S(2)}, u32[]{:S(2)}) collective-permute-start(f32[80,960]{1,0:T(8,128)} %get-tuple-element.8), channel_id=1, source_target_pairs={{0,1},{1,0},{2,3},{3,2},{4,5},{5,4},{6,7},{7,6},{8,9},{9,8},{10,11... | collective-permute-start | bytes 921608 | tf_op jit(solution)/shard_map/ppermute | solution.py:19
  12.7 7.4 %collective-permute-start.1 = (f32[40,960]{1,0:T(8,128)S(1)}, f32[40,960]{1,0:T(8,128)S(1)}, u32[]{:S(2)}, u32[]{:S(2)}) collective-permute-start(f32[40,960]{1,0:T(8,128)S(1)} %add_bitcast_fusion), channel_id=1, source_target_pairs={{0,2},{1,3},{2,0},{3,1},{4,6},{5,7},{6,4},{7,5},{8,10},{9,11},{10,... | collective-permute-start | bytes 460808 | tf_op jit(solution)/shard_map/ppermute | solution.py:19
  21.2 7.7 %collective-permute-start.4 = (f32[41,640]{1,0:T(8,128)S(1)}, f32[41,640]{1,0:T(8,128)S(1)}, u32[]{:S(2)}, u32[]{:S(2)}) collective-permute-start(f32[41,640]{1,0:T(8,128)S(1)} %get-tuple-element.15), channel_id=1, source_target_pairs={{28,0},{0,4},{4,8},{8,12},{12,16},{16,20},{20,24},{24,28},{29,1},{... | collective-permute-start | bytes 314888 | tf_op jit(solution)/shard_map/ppermute | solution.py:14
  23.0 6.0 %collective-permute-start.2 = (f32[40,960]{1,0:T(8,128)S(1)}, f32[40,960]{1,0:T(8,128)S(1)}, u32[]{:S(2)}, u32[]{:S(2)}) collective-permute-start(f32[40,960]{1,0:T(8,128)S(1)} %bitcast_add_fusion), channel_id=1, source_target_pairs={{0,2},{1,3},{2,0},{3,1},{4,6},{5,7},{6,4},{7,5},{8,10},{9,11},{10,... | collective-permute-start | bytes 460808 | tf_op jit(solution)/shard_map/ppermute | solution.py:19
  24.5 6.6 %collective-permute-start.5 = (f32[41,640]{1,0:T(8,128)S(1)}, f32[41,640]{1,0:T(8,128)S(1)}, u32[]{:S(2)}, u32[]{:S(2)}) collective-permute-start(f32[41,640]{1,0:T(8,128)S(1)} %get-tuple-element.16), channel_id=1, source_target_pairs={{4,0},{8,4},{12,8},{16,12},{20,16},{24,20},{28,24},{0,28},{5,1},{9... | collective-permute-start | bytes 314888 | tf_op jit(solution)/shard_map/ppermute | solution.py:14
  29.0 2.3 %collective-permute-start.3 = (f32[2,40,960]{2,1,0:T(8,128)S(1)}, f32[2,40,960]{2,1,0:T(8,128)S(1)}, u32[]{:S(2)}, u32[]{:S(2)}) collective-permute-start(f32[2,40,960]{2,1,0:T(8,128)S(1)} %pad_maximum_fusion.1), channel_id=1, source_target_pairs={{0,1},{1,0},{2,3},{3,2},{4,5},{5,4},{6,7},{7,6},{8,9},{9,8},{10,11... | collective-permute-start | bytes 921608 | tf_op jit(solution)/shard_map/ppermute | solution.py:19

commit v15 on v6

--- a/solution.py
+++ b/solution.py
@@ -24,10 +24,10 @@
     me = lax.axis_index(axis)
     count = size // 2
     quarter = keep.shape[0] // count
-    half = (keep + swapped(send, axis, 1)).reshape(count, quarter, keep.shape[1])
     mine = me // 2
     if count == 2:
         theirs = 1 - mine
+        half = (keep + swapped(send, axis, 1)).reshape(count, quarter, keep.shape[1])
         share = lax.dynamic_index_in_dim(half, mine, 0, keepdims=False) + swapped(
             lax.dynamic_index_in_dim(half, theirs, 0, keepdims=False), axis, 2
         )
@@ -35,6 +35,7 @@
         first = jnp.where(mine == 0, share, other)
         second = jnp.where(mine == 0, other, share)
         return jnp.stack([first, second]), share
+    half = (keep + swapped(send, axis, 1)).reshape(count, quarter, keep.shape[1])
     bit = 2
     while bit < size:
         half = half + swapped(half, axis, bit)
@@ -111,7 +112,7 @@
 
 def pair_block(left_t, right_t):
     return lax.dot_general(
-        left_t, right_t, (((1,), (1,)), ((), ())), precision=lax.Precision.HIGHEST
+        left_t, right_t, (((1,), (1,)), ((), ())), precision=lax.Precision.HIGH
     )
 
 
@@ -150,7 +151,8 @@
     owners = lax.axis_size("elem")
     stacked = jnp.stack([block_left, block_diag, block_right], axis=0)
     pieces = stacked.reshape(3, owners, width // owners, quarter).transpose(1, 0, 2, 3)
-    return lax.all_to_all(pieces, "elem", split_axis=0, concat_axis=0, tiled=True)
+    received = lax.all_to_all(pieces.reshape(owners, -1), "elem", split_axis=0, concat_axis=0, tiled=True)
+    return received.reshape(pieces.shape)
 
 
 def solution(mesh):

time: 47.5 us -> 45.8 us (0.964)
  other arithmetic: 2.24 us -> 1.6 us
  matrix products: 1.97 us -> 1.39 us
  local copies, waits for them, and re-layouts: 2.05 us -> 1.54 us
    all_to_all x2 -> x1, local copies, waits for them, and re-layouts: 1.25 us -> 0.22 us  [local(): lax.all_to_all(pieces.reshape(owners, -1), 'elem', split_axis=0, concat_a...]
    reshape x0 -> x2, local copies, waits for them, and re-layouts: none -> 0.88 us  [local(): return received.reshape(pieces.shape)]
    all_to_all x1, other arithmetic: 0.83 us -> 0.19 us  [local(): lax.all_to_all(pieces.reshape(owners, -1), 'elem', split_axis=0, concat_a...]
    dot_general x3, matrix products: 1.76 us -> 1.18 us  [pair_block(): lax.dot_general(left_t, right_t, (((1,), (1,)), ((), ())), precision=lax....]
where the time goes in v15:
time: 45.8 us; the launch traced here: 45.6 us
  blocking collectives  12.3 us (27%)
  starting transfers between devices  10 us (22%)
  Pallas kernels  9.84 us (21%)
  waiting for transfers between devices  8.76 us (19%)
  other arithmetic  1.6 us (3%)
  local copies, waits for them, and re-layouts  1.54 us (3%)
  matrix products  1.39 us (3%)
    all_to_all x1, blocking collectives, local(): lax.all_to_all(pieces.reshape(owners, -1), 'elem', split_axis=0, concat_a...  12.3 us
    pallas_call x1, Pallas kernels, partial_coefficients(): pl.pallas_call(functools.partial(coefficient_kernel, quarter), out_shape=...  9.84 us
    ppermute x4, waiting for transfers between devices, swapped(): return lax.ppermute(block, axis, [(i, i ^ bit) for i in devices])  5.56 us
    ppermute x4, starting transfers between devices, swapped(): return lax.ppermute(block, axis, [(i, i ^ bit) for i in devices])  5 us
    ppermute x2, starting transfers between devices, passed_along(): return lax.ppermute(block, axis, route)  5 us
    ppermute x2, waiting for transfers between devices, passed_along(): return lax.ppermute(block, axis, route)  3.2 us
    dot_general x3, matrix products, pair_block(): lax.dot_general(left_t, right_t, (((1,), (1,)), ((), ())), precision=lax....  1.18 us
    add x1, other arithmetic, summed_rows(): keep + swapped(send, axis, 1)  1.02 us
  transfers between devices with their start and end apart: 6, of which 4 were waited for; matrix products, arithmetic and copies ran while one was open for 1% of the time, Pallas kernels for 0%

profile of v15, /device:TPU:0, one launch (start us, length us, event | category | flops | bytes accessed | tf_op | source)
XLA Modules:
  0.0 45.6 jit_solution(14050392828613406638)
XLA Ops:
  0.0 0.0 copy-start
  0.0 0.0 copy-start.2
  0.0 0.0 copy-start.1
  0.0 9.8 %shard_map.64 = (f32[80,960]{1,0:T(8,128)}, f32[80,960]{1,0:T(8,128)}) custom-call(s32[1]{0:T(128)} %bitcast.parity_ref, f32[1,8192]{1,0:T(1,128)} %weight_ref.1, bf16[160,8192]{1,0:T(8,128)(2,1)} %bitcast.37, bf16[960,8192]{1,0:T(8,128)(2,1)} %bitcast.34), custom_call_target="tpu_custom_call" | custom-call | flops 2516582400 | bytes 18997248 | tf_op jit(solution)/shard_map/pallas_call | solution.py:100
  9.8 0.5 %collective-permute-start = (f32[80,960]{1,0:T(8,128)}, f32[80,960]{1,0:T(8,128)S(1)}, u32[]{:S(2)}, u32[]{:S(2)}) collective-permute-start(f32[80,960]{1,0:T(8,128)} %get-tuple-element.8), channel_id=1, source_target_pairs={{0,1},{1,0},{2,3},{3,2},{4,5},{5,4},{6,7},{7,6},{8,9},{9,8},{10,11... | collective-permute-start | bytes 921608 | tf_op jit(solution)/shard_map/ppermute | solution.py:19
  10.3 1.5 %collective-permute-done = f32[80,960]{1,0:T(8,128)S(1)} collective-permute-done((f32[80,960]{1,0:T(8,128)}, f32[80,960]{1,0:T(8,128)S(1)}, u32[]{:S(2)}, u32[]{:S(2)}) %collective-permute-start) | collective-permute-done | bytes 307232 | tf_op jit(solution)/shard_map/ppermute | solution.py:19
  11.8 1.0 %add.22 = f32[80,960]{1,0:T(8,128)S(1)} add(f32[80,960]{1,0:T(8,128)} %get-tuple-element.7, f32[80,960]{1,0:T(8,128)S(1)} %collective-permute-done) | non-fusion elementwise | flops 76800 | bytes 921600 | tf_op jit(solution)/shard_map/add | solution.py:30
  12.8 3.0 %collective-permute-start.1 = (f32[40,960]{1,0:T(8,128)S(1)}, f32[40,960]{1,0:T(8,128)S(1)}, u32[]{:S(2)}, u32[]{:S(2)}) collective-permute-start(f32[40,960]{1,0:T(8,128)S(1)} %dynamic-slice_bitcast_fusion), channel_id=1, source_target_pairs={{0,2},{1,3},{2,0},{3,1},{4,6},{5,7},{6,4},{7,5},{8,10},{9,11},{10,... | collective-permute-start | bytes 460808 | tf_op jit(solution)/shard_map/ppermute | solution.py:19
  15.8 0.0 copy-done
  15.8 0.0 copy-done.2
  15.8 0.0 copy-done.1
  15.8 0.2 convolution_select_fusion
  16.0 0.1 copy.17
  16.1 0.1 reshape.42
  16.2 4.1 %collective-permute-done.1 = f32[40,960]{1,0:T(8,128)S(1)} collective-permute-done((f32[40,960]{1,0:T(8,128)S(1)}, f32[40,960]{1,0:T(8,128)S(1)}, u32[]{:S(2)}, u32[]{:S(2)}) %collective-permute-start.1) | collective-permute-done | bytes 153632 | tf_op jit(solution)/shard_map/ppermute | solution.py:19
  20.3 0.1 fusion.10
  20.4 1.8 %collective-permute-start.4 = (f32[41,640]{1,0:T(8,128)S(1)}, f32[41,640]{1,0:T(8,128)S(1)}, u32[]{:S(2)}, u32[]{:S(2)}) collective-permute-start(f32[41,640]{1,0:T(8,128)S(1)} %get-tuple-element.15), channel_id=1, source_target_pairs={{28,0},{0,4},{4,8},{8,12},{12,16},{16,20},{20,24},{24,28},{29,1},{... | collective-permute-start | bytes 314888 | tf_op jit(solution)/shard_map/ppermute | solution.py:14
  22.2 1.5 %collective-permute-start.2 = (f32[40,960]{1,0:T(8,128)S(1)}, f32[40,960]{1,0:T(8,128)S(1)}, u32[]{:S(2)}, u32[]{:S(2)}) collective-permute-start(f32[40,960]{1,0:T(8,128)S(1)} %bitcast_add_fusion), channel_id=1, source_target_pairs={{0,2},{1,3},{2,0},{3,1},{4,6},{5,7},{6,4},{7,5},{8,10},{9,11},{10,... | collective-permute-start | bytes 460808 | tf_op jit(solution)/shard_map/ppermute | solution.py:19
  23.7 3.2 %collective-permute-start.5 = (f32[41,640]{1,0:T(8,128)S(1)}, f32[41,640]{1,0:T(8,128)S(1)}, u32[]{:S(2)}, u32[]{:S(2)}) collective-permute-start(f32[41,640]{1,0:T(8,128)S(1)} %get-tuple-element.16), channel_id=1, source_target_pairs={{4,0},{8,4},{12,8},{16,12},{20,16},{24,20},{28,24},{0,28},{5,1},{9... | collective-permute-start | bytes 314888 | tf_op jit(solution)/shard_map/ppermute | solution.py:14
  26.9 1.2 %collective-permute-done.4 = f32[41,640]{1,0:T(8,128)S(1)} collective-permute-done((f32[41,640]{1,0:T(8,128)S(1)}, f32[41,640]{1,0:T(8,128)S(1)}, u32[]{:S(2)}, u32[]{:S(2)}) %collective-permute-start.4) | collective-permute-done | bytes 104992 | tf_op jit(solution)/shard_map/ppermute | solution.py:14
  28.2 0.0 collective-permute-done.2
  28.2 0.1 collective-permute-start.3
  28.3 2.0 %collective-permute-done.5 = f32[41,640]{1,0:T(8,128)S(1)} collective-permute-done((f32[41,640]{1,0:T(8,128)S(1)}, f32[41,640]{1,0:T(8,128)S(1)}, u32[]{:S(2)}, u32[]{:S(2)}) %collective-permute-start.5) | collective-permute-done | bytes 104992 | tf_op jit(solution)/shard_map/ppermute | solution.py:14
  30.3 0.1 pad_maximum_fusion.5
  30.4 0.1 pad_maximum_fusion.4
  30.5 0.0 collective-permute-done.3
  30.5 0.1 select_bitcast_fusion.1
  30.6 0.1 pad_maximum_fusion
  30.6 0.1 reshape.43
  30.7 0.3 fusion.2
  31.0 0.4 fusion
  31.5 0.5 %convolution_bitcast_fusion = f32[1,8,20,40]{3,2,1,0:T(8,128)S(1)} fusion(f32[8,20,960]{2,1,0:T(8,128)S(1)} %reshape.43, f32[40,960]{1,0:T(8,128)S(1)} %bitcast_add_fusion, f32[960]{0:T(1024)S(1)} %pad_maximum_fusion.5), kind=kOutput, calls=%fused_computation | convolution fusion | flops 36902400 | bytes 797440 | tf_op jit(solution)/shard_map/dot_general | solution.py:114
  32.0 0.2 all_to_all.8
  32.2 12.3 %all_to_all.10 = f32[8,1,2400]{2,1,0:T(1,128)S(1)} all-to-all(f32[8,1,2400]{2,1,0:T(1,128)S(1)} %all_to_all.8), channel_id=1, replica_groups=mesh['elem'=8,'cuts'=4] {'elem'}, dimensions={0} | all-to-all | bytes 153600 | tf_op jit(solution)/shard_map/all_to_all | solution.py:154
  44.5 0.2 reduce.2
  44.7 0.1 reshape.44
  44.8 0.7 %copy.22 = f32[8,3,20,40]{3,0,2,1:T(8,128)} copy(f32[8,3,20,40]{3,2,1,0:T(8,128)S(1)} %reshape.44) | data formatting | bytes 153600 | tf_op jit(solution)/shard_map/reshape | solution.py:155
  (13 shorter events, 0.2 us)
Async XLA Ops:
  0.0 15.8 %copy-start = (f32[4,16]{1,0:T(4,128)S(1)}, f32[4,16]{1,0:T(4,128)}, u32[]{:S(2)}) copy-start(f32[4,16]{1,0:T(4,128)} %param.11) | copy-start | bytes 772
  0.0 15.8 %copy-start.2 = (s32[1,20]{1,0:T(1,128)S(1)}, s32[1,20]{1,0:T(1,128)}, u32[]{:S(2)}) copy-start(s32[1,20]{1,0:T(1,128)} %param.10) | copy-start | bytes 244
  0.0 15.8 %copy-start.1 = (s32[1,20]{1,0:T(1,128)S(1)}, s32[1,20]{1,0:T(1,128)}, u32[]{:S(2)}) copy-start(s32[1,20]{1,0:T(1,128)} %param.9) | copy-start | bytes 244
  9.8 1.9 %collective-permute-start = (f32[80,960]{1,0:T(8,128)}, f32[80,960]{1,0:T(8,128)S(1)}, u32[]{:S(2)}, u32[]{:S(2)}) collective-permute-start(f32[80,960]{1,0:T(8,128)} %get-tuple-element.8), channel_id=1, source_target_pairs={{0,1},{1,0},{2,3},{3,2},{4,5},{5,4},{6,7},{7,6},{8,9},{9,8},{10,11... | collective-permute-start | bytes 921608 | tf_op jit(solution)/shard_map/ppermute | solution.py:19
  12.8 7.5 %collective-permute-start.1 = (f32[40,960]{1,0:T(8,128)S(1)}, f32[40,960]{1,0:T(8,128)S(1)}, u32[]{:S(2)}, u32[]{:S(2)}) collective-permute-start(f32[40,960]{1,0:T(8,128)S(1)} %dynamic-slice_bitcast_fusion), channel_id=1, source_target_pairs={{0,2},{1,3},{2,0},{3,1},{4,6},{5,7},{6,4},{7,5},{8,10},{9,11},{10,... | collective-permute-start | bytes 460808 | tf_op jit(solution)/shard_map/ppermute | solution.py:19
  20.4 7.7 %collective-permute-start.4 = (f32[41,640]{1,0:T(8,128)S(1)}, f32[41,640]{1,0:T(8,128)S(1)}, u32[]{:S(2)}, u32[]{:S(2)}) collective-permute-start(f32[41,640]{1,0:T(8,128)S(1)} %get-tuple-element.15), channel_id=1, source_target_pairs={{28,0},{0,4},{4,8},{8,12},{12,16},{16,20},{20,24},{24,28},{29,1},{... | collective-permute-start | bytes 314888 | tf_op jit(solution)/shard_map/ppermute | solution.py:14
  22.2 6.0 %collective-permute-start.2 = (f32[40,960]{1,0:T(8,128)S(1)}, f32[40,960]{1,0:T(8,128)S(1)}, u32[]{:S(2)}, u32[]{:S(2)}) collective-permute-start(f32[40,960]{1,0:T(8,128)S(1)} %bitcast_add_fusion), channel_id=1, source_target_pairs={{0,2},{1,3},{2,0},{3,1},{4,6},{5,7},{6,4},{7,5},{8,10},{9,11},{10,... | collective-permute-start | bytes 460808 | tf_op jit(solution)/shard_map/ppermute | solution.py:19
  23.7 6.6 %collective-permute-start.5 = (f32[41,640]{1,0:T(8,128)S(1)}, f32[41,640]{1,0:T(8,128)S(1)}, u32[]{:S(2)}, u32[]{:S(2)}) collective-permute-start(f32[41,640]{1,0:T(8,128)S(1)} %get-tuple-element.16), channel_id=1, source_target_pairs={{4,0},{8,4},{12,8},{16,12},{20,16},{24,20},{28,24},{0,28},{5,1},{9... | collective-permute-start | bytes 314888 | tf_op jit(solution)/shard_map/ppermute | solution.py:14
  28.2 2.3 %collective-permute-start.3 = (f32[2,40,960]{2,1,0:T(8,128)S(1)}, f32[2,40,960]{2,1,0:T(8,128)S(1)}, u32[]{:S(2)}, u32[]{:S(2)}) collective-permute-start(f32[2,40,960]{2,1,0:T(8,128)S(1)} %pad_maximum_fusion.1), channel_id=1, source_target_pairs={{0,1},{1,0},{2,3},{3,2},{4,5},{5,4},{6,7},{7,6},{8,9},{9,8},{10,11... | collective-permute-start | bytes 921608 | tf_op jit(solution)/shard_map/ppermute | solution.py:19

commit v16 on v15

--- a/solution.py
+++ b/solution.py
@@ -31,10 +31,12 @@
         share = lax.dynamic_index_in_dim(half, mine, 0, keepdims=False) + swapped(
             lax.dynamic_index_in_dim(half, theirs, 0, keepdims=False), axis, 2
         )
-        other = swapped(share, axis, 2)
-        first = jnp.where(mine == 0, share, other)
-        second = jnp.where(mine == 0, other, share)
-        return jnp.stack([first, second]), share
+        beside = swapped(share, axis, 1)
+        odd = (me & 1) != 0
+        here = jnp.stack([jnp.where(odd, beside, share), jnp.where(odd, share, beside)])
+        there = swapped(here, axis, 2)
+        whole = jnp.where(mine == 0, jnp.stack([here, there]), jnp.stack([there, here]))
+        return whole.reshape(size * quarter, keep.shape[1]), share
     half = (keep + swapped(send, axis, 1)).reshape(count, quarter, keep.shape[1])
     bit = 2
     while bit < size:
@@ -138,7 +140,7 @@
     to_left = jnp.concatenate([share[:, : 2 * span], energy_row], axis=0)
     from_left = passed_along(to_right, "elem", 1)
     from_right = passed_along(to_left, "elem", -1)
-    full_t = gathered_rows(half, "cuts")
+    full_t = half if half.ndim == 2 else gathered_rows(half, "cuts")
 
     left_energy = from_left[quarter, :span]
     right_energy = from_right[quarter, :span]

time: 45.8 us -> 49.1 us (1.072)
  waiting for transfers between devices: 8.76 us -> 14.6 us
  blocking collectives: 12.3 us -> 9.7 us
    ppermute x4, waiting for transfers between devices: 5.56 us -> 11.3 us  [swapped(): return lax.ppermute(block, axis, [(i, i ^ bit) for i in devices])]
    all_to_all x1, blocking collectives: 12.3 us -> 9.7 us  [local(): lax.all_to_all(pieces.reshape(owners, -1), 'elem', split_axis=0, concat_a...]
  transfers between devices with their start and end apart: 6 -> 6, of which waited for: 4 -> 5; matrix products, arithmetic and copies ran while one was open for 1% -> 1% of each run, Pallas kernels for 0% -> 0%
where the time goes in v16:
time: 49.1 us; the launch traced here: 48.9 us
  waiting for transfers between devices  14.6 us (30%)
  starting transfers between devices  10.1 us (21%)
  Pallas kernels  9.84 us (20%)
  blocking collectives  9.7 us (20%)
  other arithmetic  1.58 us (3%)
  local copies, waits for them, and re-layouts  1.54 us (3%)
  matrix products  1.38 us (3%)
    ppermute x4, waiting for transfers between devices, swapped(): return lax.ppermute(block, axis, [(i, i ^ bit) for i in devices])  11.3 us
    pallas_call x1, Pallas kernels, partial_coefficients(): pl.pallas_call(functools.partial(coefficient_kernel, quarter), out_shape=...  9.84 us
    all_to_all x1, blocking collectives, local(): lax.all_to_all(pieces.reshape(owners, -1), 'elem', split_axis=0, concat_a...  9.7 us
    ppermute x4, starting transfers between devices, swapped(): return lax.ppermute(block, axis, [(i, i ^ bit) for i in devices])  5.19 us
    ppermute x2, starting transfers between devices, passed_along(): return lax.ppermute(block, axis, route)  4.95 us
    ppermute x2, waiting for transfers between devices, passed_along(): return lax.ppermute(block, axis, route)  3.28 us
    dot_general x3, matrix products, pair_block(): lax.dot_general(left_t, right_t, (((1,), (1,)), ((), ())), precision=lax....  1.18 us
    add x1, other arithmetic, summed_rows(): keep + swapped(send, axis, 1)  1.02 us
  transfers between devices with their start and end apart: 6, of which 5 were waited for; matrix products, arithmetic and copies ran while one was open for 1% of the time, Pallas kernels for 0%

profile of v16, /device:TPU:0, one launch (start us, length us, event | category | flops | bytes accessed | tf_op | source)
XLA Modules:
  0.0 48.9 jit_solution(10714165166594979262)
XLA Ops:
  0.0 0.0 copy-start
  0.0 0.0 copy-start.2
  0.0 0.0 copy-start.1
  0.0 9.8 %shard_map.64 = (f32[80,960]{1,0:T(8,128)}, f32[80,960]{1,0:T(8,128)}) custom-call(s32[1]{0:T(128)} %bitcast.parity_ref, f32[1,8192]{1,0:T(1,128)} %weight_ref.1, bf16[160,8192]{1,0:T(8,128)(2,1)} %bitcast.34, bf16[960,8192]{1,0:T(8,128)(2,1)} %bitcast.31), custom_call_target="tpu_custom_call" | custom-call | flops 2516582400 | bytes 18997248 | tf_op jit(solution)/shard_map/pallas_call | solution.py:102
  9.8 0.5 collective-permute-start
  10.3 1.5 %collective-permute-done = f32[80,960]{1,0:T(8,128)S(1)} collective-permute-done((f32[80,960]{1,0:T(8,128)}, f32[80,960]{1,0:T(8,128)S(1)}, u32[]{:S(2)}, u32[]{:S(2)}) %collective-permute-start) | collective-permute-done | bytes 307232 | tf_op jit(solution)/shard_map/ppermute | solution.py:19
  11.8 1.0 %add.22 = f32[80,960]{1,0:T(8,128)S(1)} add(f32[80,960]{1,0:T(8,128)} %get-tuple-element.7, f32[80,960]{1,0:T(8,128)S(1)} %collective-permute-done) | non-fusion elementwise | flops 76800 | bytes 921600 | tf_op jit(solution)/shard_map/add | solution.py:30
  12.8 3.0 %collective-permute-start.1 = (f32[40,960]{1,0:T(8,128)S(1)}, f32[40,960]{1,0:T(8,128)S(1)}, u32[]{:S(2)}, u32[]{:S(2)}) collective-permute-start(f32[40,960]{1,0:T(8,128)S(1)} %dynamic-slice_bitcast_fusion), channel_id=1, source_target_pairs={{0,2},{1,3},{2,0},{3,1},{4,6},{5,7},{6,4},{7,5},{8,10},{9,11},{10,... | collective-permute-start | bytes 460808 | tf_op jit(solution)/shard_map/ppermute | solution.py:19
  15.8 0.0 copy-done
  15.8 0.0 copy-done.2
  15.8 0.0 copy-done.1
  15.8 0.2 convolution_select_fusion
  16.0 0.1 copy.14
  16.1 0.1 reshape.50
  16.2 4.1 %collective-permute-done.1 = f32[40,960]{1,0:T(8,128)S(1)} collective-permute-done((f32[40,960]{1,0:T(8,128)S(1)}, f32[40,960]{1,0:T(8,128)S(1)}, u32[]{:S(2)}, u32[]{:S(2)}) %collective-permute-start.1) | collective-permute-done | bytes 153632 | tf_op jit(solution)/shard_map/ppermute | solution.py:19
  20.3 0.1 fusion.11
  20.4 1.8 %collective-permute-start.4 = (f32[41,640]{1,0:T(8,128)S(1)}, f32[41,640]{1,0:T(8,128)S(1)}, u32[]{:S(2)}, u32[]{:S(2)}) collective-permute-start(f32[41,640]{1,0:T(8,128)S(1)} %get-tuple-element.15), channel_id=1, source_target_pairs={{28,0},{0,4},{4,8},{8,12},{12,16},{16,20},{20,24},{24,28},{29,1},{... | collective-permute-start | bytes 314888 | tf_op jit(solution)/shard_map/ppermute | solution.py:14
  22.2 0.0 collective-permute-start.2
  22.2 3.2 %collective-permute-start.5 = (f32[41,640]{1,0:T(8,128)S(1)}, f32[41,640]{1,0:T(8,128)S(1)}, u32[]{:S(2)}, u32[]{:S(2)}) collective-permute-start(f32[41,640]{1,0:T(8,128)S(1)} %get-tuple-element.16), channel_id=1, source_target_pairs={{4,0},{8,4},{12,8},{16,12},{20,16},{24,20},{28,24},{0,28},{5,1},{9... | collective-permute-start | bytes 314888 | tf_op jit(solution)/shard_map/ppermute | solution.py:14
  25.4 2.8 %collective-permute-done.4 = f32[41,640]{1,0:T(8,128)S(1)} collective-permute-done((f32[41,640]{1,0:T(8,128)S(1)}, f32[41,640]{1,0:T(8,128)S(1)}, u32[]{:S(2)}, u32[]{:S(2)}) %collective-permute-start.4) | collective-permute-done | bytes 104992 | tf_op jit(solution)/shard_map/ppermute | solution.py:14
  28.2 0.0 collective-permute-done.2
  28.2 0.1 fusion.10
  28.3 1.8 %collective-permute-start.3 = (f32[2,40,960]{2,1,0:T(8,128)S(1)}, f32[2,40,960]{2,1,0:T(8,128)S(1)}, u32[]{:S(2)}, u32[]{:S(2)}) collective-permute-start(f32[2,40,960]{2,1,0:T(8,128)S(1)} %get-tuple-element.10), channel_id=1, source_target_pairs={{0,2},{1,3},{2,0},{3,1},{4,6},{5,7},{6,4},{7,5},{8,10},{9,11},{10,... | collective-permute-start | bytes 921608 | tf_op jit(solution)/shard_map/ppermute | solution.py:19
  30.0 0.5 %collective-permute-done.5 = f32[41,640]{1,0:T(8,128)S(1)} collective-permute-done((f32[41,640]{1,0:T(8,128)S(1)}, f32[41,640]{1,0:T(8,128)S(1)}, u32[]{:S(2)}, u32[]{:S(2)}) %collective-permute-start.5) | collective-permute-done | bytes 104992 | tf_op jit(solution)/shard_map/ppermute | solution.py:14
  30.6 0.1 pad_maximum_fusion.4
  30.7 0.1 pad_maximum_fusion.3
  30.7 5.7 %collective-permute-done.3 = f32[2,40,960]{2,1,0:T(8,128)S(1)} collective-permute-done((f32[2,40,960]{2,1,0:T(8,128)S(1)}, f32[2,40,960]{2,1,0:T(8,128)S(1)}, u32[]{:S(2)}, u32[]{:S(2)}) %collective-permute-start.3) | collective-permute-done | bytes 307232 | tf_op jit(solution)/shard_map/ppermute | solution.py:19
  36.5 0.1 maximum_select_fusion
  36.5 0.1 select_n.59
  36.6 0.3 fusion.2
  36.9 0.4 fusion
  37.4 0.5 convolution_bitcast_fusion
  37.9 0.2 all_to_all.8
  38.1 9.7 %all_to_all.10 = f32[8,1,2400]{2,1,0:T(1,128)S(1)} all-to-all(f32[8,1,2400]{2,1,0:T(1,128)S(1)} %all_to_all.8), channel_id=1, replica_groups=mesh['elem'=8,'cuts'=4] {'elem'}, dimensions={0} | all-to-all | bytes 153600 | tf_op jit(solution)/shard_map/all_to_all | solution.py:156
  47.8 0.2 reduce.2
  48.0 0.1 reshape.51
  48.1 0.7 %copy.19 = f32[8,3,20,40]{3,0,2,1:T(8,128)} copy(f32[8,3,20,40]{3,2,1,0:T(8,128)S(1)} %reshape.51) | data formatting | bytes 153600 | tf_op jit(solution)/shard_map/reshape | solution.py:157
  (12 shorter events, 0.2 us)
Async XLA Ops:
  0.0 15.8 %copy-start = (f32[4,16]{1,0:T(4,128)S(1)}, f32[4,16]{1,0:T(4,128)}, u32[]{:S(2)}) copy-start(f32[4,16]{1,0:T(4,128)} %param.11) | copy-start | bytes 772
  0.0 15.8 %copy-start.2 = (s32[1,20]{1,0:T(1,128)S(1)}, s32[1,20]{1,0:T(1,128)}, u32[]{:S(2)}) copy-start(s32[1,20]{1,0:T(1,128)} %param.10) | copy-start | bytes 244
  0.0 15.8 %copy-start.1 = (s32[1,20]{1,0:T(1,128)S(1)}, s32[1,20]{1,0:T(1,128)}, u32[]{:S(2)}) copy-start(s32[1,20]{1,0:T(1,128)} %param.9) | copy-start | bytes 244
  9.8 1.9 %collective-permute-start = (f32[80,960]{1,0:T(8,128)}, f32[80,960]{1,0:T(8,128)S(1)}, u32[]{:S(2)}, u32[]{:S(2)}) collective-permute-start(f32[80,960]{1,0:T(8,128)} %get-tuple-element.8), channel_id=1, source_target_pairs={{0,1},{1,0},{2,3},{3,2},{4,5},{5,4},{6,7},{7,6},{8,9},{9,8},{10,11... | collective-permute-start | bytes 921608 | tf_op jit(solution)/shard_map/ppermute | solution.py:19
  12.8 7.5 %collective-permute-start.1 = (f32[40,960]{1,0:T(8,128)S(1)}, f32[40,960]{1,0:T(8,128)S(1)}, u32[]{:S(2)}, u32[]{:S(2)}) collective-permute-start(f32[40,960]{1,0:T(8,128)S(1)} %dynamic-slice_bitcast_fusion), channel_id=1, source_target_pairs={{0,2},{1,3},{2,0},{3,1},{4,6},{5,7},{6,4},{7,5},{8,10},{9,11},{10,... | collective-permute-start | bytes 460808 | tf_op jit(solution)/shard_map/ppermute | solution.py:19
  20.4 7.7 %collective-permute-start.4 = (f32[41,640]{1,0:T(8,128)S(1)}, f32[41,640]{1,0:T(8,128)S(1)}, u32[]{:S(2)}, u32[]{:S(2)}) collective-permute-start(f32[41,640]{1,0:T(8,128)S(1)} %get-tuple-element.15), channel_id=1, source_target_pairs={{28,0},{0,4},{4,8},{8,12},{12,16},{16,20},{20,24},{24,28},{29,1},{... | collective-permute-start | bytes 314888 | tf_op jit(solution)/shard_map/ppermute | solution.py:14
  22.2 6.0 %collective-permute-start.2 = (f32[40,960]{1,0:T(8,128)S(1)}, f32[40,960]{1,0:T(8,128)S(1)}, u32[]{:S(2)}, u32[]{:S(2)}) collective-permute-start(f32[40,960]{1,0:T(8,128)S(1)} %bitcast_add_fusion), channel_id=1, source_target_pairs={{0,1},{1,0},{2,3},{3,2},{4,5},{5,4},{6,7},{7,6},{8,9},{9,8},{10,11... | collective-permute-start | bytes 460808 | tf_op jit(solution)/shard_map/ppermute | solution.py:19
  22.2 8.4 %collective-permute-start.5 = (f32[41,640]{1,0:T(8,128)S(1)}, f32[41,640]{1,0:T(8,128)S(1)}, u32[]{:S(2)}, u32[]{:S(2)}) collective-permute-start(f32[41,640]{1,0:T(8,128)S(1)} %get-tuple-element.16), channel_id=1, source_target_pairs={{4,0},{8,4},{12,8},{16,12},{20,16},{24,20},{28,24},{0,28},{5,1},{9... | collective-permute-start | bytes 314888 | tf_op jit(solution)/shard_map/ppermute | solution.py:14
  28.3 8.2 %collective-permute-start.3 = (f32[2,40,960]{2,1,0:T(8,128)S(1)}, f32[2,40,960]{2,1,0:T(8,128)S(1)}, u32[]{:S(2)}, u32[]{:S(2)}) collective-permute-start(f32[2,40,960]{2,1,0:T(8,128)S(1)} %get-tuple-element.10), channel_id=1, source_target_pairs={{0,2},{1,3},{2,0},{3,1},{4,6},{5,7},{6,4},{7,5},{8,10},{9,11},{10,... | collective-permute-start | bytes 921608 | tf_op jit(solution)/shard_map/ppermute | solution.py:19

commit v17 on v15

--- a/solution.py
+++ b/solution.py
@@ -52,30 +52,30 @@
     return jnp.stack([low, high], axis=1).reshape(count * 2 * quarter, columns)
 
 
-def coefficient_kernel(quarter, parity_ref, weight_ref, basis_ref, projector_ref, keep_ref, send_ref, total_ref):
+def coefficient_kernel(quarter, parity_ref, weight_ref, basis_ref, projector_ref, keep_ref, send_ref):
     step = pl.program_id(0)
     scaled = (basis_ref[...].astype(jnp.float32) * weight_ref[...]).astype(jnp.bfloat16)
     product = lax.dot_general(
         scaled, projector_ref[...], (((1,), (1,)), ((), ())), preferred_element_type=jnp.float32
     )
+    odd = parity_ref[0] == 1
+    count = keep_ref.shape[0] // quarter
+    for t in range(count):
+        even_rows = product[2 * t * quarter : (2 * t + 1) * quarter]
+        odd_rows = product[(2 * t + 1) * quarter : (2 * t + 2) * quarter]
+        rows = slice(t * quarter, (t + 1) * quarter)
+        kept = jnp.where(odd, odd_rows, even_rows)
+        sent = jnp.where(odd, even_rows, odd_rows)
 
-    @pl.when(step == 0)
-    def _():
-        total_ref[...] = product
+        @pl.when(step == 0)
+        def _():
+            keep_ref[rows, :] = kept
+            send_ref[rows, :] = sent
 
-    @pl.when(step > 0)
-    def _():
-        total_ref[...] += product
-
-    @pl.when(step == pl.num_programs(0) - 1)
-    def _():
-        count = keep_ref.shape[0] // quarter
-        odd = parity_ref[0]
-        for t in range(count):
-            kept = pl.multiple_of((2 * t + odd) * quarter, 8)
-            sent = pl.multiple_of((2 * t + 1 - odd) * quarter, 8)
-            keep_ref[t * quarter : (t + 1) * quarter, :] = total_ref[pl.ds(kept, quarter), :]
-            send_ref[t * quarter : (t + 1) * quarter, :] = total_ref[pl.ds(sent, quarter), :]
+        @pl.when(step > 0)
+        def _():
+            keep_ref[rows, :] += kept
+            send_ref[rows, :] += sent
 
 
 def partial_coefficients(flat_projectors, basis_t, weight, parity, quarter):
@@ -95,7 +95,6 @@
             pl.BlockSpec((width // 2, rows), lambda k, p: (0, 0)),
             pl.BlockSpec((width // 2, rows), lambda k, p: (0, 0)),
         ],
-        scratch_shapes=[pltpu.VMEM((width, rows), jnp.float32)],
     )
     return pl.pallas_call(
         functools.partial(coefficient_kernel, quarter),

time: 45.8 us -> 45.7 us (level)
  no operation moved by 1% of the time
where the time goes in v17:
time: 45.7 us; the launch traced here: 45.6 us
  blocking collectives  12.3 us (27%)
  starting transfers between devices  10 us (22%)
  Pallas kernels  9.83 us (22%)
  waiting for transfers between devices  8.76 us (19%)
  other arithmetic  1.6 us (4%)
  local copies, waits for them, and re-layouts  1.54 us (3%)
  matrix products  1.39 us (3%)
    all_to_all x1, blocking collectives, local(): lax.all_to_all(pieces.reshape(owners, -1), 'elem', split_axis=0, concat_a...  12.3 us
    pallas_call x1, Pallas kernels, partial_coefficients(): pl.pallas_call(functools.partial(coefficient_kernel, quarter), out_shape=...  9.83 us
    ppermute x4, waiting for transfers between devices, swapped(): return lax.ppermute(block, axis, [(i, i ^ bit) for i in devices])  5.56 us
    ppermute x4, starting transfers between devices, swapped(): return lax.ppermute(block, axis, [(i, i ^ bit) for i in devices])  5 us
    ppermute x2, starting transfers between devices, passed_along(): return lax.ppermute(block, axis, route)  5 us
    ppermute x2, waiting for transfers between devices, passed_along(): return lax.ppermute(block, axis, route)  3.2 us
    dot_general x3, matrix products, pair_block(): lax.dot_general(left_t, right_t, (((1,), (1,)), ((), ())), precision=lax....  1.18 us
    add x1, other arithmetic, summed_rows(): keep + swapped(send, axis, 1)  1.02 us
  transfers between devices with their start and end apart: 6, of which 4 were waited for; matrix products, arithmetic and copies ran while one was open for 1% of the time, Pallas kernels for 0%

profile of v17, /device:TPU:0, one launch (start us, length us, event | category | flops | bytes accessed | tf_op | source)
XLA Modules:
  0.0 45.6 jit_solution(16100476668382299329)
XLA Ops:
  0.0 0.0 copy-start
  0.0 0.0 copy-start.2
  0.0 0.0 copy-start.1
  0.0 9.8 %shard_map.64 = (f32[80,960]{1,0:T(8,128)}, f32[80,960]{1,0:T(8,128)}) custom-call(s32[1]{0:T(128)} %bitcast.parity_ref, f32[1,8192]{1,0:T(1,128)} %weight_ref.1, bf16[160,8192]{1,0:T(8,128)(2,1)} %bitcast.37, bf16[960,8192]{1,0:T(8,128)(2,1)} %bitcast.34), custom_call_target="tpu_custom_call" | custom-call | flops 2516582400 | bytes 18997248 | tf_op jit(solution)/shard_map/pallas_call | solution.py:99
  9.8 0.5 %collective-permute-start = (f32[80,960]{1,0:T(8,128)}, f32[80,960]{1,0:T(8,128)S(1)}, u32[]{:S(2)}, u32[]{:S(2)}) collective-permute-start(f32[80,960]{1,0:T(8,128)} %get-tuple-element.8), channel_id=1, source_target_pairs={{0,1},{1,0},{2,3},{3,2},{4,5},{5,4},{6,7},{7,6},{8,9},{9,8},{10,11... | collective-permute-start | bytes 921608 | tf_op jit(solution)/shard_map/ppermute | solution.py:19
  10.3 1.5 %collective-permute-done = f32[80,960]{1,0:T(8,128)S(1)} collective-permute-done((f32[80,960]{1,0:T(8,128)}, f32[80,960]{1,0:T(8,128)S(1)}, u32[]{:S(2)}, u32[]{:S(2)}) %collective-permute-start) | collective-permute-done | bytes 307232 | tf_op jit(solution)/shard_map/ppermute | solution.py:19
  11.8 1.0 %add.22 = f32[80,960]{1,0:T(8,128)S(1)} add(f32[80,960]{1,0:T(8,128)} %get-tuple-element.7, f32[80,960]{1,0:T(8,128)S(1)} %collective-permute-done) | non-fusion elementwise | flops 76800 | bytes 921600 | tf_op jit(solution)/shard_map/add | solution.py:30
  12.8 3.0 %collective-permute-start.1 = (f32[40,960]{1,0:T(8,128)S(1)}, f32[40,960]{1,0:T(8,128)S(1)}, u32[]{:S(2)}, u32[]{:S(2)}) collective-permute-start(f32[40,960]{1,0:T(8,128)S(1)} %dynamic-slice_bitcast_fusion), channel_id=1, source_target_pairs={{0,2},{1,3},{2,0},{3,1},{4,6},{5,7},{6,4},{7,5},{8,10},{9,11},{10,... | collective-permute-start | bytes 460808 | tf_op jit(solution)/shard_map/ppermute | solution.py:19
  15.8 0.0 copy-done
  15.8 0.0 copy-done.2
  15.8 0.0 copy-done.1
  15.8 0.2 convolution_select_fusion
  16.0 0.1 copy.17
  16.1 0.1 reshape.42
  16.2 4.1 %collective-permute-done.1 = f32[40,960]{1,0:T(8,128)S(1)} collective-permute-done((f32[40,960]{1,0:T(8,128)S(1)}, f32[40,960]{1,0:T(8,128)S(1)}, u32[]{:S(2)}, u32[]{:S(2)}) %collective-permute-start.1) | collective-permute-done | bytes 153632 | tf_op jit(solution)/shard_map/ppermute | solution.py:19
  20.3 0.1 fusion.10
  20.4 1.8 %collective-permute-start.4 = (f32[41,640]{1,0:T(8,128)S(1)}, f32[41,640]{1,0:T(8,128)S(1)}, u32[]{:S(2)}, u32[]{:S(2)}) collective-permute-start(f32[41,640]{1,0:T(8,128)S(1)} %get-tuple-element.15), channel_id=1, source_target_pairs={{28,0},{0,4},{4,8},{8,12},{12,16},{16,20},{20,24},{24,28},{29,1},{... | collective-permute-start | bytes 314888 | tf_op jit(solution)/shard_map/ppermute | solution.py:14
  22.2 1.5 %collective-permute-start.2 = (f32[40,960]{1,0:T(8,128)S(1)}, f32[40,960]{1,0:T(8,128)S(1)}, u32[]{:S(2)}, u32[]{:S(2)}) collective-permute-start(f32[40,960]{1,0:T(8,128)S(1)} %bitcast_add_fusion), channel_id=1, source_target_pairs={{0,2},{1,3},{2,0},{3,1},{4,6},{5,7},{6,4},{7,5},{8,10},{9,11},{10,... | collective-permute-start | bytes 460808 | tf_op jit(solution)/shard_map/ppermute | solution.py:19
  23.7 3.2 %collective-permute-start.5 = (f32[41,640]{1,0:T(8,128)S(1)}, f32[41,640]{1,0:T(8,128)S(1)}, u32[]{:S(2)}, u32[]{:S(2)}) collective-permute-start(f32[41,640]{1,0:T(8,128)S(1)} %get-tuple-element.16), channel_id=1, source_target_pairs={{4,0},{8,4},{12,8},{16,12},{20,16},{24,20},{28,24},{0,28},{5,1},{9... | collective-permute-start | bytes 314888 | tf_op jit(solution)/shard_map/ppermute | solution.py:14
  26.9 1.2 %collective-permute-done.4 = f32[41,640]{1,0:T(8,128)S(1)} collective-permute-done((f32[41,640]{1,0:T(8,128)S(1)}, f32[41,640]{1,0:T(8,128)S(1)}, u32[]{:S(2)}, u32[]{:S(2)}) %collective-permute-start.4) | collective-permute-done | bytes 104992 | tf_op jit(solution)/shard_map/ppermute | solution.py:14
  28.2 0.0 collective-permute-done.2
  28.2 0.1 collective-permute-start.3
  28.3 2.0 %collective-permute-done.5 = f32[41,640]{1,0:T(8,128)S(1)} collective-permute-done((f32[41,640]{1,0:T(8,128)S(1)}, f32[41,640]{1,0:T(8,128)S(1)}, u32[]{:S(2)}, u32[]{:S(2)}) %collective-permute-start.5) | collective-permute-done | bytes 104992 | tf_op jit(solution)/shard_map/ppermute | solution.py:14
  30.3 0.1 pad_maximum_fusion.5
  30.4 0.1 pad_maximum_fusion.4
  30.5 0.0 collective-permute-done.3
  30.5 0.1 select_bitcast_fusion.1
  30.6 0.1 pad_maximum_fusion
  30.6 0.1 reshape.43
  30.7 0.3 fusion.2
  31.0 0.4 fusion
  31.5 0.5 %convolution_bitcast_fusion = f32[1,8,20,40]{3,2,1,0:T(8,128)S(1)} fusion(f32[8,20,960]{2,1,0:T(8,128)S(1)} %reshape.43, f32[40,960]{1,0:T(8,128)S(1)} %bitcast_add_fusion, f32[960]{0:T(1024)S(1)} %pad_maximum_fusion.5), kind=kOutput, calls=%fused_computation | convolution fusion | flops 36902400 | bytes 797440 | tf_op jit(solution)/shard_map/dot_general | solution.py:113
  32.0 0.2 all_to_all.8
  32.2 12.3 %all_to_all.10 = f32[8,1,2400]{2,1,0:T(1,128)S(1)} all-to-all(f32[8,1,2400]{2,1,0:T(1,128)S(1)} %all_to_all.8), channel_id=1, replica_groups=mesh['elem'=8,'cuts'=4] {'elem'}, dimensions={0} | all-to-all | bytes 153600 | tf_op jit(solution)/shard_map/all_to_all | solution.py:153
  44.5 0.2 reduce.2
  44.7 0.1 reshape.44
  44.8 0.7 %copy.22 = f32[8,3,20,40]{3,0,2,1:T(8,128)} copy(f32[8,3,20,40]{3,2,1,0:T(8,128)S(1)} %reshape.44) | data formatting | bytes 153600 | tf_op jit(solution)/shard_map/reshape | solution.py:154
  (13 shorter events, 0.2 us)
Async XLA Ops:
  0.0 15.8 %copy-start = (f32[4,16]{1,0:T(4,128)S(1)}, f32[4,16]{1,0:T(4,128)}, u32[]{:S(2)}) copy-start(f32[4,16]{1,0:T(4,128)} %param.11) | copy-start | bytes 772
  0.0 15.8 %copy-start.2 = (s32[1,20]{1,0:T(1,128)S(1)}, s32[1,20]{1,0:T(1,128)}, u32[]{:S(2)}) copy-start(s32[1,20]{1,0:T(1,128)} %param.10) | copy-start | bytes 244
  0.0 15.8 %copy-start.1 = (s32[1,20]{1,0:T(1,128)S(1)}, s32[1,20]{1,0:T(1,128)}, u32[]{:S(2)}) copy-start(s32[1,20]{1,0:T(1,128)} %param.9) | copy-start | bytes 244
  9.8 1.9 %collective-permute-start = (f32[80,960]{1,0:T(8,128)}, f32[80,960]{1,0:T(8,128)S(1)}, u32[]{:S(2)}, u32[]{:S(2)}) collective-permute-start(f32[80,960]{1,0:T(8,128)} %get-tuple-element.8), channel_id=1, source_target_pairs={{0,1},{1,0},{2,3},{3,2},{4,5},{5,4},{6,7},{7,6},{8,9},{9,8},{10,11... | collective-permute-start | bytes 921608 | tf_op jit(solution)/shard_map/ppermute | solution.py:19
  12.8 7.5 %collective-permute-start.1 = (f32[40,960]{1,0:T(8,128)S(1)}, f32[40,960]{1,0:T(8,128)S(1)}, u32[]{:S(2)}, u32[]{:S(2)}) collective-permute-start(f32[40,960]{1,0:T(8,128)S(1)} %dynamic-slice_bitcast_fusion), channel_id=1, source_target_pairs={{0,2},{1,3},{2,0},{3,1},{4,6},{5,7},{6,4},{7,5},{8,10},{9,11},{10,... | collective-permute-start | bytes 460808 | tf_op jit(solution)/shard_map/ppermute | solution.py:19
  20.4 7.7 %collective-permute-start.4 = (f32[41,640]{1,0:T(8,128)S(1)}, f32[41,640]{1,0:T(8,128)S(1)}, u32[]{:S(2)}, u32[]{:S(2)}) collective-permute-start(f32[41,640]{1,0:T(8,128)S(1)} %get-tuple-element.15), channel_id=1, source_target_pairs={{28,0},{0,4},{4,8},{8,12},{12,16},{16,20},{20,24},{24,28},{29,1},{... | collective-permute-start | bytes 314888 | tf_op jit(solution)/shard_map/ppermute | solution.py:14
  22.2 6.0 %collective-permute-start.2 = (f32[40,960]{1,0:T(8,128)S(1)}, f32[40,960]{1,0:T(8,128)S(1)}, u32[]{:S(2)}, u32[]{:S(2)}) collective-permute-start(f32[40,960]{1,0:T(8,128)S(1)} %bitcast_add_fusion), channel_id=1, source_target_pairs={{0,2},{1,3},{2,0},{3,1},{4,6},{5,7},{6,4},{7,5},{8,10},{9,11},{10,... | collective-permute-start | bytes 460808 | tf_op jit(solution)/shard_map/ppermute | solution.py:19
  23.7 6.6 %collective-permute-start.5 = (f32[41,640]{1,0:T(8,128)S(1)}, f32[41,640]{1,0:T(8,128)S(1)}, u32[]{:S(2)}, u32[]{:S(2)}) collective-permute-start(f32[41,640]{1,0:T(8,128)S(1)} %get-tuple-element.16), channel_id=1, source_target_pairs={{4,0},{8,4},{12,8},{16,12},{20,16},{24,20},{28,24},{0,28},{5,1},{9... | collective-permute-start | bytes 314888 | tf_op jit(solution)/shard_map/ppermute | solution.py:14
  28.2 2.3 %collective-permute-start.3 = (f32[2,40,960]{2,1,0:T(8,128)S(1)}, f32[2,40,960]{2,1,0:T(8,128)S(1)}, u32[]{:S(2)}, u32[]{:S(2)}) collective-permute-start(f32[2,40,960]{2,1,0:T(8,128)S(1)} %pad_maximum_fusion.1), channel_id=1, source_target_pairs={{0,1},{1,0},{2,3},{3,2},{4,5},{5,4},{6,7},{7,6},{8,9},{9,8},{10,11... | collective-permute-start | bytes 921608 | tf_op jit(solution)/shard_map/ppermute | solution.py:19

commit v18 on v17

--- a/solution.py
+++ b/solution.py
@@ -81,7 +81,7 @@
 def partial_coefficients(flat_projectors, basis_t, weight, parity, quarter):
     rows, points = flat_projectors.shape
     width = basis_t.shape[0]
-    depth = min(points, 4096)
+    depth = min(points, 2048)
     half = jax.ShapeDtypeStruct((width // 2, rows), jnp.float32)
     grid_spec = pltpu.PrefetchScalarGridSpec(
         num_scalar_prefetch=1,

time: 45.7 us -> 46 us (level)
  no operation moved by 1% of the time
where the time goes in v18:
time: 46 us; the launch traced here: 45.8 us
  blocking collectives  12.3 us (27%)
  Pallas kernels  10.1 us (22%)
  starting transfers between devices  10 us (22%)
  waiting for transfers between devices  8.76 us (19%)
  other arithmetic  1.6 us (3%)
  local copies, waits for them, and re-layouts  1.54 us (3%)
  matrix products  1.39 us (3%)
    all_to_all x1, blocking collectives, local(): lax.all_to_all(pieces.reshape(owners, -1), 'elem', split_axis=0, concat_a...  12.3 us
    pallas_call x1, Pallas kernels, partial_coefficients(): pl.pallas_call(functools.partial(coefficient_kernel, quarter), out_shape=...  10.1 us
    ppermute x4, waiting for transfers between devices, swapped(): return lax.ppermute(block, axis, [(i, i ^ bit) for i in devices])  5.56 us
    ppermute x4, starting transfers between devices, swapped(): return lax.ppermute(block, axis, [(i, i ^ bit) for i in devices])  5 us
    ppermute x2, starting transfers between devices, passed_along(): return lax.ppermute(block, axis, route)  5 us
    ppermute x2, waiting for transfers between devices, passed_along(): return lax.ppermute(block, axis, route)  3.2 us
    dot_general x3, matrix products, pair_block(): lax.dot_general(left_t, right_t, (((1,), (1,)), ((), ())), precision=lax....  1.18 us
    add x1, other arithmetic, summed_rows(): keep + swapped(send, axis, 1)  1.02 us
  transfers between devices with their start and end apart: 6, of which 4 were waited for; matrix products, arithmetic and copies ran while one was open for 1% of the time, Pallas kernels for 0%

profile of v18, /device:TPU:0, one launch (start us, length us, event | category | flops | bytes accessed | tf_op | source)
XLA Modules:
  0.0 45.8 jit_solution(13922665758321285948)
XLA Ops:
  0.0 0.0 copy-start
  0.0 0.0 copy-start.2
  0.0 0.0 copy-start.1
  0.0 10.1 %shard_map.64 = (f32[80,960]{1,0:T(8,128)}, f32[80,960]{1,0:T(8,128)}) custom-call(s32[1]{0:T(128)} %bitcast.parity_ref, f32[1,8192]{1,0:T(1,128)} %weight_ref.1, bf16[160,8192]{1,0:T(8,128)(2,1)} %bitcast.37, bf16[960,8192]{1,0:T(8,128)(2,1)} %bitcast.34), custom_call_target="tpu_custom_call" | custom-call | flops 2516582400 | bytes 18997248 | tf_op jit(solution)/shard_map/pallas_call | solution.py:99
  10.1 0.5 %collective-permute-start = (f32[80,960]{1,0:T(8,128)}, f32[80,960]{1,0:T(8,128)S(1)}, u32[]{:S(2)}, u32[]{:S(2)}) collective-permute-start(f32[80,960]{1,0:T(8,128)} %get-tuple-element.8), channel_id=1, source_target_pairs={{0,1},{1,0},{2,3},{3,2},{4,5},{5,4},{6,7},{7,6},{8,9},{9,8},{10,11... | collective-permute-start | bytes 921608 | tf_op jit(solution)/shard_map/ppermute | solution.py:19
  10.5 1.5 %collective-permute-done = f32[80,960]{1,0:T(8,128)S(1)} collective-permute-done((f32[80,960]{1,0:T(8,128)}, f32[80,960]{1,0:T(8,128)S(1)}, u32[]{:S(2)}, u32[]{:S(2)}) %collective-permute-start) | collective-permute-done | bytes 307232 | tf_op jit(solution)/shard_map/ppermute | solution.py:19
  12.0 1.0 %add.22 = f32[80,960]{1,0:T(8,128)S(1)} add(f32[80,960]{1,0:T(8,128)} %get-tuple-element.7, f32[80,960]{1,0:T(8,128)S(1)} %collective-permute-done) | non-fusion elementwise | flops 76800 | bytes 921600 | tf_op jit(solution)/shard_map/add | solution.py:30
  13.1 3.0 %collective-permute-start.1 = (f32[40,960]{1,0:T(8,128)S(1)}, f32[40,960]{1,0:T(8,128)S(1)}, u32[]{:S(2)}, u32[]{:S(2)}) collective-permute-start(f32[40,960]{1,0:T(8,128)S(1)} %dynamic-slice_bitcast_fusion), channel_id=1, source_target_pairs={{0,2},{1,3},{2,0},{3,1},{4,6},{5,7},{6,4},{7,5},{8,10},{9,11},{10,... | collective-permute-start | bytes 460808 | tf_op jit(solution)/shard_map/ppermute | solution.py:19
  16.0 0.0 copy-done
  16.0 0.0 copy-done.2
  16.0 0.0 copy-done.1
  16.0 0.2 convolution_select_fusion
  16.2 0.1 copy.17
  16.3 0.1 reshape.42
  16.4 4.1 %collective-permute-done.1 = f32[40,960]{1,0:T(8,128)S(1)} collective-permute-done((f32[40,960]{1,0:T(8,128)S(1)}, f32[40,960]{1,0:T(8,128)S(1)}, u32[]{:S(2)}, u32[]{:S(2)}) %collective-permute-start.1) | collective-permute-done | bytes 153632 | tf_op jit(solution)/shard_map/ppermute | solution.py:19
  20.5 0.1 fusion.10
  20.7 1.8 %collective-permute-start.4 = (f32[41,640]{1,0:T(8,128)S(1)}, f32[41,640]{1,0:T(8,128)S(1)}, u32[]{:S(2)}, u32[]{:S(2)}) collective-permute-start(f32[41,640]{1,0:T(8,128)S(1)} %get-tuple-element.15), channel_id=1, source_target_pairs={{28,0},{0,4},{4,8},{8,12},{12,16},{16,20},{20,24},{24,28},{29,1},{... | collective-permute-start | bytes 314888 | tf_op jit(solution)/shard_map/ppermute | solution.py:14
  22.4 1.5 %collective-permute-start.2 = (f32[40,960]{1,0:T(8,128)S(1)}, f32[40,960]{1,0:T(8,128)S(1)}, u32[]{:S(2)}, u32[]{:S(2)}) collective-permute-start(f32[40,960]{1,0:T(8,128)S(1)} %bitcast_add_fusion), channel_id=1, source_target_pairs={{0,2},{1,3},{2,0},{3,1},{4,6},{5,7},{6,4},{7,5},{8,10},{9,11},{10,... | collective-permute-start | bytes 460808 | tf_op jit(solution)/shard_map/ppermute | solution.py:19
  23.9 3.2 %collective-permute-start.5 = (f32[41,640]{1,0:T(8,128)S(1)}, f32[41,640]{1,0:T(8,128)S(1)}, u32[]{:S(2)}, u32[]{:S(2)}) collective-permute-start(f32[41,640]{1,0:T(8,128)S(1)} %get-tuple-element.16), channel_id=1, source_target_pairs={{4,0},{8,4},{12,8},{16,12},{20,16},{24,20},{28,24},{0,28},{5,1},{9... | collective-permute-start | bytes 314888 | tf_op jit(solution)/shard_map/ppermute | solution.py:14
  27.2 1.2 %collective-permute-done.4 = f32[41,640]{1,0:T(8,128)S(1)} collective-permute-done((f32[41,640]{1,0:T(8,128)S(1)}, f32[41,640]{1,0:T(8,128)S(1)}, u32[]{:S(2)}, u32[]{:S(2)}) %collective-permute-start.4) | collective-permute-done | bytes 104992 | tf_op jit(solution)/shard_map/ppermute | solution.py:14
  28.4 0.0 collective-permute-done.2
  28.5 0.1 collective-permute-start.3
  28.6 2.0 %collective-permute-done.5 = f32[41,640]{1,0:T(8,128)S(1)} collective-permute-done((f32[41,640]{1,0:T(8,128)S(1)}, f32[41,640]{1,0:T(8,128)S(1)}, u32[]{:S(2)}, u32[]{:S(2)}) %collective-permute-start.5) | collective-permute-done | bytes 104992 | tf_op jit(solution)/shard_map/ppermute | solution.py:14
  30.6 0.1 pad_maximum_fusion.5
  30.7 0.1 pad_maximum_fusion.4
  30.7 0.0 collective-permute-done.3
  30.7 0.1 select_bitcast_fusion.1
  30.8 0.1 pad_maximum_fusion
  30.9 0.1 reshape.43
  30.9 0.3 fusion.2
  31.3 0.4 fusion
  31.7 0.5 %convolution_bitcast_fusion = f32[1,8,20,40]{3,2,1,0:T(8,128)S(1)} fusion(f32[8,20,960]{2,1,0:T(8,128)S(1)} %reshape.43, f32[40,960]{1,0:T(8,128)S(1)} %bitcast_add_fusion, f32[960]{0:T(1024)S(1)} %pad_maximum_fusion.5), kind=kOutput, calls=%fused_computation | convolution fusion | flops 36902400 | bytes 797440 | tf_op jit(solution)/shard_map/dot_general | solution.py:113
  32.2 0.2 all_to_all.8
  32.5 12.3 %all_to_all.10 = f32[8,1,2400]{2,1,0:T(1,128)S(1)} all-to-all(f32[8,1,2400]{2,1,0:T(1,128)S(1)} %all_to_all.8), channel_id=1, replica_groups=mesh['elem'=8,'cuts'=4] {'elem'}, dimensions={0} | all-to-all | bytes 153600 | tf_op jit(solution)/shard_map/all_to_all | solution.py:153
  44.7 0.2 reduce.2
  44.9 0.1 reshape.44
  45.1 0.7 %copy.22 = f32[8,3,20,40]{3,0,2,1:T(8,128)} copy(f32[8,3,20,40]{3,2,1,0:T(8,128)S(1)} %reshape.44) | data formatting | bytes 153600 | tf_op jit(solution)/shard_map/reshape | solution.py:154
  (13 shorter events, 0.2 us)
Async XLA Ops:
  0.0 16.0 %copy-start = (f32[4,16]{1,0:T(4,128)S(1)}, f32[4,16]{1,0:T(4,128)}, u32[]{:S(2)}) copy-start(f32[4,16]{1,0:T(4,128)} %param.11) | copy-start | bytes 772
  0.0 16.0 %copy-start.2 = (s32[1,20]{1,0:T(1,128)S(1)}, s32[1,20]{1,0:T(1,128)}, u32[]{:S(2)}) copy-start(s32[1,20]{1,0:T(1,128)} %param.10) | copy-start | bytes 244
  0.0 16.0 %copy-start.1 = (s32[1,20]{1,0:T(1,128)S(1)}, s32[1,20]{1,0:T(1,128)}, u32[]{:S(2)}) copy-start(s32[1,20]{1,0:T(1,128)} %param.9) | copy-start | bytes 244
  10.1 1.9 %collective-permute-start = (f32[80,960]{1,0:T(8,128)}, f32[80,960]{1,0:T(8,128)S(1)}, u32[]{:S(2)}, u32[]{:S(2)}) collective-permute-start(f32[80,960]{1,0:T(8,128)} %get-tuple-element.8), channel_id=1, source_target_pairs={{0,1},{1,0},{2,3},{3,2},{4,5},{5,4},{6,7},{7,6},{8,9},{9,8},{10,11... | collective-permute-start | bytes 921608 | tf_op jit(solution)/shard_map/ppermute | solution.py:19
  13.1 7.5 %collective-permute-start.1 = (f32[40,960]{1,0:T(8,128)S(1)}, f32[40,960]{1,0:T(8,128)S(1)}, u32[]{:S(2)}, u32[]{:S(2)}) collective-permute-start(f32[40,960]{1,0:T(8,128)S(1)} %dynamic-slice_bitcast_fusion), channel_id=1, source_target_pairs={{0,2},{1,3},{2,0},{3,1},{4,6},{5,7},{6,4},{7,5},{8,10},{9,11},{10,... | collective-permute-start | bytes 460808 | tf_op jit(solution)/shard_map/ppermute | solution.py:19
  20.7 7.7 %collective-permute-start.4 = (f32[41,640]{1,0:T(8,128)S(1)}, f32[41,640]{1,0:T(8,128)S(1)}, u32[]{:S(2)}, u32[]{:S(2)}) collective-permute-start(f32[41,640]{1,0:T(8,128)S(1)} %get-tuple-element.15), channel_id=1, source_target_pairs={{28,0},{0,4},{4,8},{8,12},{12,16},{16,20},{20,24},{24,28},{29,1},{... | collective-permute-start | bytes 314888 | tf_op jit(solution)/shard_map/ppermute | solution.py:14
  22.4 6.0 %collective-permute-start.2 = (f32[40,960]{1,0:T(8,128)S(1)}, f32[40,960]{1,0:T(8,128)S(1)}, u32[]{:S(2)}, u32[]{:S(2)}) collective-permute-start(f32[40,960]{1,0:T(8,128)S(1)} %bitcast_add_fusion), channel_id=1, source_target_pairs={{0,2},{1,3},{2,0},{3,1},{4,6},{5,7},{6,4},{7,5},{8,10},{9,11},{10,... | collective-permute-start | bytes 460808 | tf_op jit(solution)/shard_map/ppermute | solution.py:19
  23.9 6.6 %collective-permute-start.5 = (f32[41,640]{1,0:T(8,128)S(1)}, f32[41,640]{1,0:T(8,128)S(1)}, u32[]{:S(2)}, u32[]{:S(2)}) collective-permute-start(f32[41,640]{1,0:T(8,128)S(1)} %get-tuple-element.16), channel_id=1, source_target_pairs={{4,0},{8,4},{12,8},{16,12},{20,16},{24,20},{28,24},{0,28},{5,1},{9... | collective-permute-start | bytes 314888 | tf_op jit(solution)/shard_map/ppermute | solution.py:14
  28.5 2.2 %collective-permute-start.3 = (f32[2,40,960]{2,1,0:T(8,128)S(1)}, f32[2,40,960]{2,1,0:T(8,128)S(1)}, u32[]{:S(2)}, u32[]{:S(2)}) collective-permute-start(f32[2,40,960]{2,1,0:T(8,128)S(1)} %pad_maximum_fusion.1), channel_id=1, source_target_pairs={{0,1},{1,0},{2,3},{3,2},{4,5},{5,4},{6,7},{7,6},{8,9},{9,8},{10,11... | collective-permute-start | bytes 921608 | tf_op jit(solution)/shard_map/ppermute | solution.py:19
